TPU v7x, 32 devices: a whole 2x2x4 slice. The times are simulated.
32 devices in a mesh: groups: 2 (over x), band: 16 (over z, y, core).
Axes of the slice: x: 2, y: 2, z: 4, core: 2. Of those that a mesh axis runs over, the one named last changes fastest.
Arguments:
- initial_height_velocity: float32 [64, 3, 16, 512], P(('groups', 'band')), parts along dimension 0, may hold values from -3 to 3
- member_fidelity: int32 [64], P('groups'), parts along dimension 0, may hold values from 0 to 2, as said below
- obs_cell: int32 [32, 256], P(('groups', 'band')), parts along dimension 0, may hold values from 0 to 4607, as said below
- obs_value: float32 [32, 256], P(('groups', 'band')), parts along dimension 0, may hold values from -3 to 3
- obs_var: float32 [32, 256], P(('groups', 'band')), parts along dimension 0, may hold values from 0.04 to 0.4
- obs_noise: float32 [32, 256, 32], P(('groups', 'band')), parts along dimension 0, may hold values from -6 to 6
Outputs:
- analysis: float32 [64, 3, 16, 512], P(('groups', 'band')), parts along dimension 0
There are 2 independent parts, one for each index of `groups`. A program takes and returns all parts, laid end to end along the dimension named above; each array names one. Nothing has to cross between parts.
Inputs may be any that keep to these rules, and one draw needn't show every extreme that they name: `member_fidelity`: exactly half of the 32 members have class 0, a quarter class 1 and a quarter class 2. `obs_cell`: an entry is c * 3 * 512 + r * 512 + j for component c, row r of the tile's extended block and column j; the row always lies inside the grid. Observation 0 of tile 1 is 0 and observation 1 of tile 1 is the largest value.
All inputs are finite; a program needn't handle non-finite values.
Results may differ from a plain program's by a relative error of at most 0.0003.
Values sent between devices are 32-bit elements; how exact they have to be, the bound alone decides.
No kernel may reach another device: no remote copies, remote signals or barrier semaphores. Data moves between devices by JAX's collectives and lax.ppermute only.
A program may use at most 64 MiB of HBM per device.

v0:
```python
import jax
import jax.numpy as jnp
from jax import lax
from jax.sharding import PartitionSpec as P

PREDICTION_COUNT = 4


exact = lax.Precision.HIGHEST
time_step = 0.25
viscous = 0.05
slow_friction = 0.2
control_weight = 0.5


def extended(shard, sides, width):
    for axis, dim in sides:
        devices, length = (lax.axis_size(axis), shard.shape[dim])
        up = [(i, (i + 1) % devices) for i in range(devices - 1)]
        down = [(j, i) for i, j in up]
        last = lax.slice_in_dim(shard, length - width, length, axis=dim)
        leading = lax.slice_in_dim(shard, 0, width, axis=dim)
        before = lax.ppermute(last, axis, up)
        after = lax.ppermute(leading, axis, down)
        shard = jnp.concatenate([before, shard, after], axis=dim)
    return shard


def neighbours(field):
    lon_pad = jnp.pad(field, [(0, 0)] * (field.ndim - 1) + [(1, 1)])
    lat_pad = jnp.pad(field, [(0, 0)] * (field.ndim - 2) + [(1, 1), (0, 0)])
    return (lon_pad[..., 2:], lon_pad[..., :-2], lat_pad[..., 2:, :], lat_pad[..., :-2, :])


def east_slope(field):
    ahead, behind, upper, lower = neighbours(field)
    return 0.5 * (ahead - behind)


def north_slope(field):
    ahead, behind, upper, lower = neighbours(field)
    return 0.5 * (upper - lower)


def laplace(field):
    ahead, behind, upper, lower = neighbours(field)
    return ahead + behind + upper + lower - 4.0 * field


def advance(height, eastward, northward, nonlinear, friction, coriolis):
    depth = 1.0 + nonlinear * height
    height_new = (
        height
        - time_step * (east_slope(depth * eastward) + north_slope(depth * northward))
        + time_step * viscous * laplace(height)
    )
    east_new = eastward + time_step * (
        -nonlinear * (eastward * east_slope(eastward) + northward * north_slope(eastward))
        + coriolis * northward
        - east_slope(height_new)
        + viscous * laplace(eastward)
        - friction * eastward
    )
    north_new = northward + time_step * (
        -nonlinear * (eastward * east_slope(northward) + northward * north_slope(northward))
        - coriolis * eastward
        - north_slope(height_new)
        + viscous * laplace(northward)
        - friction * northward
    )
    return (height_new, east_new, north_new)


def begin_prediction(marine_condition, accuracy_levels, realization_count):
    nonlinear = (accuracy_levels == 0).astype(jnp.float32)[:, None, None]
    friction = jnp.where(accuracy_levels == 0, 0.0, slow_friction).astype(jnp.float32)[
        :, None, None
    ]
    lat_rows = marine_condition.shape[2]
    coriolis = (0.1 + 0.2 * (jnp.arange(lat_rows).astype(jnp.float32) + 0.5) / lat_rows)[:, None]
    height, eastward, northward = (
        marine_condition[:, 0],
        marine_condition[:, 1],
        marine_condition[:, 2],
    )
    for step in range(realization_count):
        height, eastward, northward = advance(
            height, eastward, northward, nonlinear, friction, coriolis
        )
    return jnp.stack([height, eastward, northward], axis=1)


def class_tables(accuracy_levels):
    onehot = (accuracy_levels[:, None] == jnp.arange(3)[None, :]).astype(jnp.float32)
    counts = jnp.sum(onehot, axis=0)
    coefs = jnp.stack(
        [
            1.0 / (counts[0] - 1.0),
            -control_weight / (counts[1] - 1.0),
            control_weight / (counts[2] - 1.0),
        ]
    )
    member_weight = jnp.sum(onehot * coefs[None, :], axis=1)
    return (onehot, counts, member_weight)


def remove_means(data, onehot, counts):
    means = jnp.dot(onehot.T, data, precision=exact) / counts[:, None]
    return data - jnp.dot(onehot, means, precision=exact)


def spd_solve(factor, rhs):
    inner = lax.linalg.triangular_solve(factor, rhs, left_side=True, lower=True)
    return lax.linalg.triangular_solve(factor, inner, left_side=True, lower=True, transpose_a=True)


def shards(initial_height_velocity, member_fidelity, obs_cell, obs_value, obs_var, obs_noise):
    per_device = initial_height_velocity.shape[0]
    resident_realizations = lax.dynamic_slice_in_dim(
        member_fidelity, lax.axis_index("band") * per_device, per_device
    )
    integrate_realizations = begin_prediction(
        initial_height_velocity, resident_realizations, PREDICTION_COUNT
    )
    tile_worker = lax.all_to_all(
        integrate_realizations, "band", split_axis=2, concat_axis=0, tiled=True
    )
    ensemble_members = tile_worker.shape[0]
    tile_rows = tile_worker.shape[2]
    flat = tile_worker.reshape(ensemble_members, -1)
    block = extended(tile_worker, (("band", 2),), tile_rows)
    observed = jnp.take(block.reshape(ensemble_members, -1), obs_cell[0], axis=1)
    onehot, counts, member_weight = class_tables(member_fidelity)
    spread = remove_means(flat, onehot, counts)
    obs_spread = remove_means(observed, onehot, counts)
    variance = obs_var[0]
    principal = onehot[:, 0] / (counts[0] - 1.0)
    innovation_cov = jnp.dot(
        (obs_spread * principal[:, None]).T, obs_spread, precision=exact
    ) + jnp.diag(variance)
    perturbed = obs_value[0][:, None] + jnp.sqrt(variance)[:, None] * obs_noise[0] - observed.T
    factor = jnp.linalg.cholesky(innovation_cov)
    cross_t = jnp.dot((obs_spread * member_weight[:, None]).T, spread, precision=exact)
    gain_t = spd_solve(factor, cross_t)
    update = jnp.dot(perturbed.T, gain_t, precision=exact)
    result = (flat + update).reshape(tile_worker.shape)
    return lax.all_to_all(result, "band", split_axis=0, concat_axis=2, tiled=True)


def solution(mesh):
    in_specs = (
        P(("groups", "band"), None, None, None),
        P("groups"),
        P(("groups", "band"), None),
        P(("groups", "band"), None),
        P(("groups", "band"), None),
        P(("groups", "band"), None, None),
    )
    out_specs = P(("groups", "band"), None, None, None)
    return jax.shard_map(shards, mesh=mesh, in_specs=in_specs, out_specs=out_specs, check_vma=False)
```

profile of v0, /device:TPU:0, one launch (start us, length us, event | category | flops | bytes accessed | tf_op | source)
XLA Modules:
  0.0 120.0 jit_solution(16549820008751581555)
XLA Ops:
  0.0 0.9 slice_bitcast_fusion.2
  0.9 0.7 fusion.94
  1.7 1.0 fusion.60
  2.7 0.1 fusion.11
  2.8 1.1 fusion.62
  3.9 0.0 copy-start.6
  3.9 0.1 fusion.21
  4.1 0.2 fusion.64
  4.3 0.1 fusion.26
  4.5 0.2 fusion.67
  4.7 0.1 fusion.31
  4.9 0.2 fusion.39
  5.1 0.8 copy.43
  5.9 7.4 %all-to-all-start = ((f32[2,3,16,512]{3,0,1,2:T(2,128)}), f32[2,3,16,512]{3,0,1,2:T(2,128)S(1)}, u32[]{:S(2)}, u32[]{:S(2)}) async-start(f32[2,3,16,512]{3,0,1,2:T(2,128)} %copy.43), calls=%async_computation | async-start | bytes 393216 | tf_op jit(solution)/shard_map/all_to_all | solution.py:125
  13.4 0.1 fusion.90
  13.5 0.5 iota_multiply_fusion
  14.0 0.6 compare_and_fusion
  14.6 0.6 fusion.96
  17.3 0.1 pad_maximum_fusion.2
  17.4 0.6 sqrt.7
  18.0 0.7 select_reduce_fusion.2
  18.7 0.6 divide_bitcast_fusion
  19.3 3.1 %all-to-all-done = f32[2,3,16,512]{3,0,1,2:T(2,128)S(1)} async-done(((f32[2,3,16,512]{3,0,1,2:T(2,128)}), f32[2,3,16,512]{3,0,1,2:T(2,128)S(1)}, u32[]{:S(2)}, u32[]{:S(2)}) %all-to-all-start) | async-done | bytes 196640 | tf_op jit(solution)/shard_map/all_to_all | solution.py:125
  22.3 0.2 copy.45
  22.5 1.7 %collective-permute-start = (f32[32,3,1,512]{3,2,1,0:T(1,128)S(1)}, f32[32,3,1,512]{3,2,1,0:T(1,128)S(1)}, u32[]{:S(2)}, u32[]{:S(2)}) collective-permute-start(f32[32,3,1,512]{3,2,1,0:T(1,128)S(1)} %bitcast.116), channel_id=1, source_target_pairs={{0,1},{1,2},{2,3},{3,4},{4,5},{5,6},{6,7},{7,8},{8,9},{9,10},{10,1... | collective-permute-start | bytes 589832 | tf_op jit(solution)/shard_map/ppermute | solution.py:23
  24.2 1.3 %collective-permute-start.1 = (f32[32,3,1,512]{3,2,1,0:T(1,128)S(1)}, f32[32,3,1,512]{3,2,1,0:T(1,128)S(1)}, u32[]{:S(2)}, u32[]{:S(2)}) collective-permute-start(f32[32,3,1,512]{3,2,1,0:T(1,128)S(1)} %bitcast.117), channel_id=1, source_target_pairs={{1,0},{2,1},{3,2},{4,3},{5,4},{6,5},{7,6},{8,7},{9,8},{10,9},{11,1... | collective-permute-start | bytes 589832 | tf_op jit(solution)/shard_map/ppermute | solution.py:24
  25.5 0.1 copy.44
  25.6 0.1 copy.54
  25.6 0.2 convolution_divide_fusion
  25.8 0.3 convolution_subtract_fusion.2
  26.1 1.4 %collective-permute-done.1 = f32[32,3,1,512]{3,2,1,0:T(1,128)S(1)} collective-permute-done((f32[32,3,1,512]{3,2,1,0:T(1,128)S(1)}, f32[32,3,1,512]{3,2,1,0:T(1,128)S(1)}, u32[]{:S(2)}, u32[]{:S(2)}) %collective-permute-start.1) | collective-permute-done | bytes 196640 | tf_op jit(solution)/shard_map/ppermute | solution.py:24
  27.5 0.5 pad_maximum_fusion
  28.0 1.0 copy.46
  29.1 0.7 gather_fusion
  29.8 0.1 copy.47
  29.9 0.8 convolution_divide_fusion.1
  30.7 0.9 convolution_subtract_fusion.4
  31.6 1.2 fusion.68
  32.7 0.1 copy.48
  32.9 0.1 fusion.6
  33.0 11.7 %cholesky.49 = f32[128,128]{1,0:T(8,128)S(1)} custom-call(f32[128,128]{1,0:T(8,128)S(1)} %cholesky.115), custom_call_target="Cholesky" | custom-call | tf_op jit(solution)/shard_map/jit(cholesky)/cholesky | solution.py:142
  44.8 9.8 %custom-call.16 = f32[1,128,128]{1,2,0:T(8,128)S(1)} custom-call(f32[1,128,128]{2,1,0:T(8,128)S(1)} %get-tuple-element.53), custom_call_target="InvertDiagBlocksLowerTriangular" | custom-call | tf_op jit(solution)/shard_map/jit(cholesky)/cholesky | solution.py:142
  54.6 0.2 constant_dynamic-update-slice_fusion.1
  54.8 0.3 convolution_subtract_fusion.3
  55.1 11.7 %cholesky.103 = f32[128,128]{1,0:T(8,128)S(1)} custom-call(f32[128,128]{1,0:T(8,128)S(1)} %convolution_subtract_fusion.3), custom_call_target="Cholesky" | custom-call | tf_op jit(solution)/shard_map/jit(cholesky)/cholesky | solution.py:142
  66.8 0.7 compare_reduce_fusion
  68.8 0.1 triangular_solve.72
  68.9 5.2 %while.1 = (s32[]{:T(128)}, f32[256,256]{1,0:T(8,128)S(1)}, s32[2,2]{1,0:T(2,128)S(1)}, f32[2,128,128]{2,1,0:T(8,128)}, s32[]{:T(128)}) while((s32[]{:T(128)}, f32[256,256]{1,0:T(8,128)S(1)}, s32[2,2]{1,0:T(2,128)S(1)}, f32[2,128,128]{2,1,0:T(8,128)}, s32[]{:T(128)}) %tuple.43), condition=%wide.while_cond, body=%wide.while_body.sunk | while | flops 2 | bytes 132705 | solution.py:114
  68.9 0.6 fusion.110
  69.5 2.0 %bitcast_dynamic-update-slice_fusion.2 = f32[2,128,128]{2,1,0:T(8,128)} fusion(f32[2,128,128]{2,1,0:T(8,128)} %get-tuple-element.99, s32[]{:T(128)} %get-tuple-element.96, f32[256,256]{1,0:T(8,128)S(1)} %get-tuple-element.102, s32[]{:T(128)} %bitcast.106, s32[]{:T(128)} %bitcast.107), kind=kLoop, calls=%fused_computation.1.clone.1 | loop fusion | bytes 132608 | tf_op jit(solution)/shard_map/triangular_solve
  71.5 0.6 fusion.110
  72.1 2.0 %bitcast_dynamic-update-slice_fusion.2 = f32[2,128,128]{2,1,0:T(8,128)} fusion(f32[2,128,128]{2,1,0:T(8,128)} %get-tuple-element.99, s32[]{:T(128)} %get-tuple-element.96, f32[256,256]{1,0:T(8,128)S(1)} %get-tuple-element.102, s32[]{:T(128)} %bitcast.106, s32[]{:T(128)} %bitcast.107), kind=kLoop, calls=%fused_computation.1.clone.1 | loop fusion | bytes 132608 | tf_op jit(solution)/shard_map/triangular_solve
  74.1 20.5 %custom-call.17 = f32[2,128,128]{1,2,0:T(8,128)S(1)} custom-call(f32[2,128,128]{2,1,0:T(8,128)} %get-tuple-element.12), custom_call_target="InvertDiagBlocksLowerTriangular" | custom-call | tf_op jit(solution)/shard_map/triangular_solve | solution.py:114
  94.6 1.5 %fusion.73 = f32[256,1536]{1,0:T(8,128)S(1)} fusion(f32[32,1536]{1,0:T(8,128)S(1)} %convolution_subtract_fusion.2, f32[32,256]{1,0:T(8,128)S(1)} %convolution_subtract_fusion.4, f32[32]{0:T(128)S(1)} %copy-done.7), kind=kOutput, calls=%fused_computation.180 | convolution fusion | flops 151003136 | bytes 1802368 | tf_op jit(solution)/shard_map/dot_general | solution.py:143
  96.1 0.8 fusion.3
  96.9 0.8 convolution_subtract_fusion.1
  97.7 0.8 fusion.57
  98.6 0.8 fusion.56
  99.4 0.8 convolution_subtract_fusion
  100.2 0.8 fusion.55
  101.1 1.0 convolution_add_fusion
  102.1 0.2 reshape.130
  102.3 17.0 %all_to_all.36 = f32[32,3,1,512]{3,2,1,0:T(1,128)S(1)} all-to-all(f32[32,3,1,512]{3,2,1,0:T(1,128)S(1)} %reshape.130), channel_id=1, replica_groups=mesh['groups'=2,'band'=16] {'band'}, dimensions={0} | all-to-all | bytes 393216 | tf_op jit(solution)/shard_map/all_to_all | solution.py:147
  119.3 0.7 copy.56
  (31 shorter events, 0.2 us)
Async XLA Ops:
  3.9 9.4 %copy-start.1 = (s32[32]{0:T(128)S(1)}, s32[32]{0:T(128)}, u32[]{:S(2)}) copy-start(s32[32]{0:T(128)} %param.7) | copy-start | bytes 388
  3.9 10.1 %copy-start.6 = (s32[1,256]{1,0:T(1,128)S(1)}, s32[1,256]{1,0:T(1,128)}, u32[]{:S(2)}) copy-start(s32[1,256]{1,0:T(1,128)} %param.8) | copy-start | bytes 3076
  4.1 13.3 %copy-start.2 = (f32[1,256]{1,0:T(1,128)S(1)}, f32[1,256]{1,0:T(1,128)}, u32[]{:S(2)}) copy-start(f32[1,256]{1,0:T(1,128)} %param.10) | copy-start | bytes 3076
  5.9 16.4 %all-to-all-start = ((f32[2,3,16,512]{3,0,1,2:T(2,128)}), f32[2,3,16,512]{3,0,1,2:T(2,128)S(1)}, u32[]{:S(2)}, u32[]{:S(2)}) async-start(f32[2,3,16,512]{3,0,1,2:T(2,128)} %copy.43), calls=%async_computation | async-start | bytes 393216 | tf_op jit(solution)/shard_map/all_to_all | solution.py:125
  22.5 3.6 %collective-permute-start = (f32[32,3,1,512]{3,2,1,0:T(1,128)S(1)}, f32[32,3,1,512]{3,2,1,0:T(1,128)S(1)}, u32[]{:S(2)}, u32[]{:S(2)}) collective-permute-start(f32[32,3,1,512]{3,2,1,0:T(1,128)S(1)} %bitcast.116), channel_id=1, source_target_pairs={{0,1},{1,2},{2,3},{3,4},{4,5},{5,6},{6,7},{7,8},{8,9},{9,10},{10,1... | collective-permute-start | bytes 589832 | tf_op jit(solution)/shard_map/ppermute | solution.py:23
  24.2 3.3 %collective-permute-start.1 = (f32[32,3,1,512]{3,2,1,0:T(1,128)S(1)}, f32[32,3,1,512]{3,2,1,0:T(1,128)S(1)}, u32[]{:S(2)}, u32[]{:S(2)}) collective-permute-start(f32[32,3,1,512]{3,2,1,0:T(1,128)S(1)} %bitcast.117), channel_id=1, source_target_pairs={{1,0},{2,1},{3,2},{4,3},{5,4},{6,5},{7,6},{8,7},{9,8},{10,9},{11,1... | collective-permute-start | bytes 589832 | tf_op jit(solution)/shard_map/ppermute | solution.py:24
  32.7 36.1 %copy-start.8 = (s32[2]{0:T(128)S(1)}, s32[2]{0:T(128)}, u32[]{:S(2)}) copy-start(s32[2]{0:T(128)} %iota_multiply_fusion) | copy-start | bytes 28
  32.9 61.7 %copy-start.7 = (f32[32]{0:T(128)S(1)}, f32[32]{0:T(128)}, u32[]{:S(2)}) copy-start(f32[32]{0:T(128)} %select_reduce_fusion.2) | copy-start | bytes 388
  99.3 1.7 %copy-start = (f32[1,256,32]{1,2,0:T(8,128)S(1)}, f32[1,256,32]{1,2,0:T(8,128)}, u32[]{:S(2)}) copy-start(f32[1,256,32]{1,2,0:T(8,128)} %param.11) | copy-start | bytes 98308
  99.4 1.7 %copy-start.3 = (f32[256]{0:T(256)S(1)}, f32[256]{0:T(256)}, u32[]{:S(2)}) copy-start(f32[256]{0:T(256)} %sqrt.7) | copy-start | bytes 3076
  99.4 1.7 %copy-start.4 = (pred[256]{0:T(512)(128)(4,1)S(1)}, pred[256]{0:T(512)(128)(4,1)}, u32[]{:S(2)}) copy-start(pred[256]{0:T(512)(128)(4,1)} %compare_and_fusion) | copy-start | bytes 772
  99.4 1.7 %copy-start.5 = (f32[1,256]{1,0:T(1,128)S(1)}, f32[1,256]{1,0:T(1,128)}, u32[]{:S(2)}) copy-start(f32[1,256]{1,0:T(1,128)} %param.9) | copy-start | bytes 3076
where the time goes:
time: 121 us; the launch traced here: 120 us
  other arithmetic  61.8 us (51%)
  blocking collectives  17 us (14%)
  local copies, waits for them, and re-layouts  11.5 us (10%)
  matrix products  11.2 us (9%)
  starting transfers between devices  10.4 us (9%)
  waiting for transfers between devices  4.44 us (4%)
  between operations  3.77 us (3%)
    another operation x6, other arithmetic, shards(): factor = jnp.linalg.cholesky(innovation_cov)  34 us
    another operation x3, other arithmetic, spd_solve(): lax.linalg.triangular_solve(factor, inner, left_side=True, lower=True, tr...  21 us
    all_to_all x1, blocking collectives, shards(): lax.all_to_all(result, 'band', split_axis=0, concat_axis=2, tiled=True)  17 us
    all_to_all x1, starting transfers between devices, shards(): lax.all_to_all(integrate_realizations, 'band', split_axis=2, concat_axis=...  7.41 us
    another operation x6, local copies, waits for them, and re-layouts  5.16 us
    all_to_all x1, waiting for transfers between devices, shards(): lax.all_to_all(integrate_realizations, 'band', split_axis=2, concat_axis=...  3.06 us
    another operation x3, matrix products, spd_solve(): inner = lax.linalg.triangular_solve(factor, rhs, left_side=True, lower=True)  2.46 us
  transfers between devices with their start and end apart: 3, of which 2 were waited for; matrix products, arithmetic and copies ran while one was open for 4% of the time, Pallas kernels for 0%

commit v1 on v0

--- a/solution.py
+++ b/solution.py
@@ -2,6 +2,8 @@
 import jax.numpy as jnp
 from jax import lax
 from jax.sharding import PartitionSpec as P
+from jax.experimental import pallas as pl
+from jax.experimental.pallas import tpu as pltpu
 
 PREDICTION_COUNT = 4
 
@@ -114,6 +116,33 @@
     return lax.linalg.triangular_solve(factor, inner, left_side=True, lower=True, transpose_a=True)
 
 
+def gauss_jordan_kernel(a_ref, o_ref):
+    n = a_ref.shape[0]
+    lane = lax.broadcasted_iota(jnp.int32, a_ref.shape, 1)
+    row_id = lax.broadcasted_iota(jnp.int32, (n, 1), 0)
+
+    def step(k, a):
+        pivot_row = jnp.sum(jnp.where(row_id == k, a, 0.0), axis=0, keepdims=True)
+        column = jnp.sum(jnp.where(lane == k, a, 0.0), axis=1, keepdims=True)
+        pivot = jnp.sum(jnp.where(lane[0:1] == k, pivot_row, 0.0), axis=1, keepdims=True)
+        pivot_row = pivot_row / pivot
+        column = column - (row_id == k).astype(jnp.float32)
+        return a - column * pivot_row
+
+    a = lax.fori_loop(0, n, step, a_ref[...], unroll=n <= 64)
+    o_ref[...] = a[:, n:]
+
+
+def gauss_jordan(augmented):
+    n = augmented.shape[0]
+    return pl.pallas_call(
+        gauss_jordan_kernel,
+        out_shape=jax.ShapeDtypeStruct((n, augmented.shape[1] - n), jnp.float32),
+        in_specs=[pl.BlockSpec(memory_space=pltpu.VMEM)],
+        out_specs=pl.BlockSpec(memory_space=pltpu.VMEM),
+    )(augmented)
+
+
 def shards(initial_height_velocity, member_fidelity, obs_cell, obs_value, obs_var, obs_noise):
     per_device = initial_height_velocity.shape[0]
     resident_realizations = lax.dynamic_slice_in_dim(
@@ -135,14 +164,18 @@
     obs_spread = remove_means(observed, onehot, counts)
     variance = obs_var[0]
     principal = onehot[:, 0] / (counts[0] - 1.0)
-    innovation_cov = jnp.dot(
-        (obs_spread * principal[:, None]).T, obs_spread, precision=exact
-    ) + jnp.diag(variance)
+    scale = jnp.sqrt(principal)
     perturbed = obs_value[0][:, None] + jnp.sqrt(variance)[:, None] * obs_noise[0] - observed.T
-    factor = jnp.linalg.cholesky(innovation_cov)
-    cross_t = jnp.dot((obs_spread * member_weight[:, None]).T, spread, precision=exact)
-    gain_t = spd_solve(factor, cross_t)
-    update = jnp.dot(perturbed.T, gain_t, precision=exact)
+    weighted = obs_spread / variance[None, :]
+    both = jnp.dot(
+        weighted, jnp.concatenate([obs_spread.T, perturbed], axis=1), precision=exact
+    )
+    inner, direct = both[:, :ensemble_members], both[:, ensemble_members:]
+    system = jnp.eye(ensemble_members, dtype=jnp.float32) + scale[:, None] * inner * scale[None, :]
+    solved = gauss_jordan(jnp.concatenate([system, scale[:, None] * direct], axis=1))
+    projected = direct - jnp.dot(inner, scale[:, None] * solved, precision=exact)
+    mixing = projected * member_weight[:, None]
+    update = jnp.dot(mixing.T, spread, precision=exact)
     result = (flat + update).reshape(tile_worker.shape)
     return lax.all_to_all(result, "band", split_axis=0, concat_axis=2, tiled=True)
 

time: 121 us -> 58.3 us (0.48)
  other arithmetic: 61.8 us -> 8 us
  matrix products: 11.2 us -> 4.42 us
  local copies, waits for them, and re-layouts: 11.5 us -> 5.36 us
  Pallas kernels: 0 us -> 4.61 us
  between operations: 3.77 us -> 2.15 us
  waiting for transfers between devices: 4.44 us -> 5.76 us
    another operation x9 -> x0, other arithmetic: 55 us -> none  [the longest x6 34 us: shards(): factor = jnp.linalg.cholesky(innovation_cov)]
    another operation x8 -> x0, matrix products: 5.33 us -> none  [the longest x3 2.46 us: spd_solve(): inner = lax.linalg.triangular_solve(factor, rhs, left_side=True, lower=True)]
    another operation x9 -> x0, local copies, waits for them, and re-layouts: 5.25 us -> none
    pallas_call x0 -> x1, Pallas kernels: none -> 4.61 us  [gauss_jordan(): pl.pallas_call(gauss_jordan_kernel, out_shape=jax.ShapeDtypeStruct((n, au...]
    dot_general x3, matrix products: 3.66 us -> 2.16 us  [the longest x1 0.93 us: shards(): jnp.dot(inner, scale[:, None] * solved, precision=exact)]
    all_to_all x1, waiting for transfers between devices: 3.06 us -> 4.38 us  [shards(): lax.all_to_all(integrate_realizations, 'band', split_axis=2, concat_axis=...]
  transfers between devices with their start and end apart: 3 -> 3, of which waited for: 2 -> 2; matrix products, arithmetic and copies ran while one was open for 4% -> 6% of each run, Pallas kernels for 0% -> 0%
where the time goes in v1:
time: 58.3 us; the launch traced here: 57.6 us
  blocking collectives  17 us (29%)
  starting transfers between devices  10.4 us (18%)
  other arithmetic  8 us (14%)
  waiting for transfers between devices  5.76 us (10%)
  local copies, waits for them, and re-layouts  5.36 us (9%)
  Pallas kernels  4.61 us (8%)
  matrix products  4.42 us (8%)
  between operations  2.15 us (4%)
    all_to_all x1, blocking collectives, shards(): lax.all_to_all(result, 'band', split_axis=0, concat_axis=2, tiled=True)  17 us
    all_to_all x1, starting transfers between devices, shards(): lax.all_to_all(integrate_realizations, 'band', split_axis=2, concat_axis=...  7.41 us
    pallas_call x1, Pallas kernels, gauss_jordan(): pl.pallas_call(gauss_jordan_kernel, out_shape=jax.ShapeDtypeStruct((n, au...  4.61 us
    all_to_all x1, waiting for transfers between devices, shards(): lax.all_to_all(integrate_realizations, 'band', split_axis=2, concat_axis=...  4.38 us
    mul x3, other arithmetic, advance(): depth * northward  2.33 us
    ppermute x1, starting transfers between devices, extended(): before = lax.ppermute(last, axis, up)  1.65 us
    ppermute x1, waiting for transfers between devices, extended(): after = lax.ppermute(leading, axis, down)  1.38 us
    ppermute x1, starting transfers between devices, extended(): after = lax.ppermute(leading, axis, down)  1.29 us
  transfers between devices with their start and end apart: 3, of which 2 were waited for; matrix products, arithmetic and copies ran while one was open for 6% of the time, Pallas kernels for 0%

profile of v1, /device:TPU:0, one launch (start us, length us, event | category | flops | bytes accessed | tf_op | source)
XLA Modules:
  0.0 57.6 jit_solution(13575916224450048963)
XLA Ops:
  0.0 0.0 copy-start
  0.0 0.0 copy-start.1
  0.0 0.0 copy-start.2
  0.0 1.0 %slice_bitcast_fusion = (f32[2,16,512]{2,1,0:T(8,128)S(1)}, f32[2,16,512]{2,1,0:T(8,128)S(1)}, f32[2,16,512]{2,1,0:T(8,128)S(1)}) fusion(f32[2,3,16,512]{3,2,1,0:T(8,128)} %param.6), kind=kLoop, calls=%fused_computation.136 | loop fusion | bytes 393216 | tf_op jit(solution)/shard_map/squeeze | solution.py:86
  1.0 0.7 %fusion.82 = (f32[2]{0:T(128)S(1)}, f32[2]{0:T(128)S(1)}, f32[2]{0:T(128)S(1)}) fusion(s32[32]{0:T(128)} %param.7, s32[]{:T(128)S(6)} %select_n.32), kind=kLoop, calls=%fused_computation.189 | loop fusion | flops 8 | bytes 36 | tf_op jit(solution)/shard_map/neg | solution.py:60
  1.7 1.0 %fusion.50 = (f32[2,16,512]{2,1,0:T(8,128)S(1)}, f32[2,16,512]{2,1,0:T(8,128)S(1)}) fusion(f32[2]{0:T(128)S(1)} %get-tuple-element.18, f32[2,3,16,512]{3,2,1,0:T(8,128)} %param.6), kind=kLoop, calls=%fused_computation.140 | loop fusion | flops 65536 | bytes 327688 | tf_op jit(solution)/shard_map/mul | solution.py:56
  2.7 0.1 fusion.5
  2.8 1.1 %fusion.52 = (f32[2,16,512]{2,1,0:T(8,128)S(1)}, f32[2,16,512]{2,1,0:T(8,128)S(1)}, f32[2,16,512]{2,1,0:T(8,128)S(1)}, f32[2,16,512]{2,1,0:T(8,128)S(1)}) fusion(f32[2,16,512]{2,1,0:T(8,128)S(1)} %fusion.5, f32[2]{0:T(128)S(1)} %get-tuple-element.18, f32[2,16,512]{2,1,0:T(8,128)S(1)} %get-tuple-element.29, f32[2]{0:T(128)S(1)} %get-tuple-element.39, ...), kind=kLoop, calls=%fused_computation.142 | loop fusion | flops 851968 | bytes 589912 | tf_op jit(solution)/shard_map/mul | solution.py:56
  4.0 0.1 fusion.15
  4.1 0.2 fusion.54
  4.3 0.1 fusion.20
  4.5 0.2 fusion.57
  4.7 0.1 fusion.25
  4.9 0.2 fusion.33
  5.1 0.8 %copy.39 = f32[2,3,16,512]{3,0,1,2:T(2,128)} copy(f32[2,3,16,512]{3,2,0,1:T(8,128)S(1)} %pad_maximum_fusion.1) | data formatting | bytes 393216 | tf_op jit(solution)/shard_map/stack | solution.py:92
  5.9 7.4 %all-to-all-start = ((f32[2,3,16,512]{3,0,1,2:T(2,128)}), f32[2,3,16,512]{3,0,1,2:T(2,128)S(1)}, u32[]{:S(2)}, u32[]{:S(2)}) async-start(f32[2,3,16,512]{3,0,1,2:T(2,128)} %copy.39), calls=%async_computation | async-start | bytes 393216 | tf_op jit(solution)/shard_map/all_to_all | solution.py:154
  13.4 0.0 copy-done
  13.4 0.1 fusion.78
  13.5 0.0 copy-done.1
  13.5 0.6 %compare_and_fusion = pred[256]{0:T(512)(128)(4,1)} fusion(s32[256]{0:T(256)S(1)} %bitcast.88), kind=kLoop, calls=%fused_computation.175 | loop fusion | flops 1536 | bytes 1280 | tf_op jit(solution)/shard_map/jit(_take)/and | solution.py:161
  14.1 0.6 %fusion.83 = (f32[1]{0:T(128)}, f32[1]{0:T(128)}, f32[1]{0:T(128)}) fusion(f32[3]{0:T(128)S(1)} %fusion.78), kind=kLoop, calls=%fused_computation.190 | loop fusion | bytes 24 | tf_op jit(solution)/shard_map/slice | solution.py:101
  16.7 0.1 pad_maximum_fusion.3
  16.8 0.0 copy-done.2
  16.8 0.6 %select_reduce_fusion = f32[32]{0:T(128)} fusion(f32[3]{0:T(128)S(1)} %pad_maximum_fusion.3, s32[32]{0:T(128)S(1)} %copy-done), kind=kLoop, calls=%fused_computation.171 | loop fusion | flops 256 | bytes 268 | tf_op jit(solution)/shard_map/reduce_sum | solution.py:105
  17.4 0.5 sqrt_bitcast_fusion
  17.9 4.4 %all-to-all-done = f32[2,3,16,512]{3,0,1,2:T(2,128)S(1)} async-done(((f32[2,3,16,512]{3,0,1,2:T(2,128)}), f32[2,3,16,512]{3,0,1,2:T(2,128)S(1)}, u32[]{:S(2)}, u32[]{:S(2)}) %all-to-all-start) | async-done | bytes 196640 | tf_op jit(solution)/shard_map/all_to_all | solution.py:154
  22.3 0.2 copy.41
  22.5 1.7 %collective-permute-start = (f32[32,3,1,512]{3,2,1,0:T(1,128)S(1)}, f32[32,3,1,512]{3,2,1,0:T(1,128)S(1)}, u32[]{:S(2)}, u32[]{:S(2)}) collective-permute-start(f32[32,3,1,512]{3,2,1,0:T(1,128)S(1)} %bitcast.82), channel_id=1, source_target_pairs={{0,1},{1,2},{2,3},{3,4},{4,5},{5,6},{6,7},{7,8},{8,9},{9,10},{10,1... | collective-permute-start | bytes 589832 | tf_op jit(solution)/shard_map/ppermute | solution.py:25
  24.2 1.3 %collective-permute-start.1 = (f32[32,3,1,512]{3,2,1,0:T(1,128)S(1)}, f32[32,3,1,512]{3,2,1,0:T(1,128)S(1)}, u32[]{:S(2)}, u32[]{:S(2)}) collective-permute-start(f32[32,3,1,512]{3,2,1,0:T(1,128)S(1)} %bitcast.83), channel_id=1, source_target_pairs={{1,0},{2,1},{3,2},{4,3},{5,4},{6,5},{7,6},{8,7},{9,8},{10,9},{11,1... | collective-permute-start | bytes 589832 | tf_op jit(solution)/shard_map/ppermute | solution.py:26
  25.5 0.1 copy.40
  25.6 0.1 copy.49
  25.6 0.2 convolution_divide_fusion
  25.8 0.3 convolution_subtract_fusion
  26.1 0.0 collective-permute-done
  26.1 1.4 %collective-permute-done.1 = f32[32,3,1,512]{3,2,1,0:T(1,128)S(1)} collective-permute-done((f32[32,3,1,512]{3,2,1,0:T(1,128)S(1)}, f32[32,3,1,512]{3,2,1,0:T(1,128)S(1)}, u32[]{:S(2)}, u32[]{:S(2)}) %collective-permute-start.1) | collective-permute-done | bytes 196640 | tf_op jit(solution)/shard_map/ppermute | solution.py:26
  27.5 0.5 pad_maximum_fusion
  28.0 0.8 %copy.42 = f32[32,3,3,512]{0,3,2,1:T(8,128)S(1)} copy(f32[32,3,3,512]{3,2,1,0:T(4,128)S(1)} %pad_maximum_fusion) | data formatting | bytes 1179648 | tf_op jit(solution)/shard_map/concatenate | solution.py:27
  28.9 0.7 %gather_fusion = f32[256,32]{1,0:T(8,128)S(1)} fusion(f32[32,4608]{0,1:T(8,128)S(1)} %bitcast.77, s32[1024]{0:T(1024)S(1)} %pad_clamp_fusion), kind=kCustom, calls=%fused_computation | custom fusion | bytes 66560 | tf_op jit(solution)/shard_map/jit(_take)/gather | solution.py:161
  29.6 0.1 copy.43
  29.7 0.8 %convolution_divide_fusion.1 = f32[3,256]{1,0:T(4,128)S(1)} fusion(f32[256,32]{0,1:T(8,128)S(1)} %copy.43, pred[256]{0:T(512)(128)(4,1)} %compare_and_fusion, f32[3]{0:T(128)S(1)} %fusion.78, s32[32]{0:T(128)S(1)} %copy-done), kind=kOutput, calls=%fused_computation.6 | convolution fusion | flops 303968 | bytes 36236 | tf_op jit(solution)/shard_map/dot_general | solution.py:110
  30.5 1.0 %bitcast_subtract_fusion = (f32[256,32]{0,1:T(8,128)S(1)}, f32[256,32]{0,1:T(8,128)S(1)}, f32[32,256]{1,0:T(8,128)S(1)}) fusion(f32[256,32]{0,1:T(8,128)S(1)} %copy.43, pred[256]{0:T(512)(128)(4,1)} %compare_and_fusion, f32[1,256,32]{1,2,0:T(8,128)} %param.11, f32[256]{0:T(256)S(1)} %sqrt.16, f32[256]{0:T(256)} %bitcast.87, ...), kind=kOutput, calls=%fused_computation.151 | convolution fusion | flops 335968 | bytes 169344 | tf_op jit(solution)/shard_map/dot_general | solution.py:111
  31.5 0.9 %fusion.46 = f32[32,64]{1,0:T(8,128)S(1)} fusion(f32[256,32]{0,1:T(8,128)S(1)} %get-tuple-element.33, f32[256,32]{0,1:T(8,128)S(1)} %get-tuple-element.32, f32[32,256]{1,0:T(8,128)S(1)} %get-tuple-element.40, f32[256,32]{0,1:T(8,128)S(1)} %copy.43, f32[256]{0:T(256)} %bitcast.89, pred[256]{0:T(512)(128)(4,1)} %compare_and_fusion), kind=kOutput, calls=%fused_computation.123 | convolution fusion | flops 6332416 | bytes 140544 | tf_op jit(solution)/shard_map/dot_general | solution.py:170
  32.3 0.8 %multiply_add_fusion.10 = (f32[32,32]{1,0:T(8,128)S(1)}, f32[32,32]{1,0:T(8,128)S(1)}) fusion(f32[32,64]{1,0:T(8,128)S(1)} %fusion.46, f32[32]{0:T(128)} %sqrt_bitcast_fusion), kind=kLoop, calls=%fused_computation.160 | loop fusion | flops 6144 | bytes 17408 | tf_op jit(solution)/shard_map/add | solution.py:174
  33.1 0.7 %pad_maximum_fusion.2.a_ref = f32[32,64]{1,0:T(8,128)} fusion(f32[32,32]{1,0:T(8,128)S(1)} %get-tuple-element.35, f32[32,32]{1,0:T(8,128)S(1)} %get-tuple-element.34), kind=kLoop, calls=%fused_computation.156 | loop fusion | flops 2048 | bytes 16384 | tf_op jit(solution)/shard_map/concatenate | solution.py:175
  33.8 4.6 %shard_map.64 = f32[32,32]{1,0:T(8,128)} custom-call(f32[32,64]{1,0:T(8,128)} %pad_maximum_fusion.2.a_ref), custom_call_target="tpu_custom_call" | custom-call | tf_op jit(solution)/shard_map/pallas_call | solution.py:138
  38.4 0.9 %fusion = f32[32,32]{1,0:T(8,128)S(1)} fusion(f32[32,32]{1,0:T(8,128)} %shard_map.64, f32[32,64]{1,0:T(8,128)S(1)} %fusion.46, f32[32]{0:T(128)} %select_reduce_fusion, f32[32]{0:T(128)} %sqrt_bitcast_fusion), kind=kOutput, calls=%fused_computation.5 | convolution fusion | flops 396288 | bytes 41216 | tf_op jit(solution)/shard_map/dot_general | solution.py:176
  39.3 0.4 convolution_add_fusion
  39.7 0.2 reshape.97
  39.9 17.0 %all_to_all.36 = f32[32,3,1,512]{3,2,1,0:T(1,128)S(1)} all-to-all(f32[32,3,1,512]{3,2,1,0:T(1,128)S(1)} %reshape.97), channel_id=1, replica_groups=mesh['groups'=2,'band'=16] {'band'}, dimensions={0} | all-to-all | bytes 393216 | tf_op jit(solution)/shard_map/all_to_all | solution.py:180
  56.9 0.7 %copy.51 = f32[2,3,16,1,512]{4,2,1,0,3:T(8,128)} copy(f32[2,3,16,1,512]{4,3,1,0,2:T(1,128)S(1)} %bitcast.81) | data formatting | bytes 393216 | tf_op jit(solution)/shard_map/all_to_all | solution.py:180
  (6 shorter events, 0.0 us)
Async XLA Ops:
  0.0 13.4 %copy-start = (s32[32]{0:T(128)S(1)}, s32[32]{0:T(128)}, u32[]{:S(2)}) copy-start(s32[32]{0:T(128)} %param.7) | copy-start | bytes 388
  0.0 13.5 %copy-start.1 = (s32[1,256]{1,0:T(1,128)S(1)}, s32[1,256]{1,0:T(1,128)}, u32[]{:S(2)}) copy-start(s32[1,256]{1,0:T(1,128)} %param.8) | copy-start | bytes 3076
  0.0 16.8 %copy-start.2 = (f32[1,256]{1,0:T(1,128)S(1)}, f32[1,256]{1,0:T(1,128)}, u32[]{:S(2)}) copy-start(f32[1,256]{1,0:T(1,128)} %param.10) | copy-start | bytes 3076
  5.9 16.4 %all-to-all-start = ((f32[2,3,16,512]{3,0,1,2:T(2,128)}), f32[2,3,16,512]{3,0,1,2:T(2,128)S(1)}, u32[]{:S(2)}, u32[]{:S(2)}) async-start(f32[2,3,16,512]{3,0,1,2:T(2,128)} %copy.39), calls=%async_computation | async-start | bytes 393216 | tf_op jit(solution)/shard_map/all_to_all | solution.py:154
  22.5 3.6 %collective-permute-start = (f32[32,3,1,512]{3,2,1,0:T(1,128)S(1)}, f32[32,3,1,512]{3,2,1,0:T(1,128)S(1)}, u32[]{:S(2)}, u32[]{:S(2)}) collective-permute-start(f32[32,3,1,512]{3,2,1,0:T(1,128)S(1)} %bitcast.82), channel_id=1, source_target_pairs={{0,1},{1,2},{2,3},{3,4},{4,5},{5,6},{6,7},{7,8},{8,9},{9,10},{10,1... | collective-permute-start | bytes 589832 | tf_op jit(solution)/shard_map/ppermute | solution.py:25
  24.2 3.3 %collective-permute-start.1 = (f32[32,3,1,512]{3,2,1,0:T(1,128)S(1)}, f32[32,3,1,512]{3,2,1,0:T(1,128)S(1)}, u32[]{:S(2)}, u32[]{:S(2)}) collective-permute-start(f32[32,3,1,512]{3,2,1,0:T(1,128)S(1)} %bitcast.83), channel_id=1, source_target_pairs={{1,0},{2,1},{3,2},{4,3},{5,4},{6,5},{7,6},{8,7},{9,8},{10,9},{11,1... | collective-permute-start | bytes 589832 | tf_op jit(solution)/shard_map/ppermute | solution.py:26

commit v2 on v0

--- a/solution.py
+++ b/solution.py
@@ -2,6 +2,8 @@
 import jax.numpy as jnp
 from jax import lax
 from jax.sharding import PartitionSpec as P
+from jax.experimental import pallas as pl
+from jax.experimental.pallas import tpu as pltpu
 
 PREDICTION_COUNT = 4
 
@@ -114,6 +116,91 @@
     return lax.linalg.triangular_solve(factor, inner, left_side=True, lower=True, transpose_a=True)
 
 
+def gauss_jordan_steps(a):
+    n = a.shape[0]
+    lane = lax.broadcasted_iota(jnp.int32, a.shape, 1)
+    row_id = lax.broadcasted_iota(jnp.int32, (n, 1), 0)
+
+    def step(k, a):
+        pivot_row = jnp.sum(jnp.where(row_id == k, a, 0.0), axis=0, keepdims=True)
+        column = jnp.sum(jnp.where(lane == k, a, 0.0), axis=1, keepdims=True)
+        pivot = jnp.sum(jnp.where(lane[0:1] == k, pivot_row, 0.0), axis=1, keepdims=True)
+        pivot_row = pivot_row / pivot
+        column = column - (row_id == k).astype(jnp.float32)
+        return a - column * pivot_row
+
+    return lax.fori_loop(0, n, step, a, unroll=n <= 64)
+
+def contract(a, b, dims):
+    return lax.dot_general(
+        a, b, (dims, ((), ())), precision=exact, preferred_element_type=jnp.float32
+    )
+
+
+def analysis_kernel(x_ref, ob_ref, fid_col_ref, fid_row_ref, value_ref, var_ref, noise_ref, o_ref):
+    m = x_ref.shape[0]
+    x = x_ref[...]
+    ob = ob_ref[...]
+    fid_col = fid_col_ref[...]
+    fid_row = fid_row_ref[...]
+    variance = var_ref[...]
+    masks = [(fid_col == c).astype(jnp.float32) for c in range(3)]
+    masks_row = [(fid_row == c).astype(jnp.float32) for c in range(3)]
+    counts = [jnp.sum(mask, axis=0, keepdims=True) for mask in masks]
+
+    def remove_means(data):
+        centred = data
+        for mask, count in zip(masks, counts):
+            centred = centred - mask * (jnp.sum(mask * data, axis=0, keepdims=True) / count)
+        return centred
+
+    spread = remove_means(x)
+    obs_spread = remove_means(ob)
+    weight = (
+        masks[0] * (1.0 / (counts[0] - 1.0))
+        + masks[1] * (-control_weight / (counts[1] - 1.0))
+        + masks[2] * (control_weight / (counts[2] - 1.0))
+    )
+    scale_col = jnp.sqrt(masks[0] / (counts[0] - 1.0))
+    count_row = jnp.sum(masks_row[0], axis=1, keepdims=True)
+    scale_row = jnp.sqrt(masks_row[0] / (count_row - 1.0))
+    weighted = obs_spread / variance
+    inner = contract(weighted, obs_spread, ((1,), (1,)))
+    direct = (
+        jnp.sum(weighted * value_ref[...], axis=1, keepdims=True)
+        + contract(weighted * jnp.sqrt(variance), noise_ref[...], ((1,), (0,)))
+        - contract(weighted, ob, ((1,), (1,)))
+    )
+    row_id = lax.broadcasted_iota(jnp.int32, (m, m), 0)
+    col_id = lax.broadcasted_iota(jnp.int32, (m, m), 1)
+    system = (row_id == col_id).astype(jnp.float32) + scale_col * inner * scale_row
+    augmented = jnp.concatenate([system, scale_col * direct], axis=1)
+    solved = gauss_jordan_steps(augmented)[:, m:]
+    projected = direct - contract(inner, scale_col * solved, ((1,), (0,)))
+    mixing = projected * weight
+    o_ref[...] = x + contract(mixing, spread, ((0,), (0,)))
+
+
+def analysis(flat, observed, fidelity, value, variance, noise):
+    m = flat.shape[0]
+    vmem = pl.BlockSpec(memory_space=pltpu.VMEM)
+    return pl.pallas_call(
+        analysis_kernel,
+        out_shape=jax.ShapeDtypeStruct(flat.shape, jnp.float32),
+        in_specs=[vmem] * 7,
+        out_specs=vmem,
+        compiler_params=pltpu.CompilerParams(vmem_limit_bytes=48 * 1024 * 1024),
+    )(
+        flat,
+        observed,
+        fidelity.reshape(m, 1),
+        fidelity.reshape(1, m),
+        value.reshape(1, -1),
+        variance.reshape(1, -1),
+        noise,
+    )
+
+
 def shards(initial_height_velocity, member_fidelity, obs_cell, obs_value, obs_var, obs_noise):
     per_device = initial_height_velocity.shape[0]
     resident_realizations = lax.dynamic_slice_in_dim(
@@ -130,20 +217,14 @@
     flat = tile_worker.reshape(ensemble_members, -1)
     block = extended(tile_worker, (("band", 2),), tile_rows)
     observed = jnp.take(block.reshape(ensemble_members, -1), obs_cell[0], axis=1)
-    onehot, counts, member_weight = class_tables(member_fidelity)
-    spread = remove_means(flat, onehot, counts)
-    obs_spread = remove_means(observed, onehot, counts)
-    variance = obs_var[0]
-    principal = onehot[:, 0] / (counts[0] - 1.0)
-    innovation_cov = jnp.dot(
-        (obs_spread * principal[:, None]).T, obs_spread, precision=exact
-    ) + jnp.diag(variance)
-    perturbed = obs_value[0][:, None] + jnp.sqrt(variance)[:, None] * obs_noise[0] - observed.T
-    factor = jnp.linalg.cholesky(innovation_cov)
-    cross_t = jnp.dot((obs_spread * member_weight[:, None]).T, spread, precision=exact)
-    gain_t = spd_solve(factor, cross_t)
-    update = jnp.dot(perturbed.T, gain_t, precision=exact)
-    result = (flat + update).reshape(tile_worker.shape)
+    result = analysis(
+        flat,
+        observed,
+        member_fidelity,
+        obs_value[0],
+        obs_var[0],
+        obs_noise[0],
+    ).reshape(tile_worker.shape)
     return lax.all_to_all(result, "band", split_axis=0, concat_axis=2, tiled=True)
 
 

time: 121 us -> 52.4 us (0.43)
  other arithmetic: 61.8 us -> 4.69 us
  matrix products: 11.2 us -> 0 us
  local copies, waits for them, and re-layouts: 11.5 us -> 4.89 us
  waiting for transfers between devices: 4.44 us -> 10.6 us
  Pallas kernels: 0 us -> 4.3 us
  between operations: 3.77 us -> 0.21 us
    another operation x10 -> x0, other arithmetic: 55.1 us -> none  [the longest x6 34 us: shards(): factor = jnp.linalg.cholesky(innovation_cov)]
    dot_general x7 -> x0, matrix products: 5.84 us -> none  [the longest x1 1.5 us: shards(): jnp.dot((obs_spread * member_weight[:, None]).T, spread, precision=exact)]
    all_to_all x1, waiting for transfers between devices: 3.06 us -> 8.74 us  [shards(): lax.all_to_all(integrate_realizations, 'band', split_axis=2, concat_axis=...]
    another operation x8 -> x0, matrix products: 5.33 us -> none  [the longest x3 2.46 us: spd_solve(): inner = lax.linalg.triangular_solve(factor, rhs, left_side=True, lower=True)]
    another operation x9 -> x0, local copies, waits for them, and re-layouts: 5.25 us -> none
    pallas_call x0 -> x1, Pallas kernels: none -> 4.3 us  [analysis(): pl.pallas_call(analysis_kernel, out_shape=jax.ShapeDtypeStruct(flat.shape...]
  transfers between devices with their start and end apart: 3 -> 3, of which waited for: 2 -> 2; matrix products, arithmetic and copies ran while one was open for 4% -> 1% of each run, Pallas kernels for 0% -> 0%
where the time goes in v2:
time: 52.4 us; the launch traced here: 52 us
  blocking collectives  17 us (32%)
  waiting for transfers between devices  10.6 us (20%)
  starting transfers between devices  10.4 us (20%)
  local copies, waits for them, and re-layouts  4.89 us (9%)
  other arithmetic  4.69 us (9%)
  Pallas kernels  4.3 us (8%)
    all_to_all x1, blocking collectives, shards(): lax.all_to_all(result, 'band', split_axis=0, concat_axis=2, tiled=True)  17 us
    all_to_all x1, waiting for transfers between devices, shards(): lax.all_to_all(integrate_realizations, 'band', split_axis=2, concat_axis=...  8.74 us
    all_to_all x1, starting transfers between devices, shards(): lax.all_to_all(integrate_realizations, 'band', split_axis=2, concat_axis=...  7.42 us
    pallas_call x1, Pallas kernels, analysis(): pl.pallas_call(analysis_kernel, out_shape=jax.ShapeDtypeStruct(flat.shape...  4.3 us
    mul x3, other arithmetic, advance(): depth * northward  2.34 us
    ppermute x1, waiting for transfers between devices, extended(): after = lax.ppermute(leading, axis, down)  1.84 us
    ppermute x1, starting transfers between devices, extended(): before = lax.ppermute(last, axis, up)  1.65 us
    ppermute x1, starting transfers between devices, extended(): after = lax.ppermute(leading, axis, down)  1.29 us
  transfers between devices with their start and end apart: 3, of which 2 were waited for; matrix products, arithmetic and copies ran while one was open for 1% of the time, Pallas kernels for 0%

profile of v2, /device:TPU:0, one launch (start us, length us, event | category | flops | bytes accessed | tf_op | source)
XLA Modules:
  0.0 52.0 jit_solution(16733561656378058917)
XLA Ops:
  0.0 0.0 copy-start.3
  0.0 0.9 %slice_bitcast_fusion = (f32[2,16,512]{2,1,0:T(8,128)S(1)}, f32[2,16,512]{2,1,0:T(8,128)S(1)}, f32[2,16,512]{2,1,0:T(8,128)S(1)}) fusion(f32[2,3,16,512]{3,2,1,0:T(8,128)} %param.6), kind=kLoop, calls=%fused_computation.126 | loop fusion | bytes 393216 | tf_op jit(solution)/shard_map/squeeze | solution.py:86
  0.9 0.0 copy-start
  0.9 0.0 copy-start.4
  1.0 0.8 %fusion.53 = (f32[2]{0:T(128)S(1)}, f32[2]{0:T(128)S(1)}, f32[2]{0:T(128)S(1)}) fusion(s32[32]{0:T(128)} %param.7, s32[]{:T(128)S(6)} %select_n.27), kind=kLoop, calls=%fused_computation.146 | loop fusion | flops 8 | bytes 36 | tf_op jit(solution)/shard_map/neg | solution.py:60
  1.7 1.0 %fusion.45 = (f32[2,16,512]{2,1,0:T(8,128)S(1)}, f32[2,16,512]{2,1,0:T(8,128)S(1)}) fusion(f32[2]{0:T(128)S(1)} %get-tuple-element.18, f32[2,3,16,512]{3,2,1,0:T(8,128)} %param.6), kind=kLoop, calls=%fused_computation.130 | loop fusion | flops 65536 | bytes 327688 | tf_op jit(solution)/shard_map/mul | solution.py:56
  2.7 0.1 fusion.4
  2.9 1.1 %fusion.47 = (f32[2,16,512]{2,1,0:T(8,128)S(1)}, f32[2,16,512]{2,1,0:T(8,128)S(1)}, f32[2,16,512]{2,1,0:T(8,128)S(1)}, f32[2,16,512]{2,1,0:T(8,128)S(1)}) fusion(f32[2,16,512]{2,1,0:T(8,128)S(1)} %fusion.4, f32[2]{0:T(128)S(1)} %get-tuple-element.18, f32[2,16,512]{2,1,0:T(8,128)S(1)} %get-tuple-element.29, f32[2]{0:T(128)S(1)} %get-tuple-element.32, ...), kind=kLoop, calls=%fused_computation.132 | loop fusion | flops 851968 | bytes 589912 | tf_op jit(solution)/shard_map/mul | solution.py:56
  4.0 0.1 fusion.14
  4.1 0.2 fusion.49
  4.4 0.1 fusion.19
  4.5 0.2 fusion.52
  4.8 0.1 fusion.24
  4.9 0.2 fusion.32
  5.1 0.8 %copy.47 = f32[2,3,16,512]{3,0,1,2:T(2,128)} copy(f32[2,3,16,512]{3,2,0,1:T(8,128)S(1)} %pad_maximum_fusion.1) | data formatting | bytes 393216 | tf_op jit(solution)/shard_map/stack | solution.py:92
  6.0 7.4 %all-to-all-start = ((f32[2,3,16,512]{3,0,1,2:T(2,128)}), f32[2,3,16,512]{3,0,1,2:T(2,128)S(1)}, u32[]{:S(2)}, u32[]{:S(2)}) async-start(f32[2,3,16,512]{3,0,1,2:T(2,128)} %copy.47), calls=%async_computation | async-start | bytes 393216 | tf_op jit(solution)/shard_map/all_to_all | solution.py:212
  13.4 0.0 copy-done.3
  13.4 0.1 copy.52
  13.5 0.0 copy-done
  13.5 0.1 copy.53.fid_col_ref
  13.6 0.0 copy-done.4
  13.6 8.7 %all-to-all-done = f32[2,3,16,512]{3,0,1,2:T(2,128)S(1)} async-done(((f32[2,3,16,512]{3,0,1,2:T(2,128)}), f32[2,3,16,512]{3,0,1,2:T(2,128)S(1)}, u32[]{:S(2)}, u32[]{:S(2)}) %all-to-all-start) | async-done | bytes 196640 | tf_op jit(solution)/shard_map/all_to_all | solution.py:212
  22.4 0.2 copy.49
  22.6 1.7 %collective-permute-start = (f32[32,3,1,512]{3,2,1,0:T(1,128)S(1)}, f32[32,3,1,512]{3,2,1,0:T(1,128)S(1)}, u32[]{:S(2)}, u32[]{:S(2)}) collective-permute-start(f32[32,3,1,512]{3,2,1,0:T(1,128)S(1)} %bitcast.64), channel_id=1, source_target_pairs={{0,1},{1,2},{2,3},{3,4},{4,5},{5,6},{6,7},{7,8},{8,9},{9,10},{10,1... | collective-permute-start | bytes 589832 | tf_op jit(solution)/shard_map/ppermute | solution.py:25
  24.2 1.3 %collective-permute-start.1 = (f32[32,3,1,512]{3,2,1,0:T(1,128)S(1)}, f32[32,3,1,512]{3,2,1,0:T(1,128)S(1)}, u32[]{:S(2)}, u32[]{:S(2)}) collective-permute-start(f32[32,3,1,512]{3,2,1,0:T(1,128)S(1)} %bitcast.65), channel_id=1, source_target_pairs={{1,0},{2,1},{3,2},{4,3},{5,4},{6,5},{7,6},{8,7},{9,8},{10,9},{11,1... | collective-permute-start | bytes 589832 | tf_op jit(solution)/shard_map/ppermute | solution.py:26
  25.6 0.1 copy.48
  25.6 0.1 copy.59
  25.7 0.0 copy-start.1
  25.7 0.0 copy-start.2
  25.7 0.0 collective-permute-done
  25.7 1.8 %collective-permute-done.1 = f32[32,3,1,512]{3,2,1,0:T(1,128)S(1)} collective-permute-done((f32[32,3,1,512]{3,2,1,0:T(1,128)S(1)}, f32[32,3,1,512]{3,2,1,0:T(1,128)S(1)}, u32[]{:S(2)}, u32[]{:S(2)}) %collective-permute-start.1) | collective-permute-done | bytes 196640 | tf_op jit(solution)/shard_map/ppermute | solution.py:26
  27.6 0.5 pad_maximum_fusion
  28.1 0.8 %copy.50 = f32[32,3,3,512]{0,3,2,1:T(8,128)S(1)} copy(f32[32,3,3,512]{3,2,1,0:T(4,128)S(1)} %pad_maximum_fusion) | data formatting | bytes 1179648 | tf_op jit(solution)/shard_map/concatenate | solution.py:27
  28.9 0.7 %gather_fusion = f32[256,32]{1,0:T(8,128)S(1)} fusion(f32[32,4608]{0,1:T(8,128)S(1)} %bitcast.59, s32[1024]{0:T(1024)S(1)} %pad_clamp_fusion), kind=kCustom, calls=%fused_computation | custom fusion | bytes 66560 | tf_op jit(solution)/shard_map/jit(_take)/gather | solution.py:219
  29.7 0.1 copy.51
  29.8 0.0 copy-done.1
  29.8 0.0 copy-done.2
  29.8 4.3 %shard_map.64 = f32[32,1536]{1,0:T(8,128)S(1)} custom-call(f32[32,1536]{1,0:T(8,128)S(1)} %bitcast.55, f32[32,256]{1,0:T(8,128)S(1)} %select_bitcast_fusion.ob_ref, s32[32,1]{1,0:T(8,128)S(1)} %copy.53.fid_col_ref, s32[1,32]{1,0:T(1,128)S(1)} %bitcast.58, f32[1,256]{1,0:T(1,128)S(1)} %copy-done.1, f32[1,256]{1,0:T(1,128)S(1)} %copy-done.2, ...), custom_call_target="tpu_custom_call" | custom-call | tf_op jit(solution)/shard_map/pallas_call | solution.py:187
  34.1 0.2 reshape.74
  34.3 17.0 %all_to_all.36 = f32[32,3,1,512]{3,2,1,0:T(1,128)S(1)} all-to-all(f32[32,3,1,512]{3,2,1,0:T(1,128)S(1)} %reshape.74), channel_id=1, replica_groups=mesh['groups'=2,'band'=16] {'band'}, dimensions={0} | all-to-all | bytes 393216 | tf_op jit(solution)/shard_map/all_to_all | solution.py:228
  51.3 0.7 %copy.61 = f32[2,3,16,1,512]{4,2,1,0,3:T(8,128)} copy(f32[2,3,16,1,512]{4,3,1,0,2:T(1,128)S(1)} %bitcast.63) | data formatting | bytes 393216 | tf_op jit(solution)/shard_map/all_to_all | solution.py:228
  (6 shorter events, 0.1 us)
Async XLA Ops:
  0.0 13.4 %copy-start.3 = (f32[1,256,32]{1,2,0:T(8,128)S(1)}, f32[1,256,32]{1,2,0:T(8,128)}, u32[]{:S(2)}) copy-start(f32[1,256,32]{1,2,0:T(8,128)} %param.11) | copy-start | bytes 98308
  0.9 12.6 %copy-start = (s32[32]{0:T(128)S(1)}, s32[32]{0:T(128)}, u32[]{:S(2)}) copy-start(s32[32]{0:T(128)} %param.7) | copy-start | bytes 388
  0.9 12.7 %copy-start.4 = (s32[1,256]{1,0:T(1,128)S(1)}, s32[1,256]{1,0:T(1,128)}, u32[]{:S(2)}) copy-start(s32[1,256]{1,0:T(1,128)} %param.8) | copy-start | bytes 3076
  6.0 16.4 %all-to-all-start = ((f32[2,3,16,512]{3,0,1,2:T(2,128)}), f32[2,3,16,512]{3,0,1,2:T(2,128)S(1)}, u32[]{:S(2)}, u32[]{:S(2)}) async-start(f32[2,3,16,512]{3,0,1,2:T(2,128)} %copy.47), calls=%async_computation | async-start | bytes 393216 | tf_op jit(solution)/shard_map/all_to_all | solution.py:212
  22.6 3.1 %collective-permute-start = (f32[32,3,1,512]{3,2,1,0:T(1,128)S(1)}, f32[32,3,1,512]{3,2,1,0:T(1,128)S(1)}, u32[]{:S(2)}, u32[]{:S(2)}) collective-permute-start(f32[32,3,1,512]{3,2,1,0:T(1,128)S(1)} %bitcast.64), channel_id=1, source_target_pairs={{0,1},{1,2},{2,3},{3,4},{4,5},{5,6},{6,7},{7,8},{8,9},{9,10},{10,1... | collective-permute-start | bytes 589832 | tf_op jit(solution)/shard_map/ppermute | solution.py:25
  24.2 3.3 %collective-permute-start.1 = (f32[32,3,1,512]{3,2,1,0:T(1,128)S(1)}, f32[32,3,1,512]{3,2,1,0:T(1,128)S(1)}, u32[]{:S(2)}, u32[]{:S(2)}) collective-permute-start(f32[32,3,1,512]{3,2,1,0:T(1,128)S(1)} %bitcast.65), channel_id=1, source_target_pairs={{1,0},{2,1},{3,2},{4,3},{5,4},{6,5},{7,6},{8,7},{9,8},{10,9},{11,1... | collective-permute-start | bytes 589832 | tf_op jit(solution)/shard_map/ppermute | solution.py:26
  25.7 4.1 %copy-start.1 = (f32[1,256]{1,0:T(1,128)S(1)}, f32[1,256]{1,0:T(1,128)}, u32[]{:S(2)}) copy-start(f32[1,256]{1,0:T(1,128)} %value_ref.1) | copy-start | bytes 3076
  25.7 4.1 %copy-start.2 = (f32[1,256]{1,0:T(1,128)S(1)}, f32[1,256]{1,0:T(1,128)}, u32[]{:S(2)}) copy-start(f32[1,256]{1,0:T(1,128)} %var_ref.1) | copy-start | bytes 3076

commit v3 on v2

--- a/solution.py
+++ b/solution.py
@@ -120,6 +120,12 @@
     n = a.shape[0]
     lane = lax.broadcasted_iota(jnp.int32, a.shape, 1)
     row_id = lax.broadcasted_iota(jnp.int32, (n, 1), 0)
+    if n <= 64:
+        for k in range(n):
+            pivot_row = a[k : k + 1, :] * (1.0 / a[k : k + 1, k : k + 1])
+            column = a[:, k : k + 1] - (row_id == k).astype(jnp.float32)
+            a = a - column * pivot_row
+        return a
 
     def step(k, a):
         pivot_row = jnp.sum(jnp.where(row_id == k, a, 0.0), axis=0, keepdims=True)
@@ -129,7 +135,7 @@
         column = column - (row_id == k).astype(jnp.float32)
         return a - column * pivot_row
 
-    return lax.fori_loop(0, n, step, a, unroll=n <= 64)
+    return lax.fori_loop(0, n, step, a)
 
 def contract(a, b, dims):
     return lax.dot_general(
@@ -201,14 +207,86 @@
     )
 
 
+def shifted(field, offset, axis):
+    size = field.shape[axis]
+    rolled = pltpu.roll(field, (-offset) % size, axis)
+    place = lax.broadcasted_iota(jnp.int32, field.shape, axis) + offset
+    return jnp.where((place >= 0) & (place < size), rolled, 0.0)
+
+
+def kernel_neighbours(field):
+    return (shifted(field, 1, 1), shifted(field, -1, 1), shifted(field, 1, 0), shifted(field, -1, 0))
+
+
+def kernel_east(field):
+    ahead, behind, upper, lower = kernel_neighbours(field)
+    return 0.5 * (ahead - behind)
+
+
+def kernel_north(field):
+    ahead, behind, upper, lower = kernel_neighbours(field)
+    return 0.5 * (upper - lower)
+
+
+def kernel_laplace(field):
+    ahead, behind, upper, lower = kernel_neighbours(field)
+    return ahead + behind + upper + lower - 4.0 * field
+
+
+def forecast_kernel(fid_ref, x_ref, o_ref):
+    members, _, lat_rows, _ = x_ref.shape
+    row = lax.broadcasted_iota(jnp.int32, (lat_rows, 1), 0).astype(jnp.float32)
+    coriolis = 0.1 + 0.2 * (row + 0.5) / lat_rows
+    for member in range(members):
+        level = fid_ref[member]
+        nonlinear = jnp.where(level == 0, 1.0, 0.0).astype(jnp.float32)
+        friction = jnp.where(level == 0, 0.0, slow_friction).astype(jnp.float32)
+        height, eastward, northward = x_ref[member, 0], x_ref[member, 1], x_ref[member, 2]
+        for step in range(PREDICTION_COUNT):
+            depth = 1.0 + nonlinear * height
+            height_new = (
+                height
+                - time_step * (kernel_east(depth * eastward) + kernel_north(depth * northward))
+                + time_step * viscous * kernel_laplace(height)
+            )
+            east_new = eastward + time_step * (
+                -nonlinear * (eastward * kernel_east(eastward) + northward * kernel_north(eastward))
+                + coriolis * northward
+                - kernel_east(height_new)
+                + viscous * kernel_laplace(eastward)
+                - friction * eastward
+            )
+            north_new = northward + time_step * (
+                -nonlinear * (eastward * kernel_east(northward) + northward * kernel_north(northward))
+                - coriolis * eastward
+                - kernel_north(height_new)
+                + viscous * kernel_laplace(northward)
+                - friction * northward
+            )
+            height, eastward, northward = height_new, east_new, north_new
+        o_ref[member, 0] = height
+        o_ref[member, 1] = eastward
+        o_ref[member, 2] = northward
+
+
+def forecast(initial, levels):
+    return pl.pallas_call(
+        forecast_kernel,
+        out_shape=jax.ShapeDtypeStruct(initial.shape, jnp.float32),
+        in_specs=[
+            pl.BlockSpec(memory_space=pltpu.SMEM),
+            pl.BlockSpec(memory_space=pltpu.VMEM),
+        ],
+        out_specs=pl.BlockSpec(memory_space=pltpu.VMEM),
+    )(levels, initial)
+
+
 def shards(initial_height_velocity, member_fidelity, obs_cell, obs_value, obs_var, obs_noise):
     per_device = initial_height_velocity.shape[0]
     resident_realizations = lax.dynamic_slice_in_dim(
         member_fidelity, lax.axis_index("band") * per_device, per_device
     )
-    integrate_realizations = begin_prediction(
-        initial_height_velocity, resident_realizations, PREDICTION_COUNT
-    )
+    integrate_realizations = forecast(initial_height_velocity, resident_realizations)
     tile_worker = lax.all_to_all(
         integrate_realizations, "band", split_axis=2, concat_axis=0, tiled=True
     )

time: 52.4 us -> 51.5 us (0.983)
  other arithmetic: 4.69 us -> 1.9 us
  waiting for transfers between devices: 10.6 us -> 7.83 us
  local copies, waits for them, and re-layouts: 4.89 us -> 7.59 us
  Pallas kernels: 4.3 us -> 6.29 us
    pallas_call x0 -> x1, Pallas kernels: none -> 2.63 us  [forecast(): pl.pallas_call(forecast_kernel, out_shape=jax.ShapeDtypeStruct(initial.sh...]
    mul x4 -> x0, other arithmetic: 2.57 us -> none  [the longest x3 2.34 us: advance(): depth * northward]
    all_to_all x1, waiting for transfers between devices: 8.74 us -> 6.67 us  [shards(): lax.all_to_all(integrate_realizations, 'band', split_axis=2, concat_axis=...]
    pallas_call x0 -> x1, local copies, waits for them, and re-layouts: none -> 1.75 us  [forecast(): pl.pallas_call(forecast_kernel, out_shape=jax.ShapeDtypeStruct(initial.sh...]
    dynamic_slice x0 -> x1, local copies, waits for them, and re-layouts: none -> 1.32 us  [shards(): lax.dynamic_slice_in_dim(member_fidelity, lax.axis_index('band') * per_de...]
    squeeze x1 -> x0, local copies, waits for them, and re-layouts: 0.92 us -> none  [begin_prediction(): marine_condition[:, 2]]
    another operation x1 -> x0, local copies, waits for them, and re-layouts: 0.83 us -> none  [begin_prediction(): return jnp.stack([height, eastward, northward], axis=1)]
    neg x1 -> x0, other arithmetic: 0.78 us -> none  [advance(): -nonlinear]
  transfers between devices with their start and end apart: 3 -> 3, of which waited for: 2 -> 2; matrix products, arithmetic and copies ran while one was open for 1% -> 6% of each run, Pallas kernels for 0% -> 0%
where the time goes in v3:
time: 51.5 us; the launch traced here: 51.1 us
  blocking collectives  17 us (33%)
  starting transfers between devices  10.4 us (20%)
  waiting for transfers between devices  7.83 us (15%)
  local copies, waits for them, and re-layouts  7.59 us (15%)
  Pallas kernels  6.29 us (12%)
  other arithmetic  1.9 us (4%)
    all_to_all x1, blocking collectives, shards(): lax.all_to_all(result, 'band', split_axis=0, concat_axis=2, tiled=True)  17 us
    all_to_all x1, starting transfers between devices, shards(): lax.all_to_all(integrate_realizations, 'band', split_axis=2, concat_axis=...  7.41 us
    all_to_all x1, waiting for transfers between devices, shards(): lax.all_to_all(integrate_realizations, 'band', split_axis=2, concat_axis=...  6.67 us
    pallas_call x1, Pallas kernels, analysis(): pl.pallas_call(analysis_kernel, out_shape=jax.ShapeDtypeStruct(flat.shape...  3.67 us
    pallas_call x1, Pallas kernels, forecast(): pl.pallas_call(forecast_kernel, out_shape=jax.ShapeDtypeStruct(initial.sh...  2.63 us
    pallas_call x1, local copies, waits for them, and re-layouts, forecast(): pl.pallas_call(forecast_kernel, out_shape=jax.ShapeDtypeStruct(initial.sh...  1.75 us
    ppermute x1, starting transfers between devices, extended(): before = lax.ppermute(last, axis, up)  1.65 us
    dynamic_slice x1, local copies, waits for them, and re-layouts, shards(): lax.dynamic_slice_in_dim(member_fidelity, lax.axis_index('band') * per_de...  1.32 us
  transfers between devices with their start and end apart: 3, of which 2 were waited for; matrix products, arithmetic and copies ran while one was open for 6% of the time, Pallas kernels for 0%

profile of v3, /device:TPU:0, one launch (start us, length us, event | category | flops | bytes accessed | tf_op | source)
XLA Modules:
  0.0 51.1 jit_solution(3091108045462138597)
XLA Ops:
  0.0 1.3 %dynamic_slice.3.fid_ref = s32[2]{0:T(128)} dynamic-slice(s32[32]{0:T(128)} %param.7, s32[]{:T(128)S(6)} %select_n.23), dynamic_slice_sizes={2} | dynamic-slice | bytes 20 | tf_op jit(solution)/shard_map/dynamic_slice | solution.py:286
  1.3 2.6 %shard_map.64 = f32[2,3,16,512]{3,2,1,0:T(8,128)} custom-call(s32[2]{0:T(128)} %dynamic_slice.3.fid_ref, f32[2,3,16,512]{3,2,1,0:T(8,128)} %x_ref.1), custom_call_target="tpu_custom_call" | custom-call | tf_op jit(solution)/shard_map/pallas_call | solution.py:273
  3.9 1.7 %copy.32 = f32[2,3,16,512]{3,0,1,2:T(2,128)} copy(f32[2,3,16,512]{3,2,1,0:T(8,128)} %shard_map.64) | data formatting | bytes 393216 | tf_op jit(solution)/shard_map/pallas_call | solution.py:273
  5.7 7.4 %all-to-all-start = ((f32[2,3,16,512]{3,0,1,2:T(2,128)}), f32[2,3,16,512]{3,0,1,2:T(2,128)S(1)}, u32[]{:S(2)}, u32[]{:S(2)}) async-start(f32[2,3,16,512]{3,0,1,2:T(2,128)} %copy.32), calls=%async_computation | async-start | bytes 393216 | tf_op jit(solution)/shard_map/all_to_all | solution.py:290
  13.1 0.9 %copy.37 = f32[1,256,32]{2,1,0:T(8,128)S(1)} copy(f32[1,256,32]{1,2,0:T(8,128)} %param.11) | data formatting | bytes 65536 | tf_op args[5]
  14.0 0.7 %copy.38.fid_col_ref = s32[32,1]{1,0:T(8,128)S(1)} copy(s32[32,1]{0,1:T(1,128)} %bitcast.26) | data formatting | bytes 256 | tf_op jit(solution)/shard_map/reshape | solution.py:202
  14.7 0.7 %compare_select_fusion = s32[256,1]{0,1:T(1,128)S(1)} fusion(s32[1,256]{1,0:T(1,128)} %param.8), kind=kLoop, calls=%fused_computation.4 | loop fusion | flops 768 | bytes 2048 | tf_op jit(solution)/shard_map/jit(_take)/jit(_where)/select_n | solution.py:297
  15.4 6.7 %all-to-all-done = f32[2,3,16,512]{3,0,1,2:T(2,128)S(1)} async-done(((f32[2,3,16,512]{3,0,1,2:T(2,128)}), f32[2,3,16,512]{3,0,1,2:T(2,128)S(1)}, u32[]{:S(2)}, u32[]{:S(2)}) %all-to-all-start) | async-done | bytes 196640 | tf_op jit(solution)/shard_map/all_to_all | solution.py:290
  22.1 0.2 copy.34
  22.3 1.7 %collective-permute-start = (f32[32,3,1,512]{3,2,1,0:T(1,128)S(1)}, f32[32,3,1,512]{3,2,1,0:T(1,128)S(1)}, u32[]{:S(2)}, u32[]{:S(2)}) collective-permute-start(f32[32,3,1,512]{3,2,1,0:T(1,128)S(1)} %bitcast.33), channel_id=1, source_target_pairs={{0,1},{1,2},{2,3},{3,4},{4,5},{5,6},{6,7},{7,8},{8,9},{9,10},{10,1... | collective-permute-start | bytes 589832 | tf_op jit(solution)/shard_map/ppermute | solution.py:25
  23.9 1.3 %collective-permute-start.1 = (f32[32,3,1,512]{3,2,1,0:T(1,128)S(1)}, f32[32,3,1,512]{3,2,1,0:T(1,128)S(1)}, u32[]{:S(2)}, u32[]{:S(2)}) collective-permute-start(f32[32,3,1,512]{3,2,1,0:T(1,128)S(1)} %bitcast.34), channel_id=1, source_target_pairs={{1,0},{2,1},{3,2},{4,3},{5,4},{6,5},{7,6},{8,7},{9,8},{10,9},{11,1... | collective-permute-start | bytes 589832 | tf_op jit(solution)/shard_map/ppermute | solution.py:26
  25.2 0.7 %compare_and_fusion = pred[256]{0:T(512)(128)(4,1)S(1)} fusion(s32[256]{0:T(256)} %bitcast.37), kind=kLoop, calls=%fused_computation.7 | loop fusion | flops 1536 | bytes 1280 | tf_op jit(solution)/shard_map/jit(_take)/and | solution.py:297
  25.9 0.1 copy.33
  26.0 0.1 copy.41
  26.1 0.0 copy-start
  26.1 0.0 copy-start.1
  26.1 0.0 copy-start.2
  26.1 0.0 collective-permute-done
  26.1 1.2 %collective-permute-done.1 = f32[32,3,1,512]{3,2,1,0:T(1,128)S(1)} collective-permute-done((f32[32,3,1,512]{3,2,1,0:T(1,128)S(1)}, f32[32,3,1,512]{3,2,1,0:T(1,128)S(1)}, u32[]{:S(2)}, u32[]{:S(2)}) %collective-permute-start.1) | collective-permute-done | bytes 196640 | tf_op jit(solution)/shard_map/ppermute | solution.py:26
  27.3 0.5 %pad_maximum_fusion = f32[32,3,3,512]{3,2,1,0:T(4,128)S(1)} fusion(f32[32,3,1,512]{3,2,1,0:T(1,128)S(1)} %collective-permute-done.1, f32[32,3,1,512]{3,2,1,0:T(1,128)S(1)} %bitcast.35, f32[32,3,1,512]{3,2,1,0:T(1,128)S(1)} %collective-permute-done), kind=kLoop, calls=%fused_computation.1 | loop fusion | flops 294912 | bytes 1179648 | tf_op jit(solution)/shard_map/concatenate | solution.py:27
  27.8 0.8 %copy.35 = f32[32,3,3,512]{0,3,2,1:T(8,128)S(1)} copy(f32[32,3,3,512]{3,2,1,0:T(4,128)S(1)} %pad_maximum_fusion) | data formatting | bytes 1179648 | tf_op jit(solution)/shard_map/concatenate | solution.py:27
  28.6 0.7 %gather_fusion = f32[256,32]{1,0:T(8,128)S(1)} fusion(f32[32,4608]{0,1:T(8,128)S(1)} %bitcast.28, s32[1024]{0:T(1024)S(1)} %pad_clamp_fusion), kind=kCustom, calls=%fused_computation | custom fusion | bytes 66560 | tf_op jit(solution)/shard_map/jit(_take)/gather | solution.py:297
  29.4 0.1 copy.36
  29.5 0.0 copy-done
  29.5 0.0 copy-done.1
  29.5 0.0 copy-done.2
  29.5 3.7 %shard_map.65 = f32[32,1536]{1,0:T(8,128)S(1)} custom-call(f32[32,1536]{1,0:T(8,128)S(1)} %bitcast.24, f32[32,256]{1,0:T(8,128)S(1)} %select_bitcast_fusion.ob_ref, s32[32,1]{1,0:T(8,128)S(1)} %copy.38.fid_col_ref, s32[1,32]{1,0:T(1,128)S(1)} %bitcast.27, f32[1,256]{1,0:T(1,128)S(1)} %copy-done.1, f32[1,256]{1,0:T(1,128)S(1)} %copy-done.2, ...), custom_call_target="tpu_custom_call" | custom-call | tf_op jit(solution)/shard_map/pallas_call | solution.py:193
  33.2 0.2 reshape.63
  33.4 17.0 %all_to_all.36 = f32[32,3,1,512]{3,2,1,0:T(1,128)S(1)} all-to-all(f32[32,3,1,512]{3,2,1,0:T(1,128)S(1)} %reshape.63), channel_id=1, replica_groups=mesh['groups'=2,'band'=16] {'band'}, dimensions={0} | all-to-all | bytes 393216 | tf_op jit(solution)/shard_map/all_to_all | solution.py:306
  50.4 0.7 %copy.43 = f32[2,3,16,1,512]{4,2,1,0,3:T(8,128)} copy(f32[2,3,16,1,512]{4,3,1,0,2:T(1,128)S(1)} %bitcast.32) | data formatting | bytes 393216 | tf_op jit(solution)/shard_map/all_to_all | solution.py:306
  (2 shorter events, 0.0 us)
Async XLA Ops:
  5.7 16.4 %all-to-all-start = ((f32[2,3,16,512]{3,0,1,2:T(2,128)}), f32[2,3,16,512]{3,0,1,2:T(2,128)S(1)}, u32[]{:S(2)}, u32[]{:S(2)}) async-start(f32[2,3,16,512]{3,0,1,2:T(2,128)} %copy.32), calls=%async_computation | async-start | bytes 393216 | tf_op jit(solution)/shard_map/all_to_all | solution.py:290
  22.3 3.8 %collective-permute-start = (f32[32,3,1,512]{3,2,1,0:T(1,128)S(1)}, f32[32,3,1,512]{3,2,1,0:T(1,128)S(1)}, u32[]{:S(2)}, u32[]{:S(2)}) collective-permute-start(f32[32,3,1,512]{3,2,1,0:T(1,128)S(1)} %bitcast.33), channel_id=1, source_target_pairs={{0,1},{1,2},{2,3},{3,4},{4,5},{5,6},{6,7},{7,8},{8,9},{9,10},{10,1... | collective-permute-start | bytes 589832 | tf_op jit(solution)/shard_map/ppermute | solution.py:25
  23.9 3.3 %collective-permute-start.1 = (f32[32,3,1,512]{3,2,1,0:T(1,128)S(1)}, f32[32,3,1,512]{3,2,1,0:T(1,128)S(1)}, u32[]{:S(2)}, u32[]{:S(2)}) collective-permute-start(f32[32,3,1,512]{3,2,1,0:T(1,128)S(1)} %bitcast.34), channel_id=1, source_target_pairs={{1,0},{2,1},{3,2},{4,3},{5,4},{6,5},{7,6},{8,7},{9,8},{10,9},{11,1... | collective-permute-start | bytes 589832 | tf_op jit(solution)/shard_map/ppermute | solution.py:26
  26.1 3.4 %copy-start = (s32[32]{0:T(128)S(1)}, s32[32]{0:T(128)}, u32[]{:S(2)}) copy-start(s32[32]{0:T(128)} %param.7) | copy-start | bytes 388
  26.1 3.4 %copy-start.1 = (f32[1,256]{1,0:T(1,128)S(1)}, f32[1,256]{1,0:T(1,128)}, u32[]{:S(2)}) copy-start(f32[1,256]{1,0:T(1,128)} %value_ref.1) | copy-start | bytes 3076
  26.1 3.4 %copy-start.2 = (f32[1,256]{1,0:T(1,128)S(1)}, f32[1,256]{1,0:T(1,128)}, u32[]{:S(2)}) copy-start(f32[1,256]{1,0:T(1,128)} %var_ref.1) | copy-start | bytes 3076

commit v4 on v3

--- a/solution.py
+++ b/solution.py
@@ -144,11 +144,13 @@
 
 
 def analysis_kernel(x_ref, ob_ref, fid_col_ref, fid_row_ref, value_ref, var_ref, noise_ref, o_ref):
-    m = x_ref.shape[0]
-    x = x_ref[...]
+    per_device = fid_col_ref.shape[1]
+    width = x_ref.shape[1] // per_device
+    x = jnp.concatenate([x_ref[:, i * width : (i + 1) * width] for i in range(per_device)], axis=0)
+    m = x.shape[0]
     ob = ob_ref[...]
-    fid_col = fid_col_ref[...]
-    fid_row = fid_row_ref[...]
+    fid_col = jnp.concatenate([fid_col_ref[:, i : i + 1] for i in range(per_device)], axis=0)
+    fid_row = jnp.concatenate([fid_row_ref[i : i + 1, :] for i in range(per_device)], axis=1)
     variance = var_ref[...]
     masks = [(fid_col == c).astype(jnp.float32) for c in range(3)]
     masks_row = [(fid_row == c).astype(jnp.float32) for c in range(3)]
@@ -184,23 +186,26 @@
     solved = gauss_jordan_steps(augmented)[:, m:]
     projected = direct - contract(inner, scale_col * solved, ((1,), (0,)))
     mixing = projected * weight
-    o_ref[...] = x + contract(mixing, spread, ((0,), (0,)))
-
-
-def analysis(flat, observed, fidelity, value, variance, noise):
-    m = flat.shape[0]
+    result = x + contract(mixing, spread, ((0,), (0,)))
+    sources = x_ref.shape[0]
+    for i in range(per_device):
+        o_ref[:, i * width : (i + 1) * width] = result[i * sources : (i + 1) * sources]
+
+
+def analysis(rows, observed, fidelity, value, variance, noise):
+    sources = rows.shape[0]
     vmem = pl.BlockSpec(memory_space=pltpu.VMEM)
     return pl.pallas_call(
         analysis_kernel,
-        out_shape=jax.ShapeDtypeStruct(flat.shape, jnp.float32),
+        out_shape=jax.ShapeDtypeStruct(rows.shape, jnp.float32),
         in_specs=[vmem] * 7,
         out_specs=vmem,
         compiler_params=pltpu.CompilerParams(vmem_limit_bytes=48 * 1024 * 1024),
     )(
-        flat,
+        rows,
         observed,
-        fidelity.reshape(m, 1),
-        fidelity.reshape(1, m),
+        fidelity.reshape(sources, -1),
+        fidelity.reshape(sources, -1).T,
         value.reshape(1, -1),
         variance.reshape(1, -1),
         noise,
@@ -234,11 +239,12 @@
 
 
 def forecast_kernel(fid_ref, x_ref, o_ref):
-    members, _, lat_rows, _ = x_ref.shape
+    members, _, lat_rows, lon = x_ref.shape
+    first = lax.axis_index("band") * members
     row = lax.broadcasted_iota(jnp.int32, (lat_rows, 1), 0).astype(jnp.float32)
     coriolis = 0.1 + 0.2 * (row + 0.5) / lat_rows
     for member in range(members):
-        level = fid_ref[member]
+        level = fid_ref[first + member]
         nonlinear = jnp.where(level == 0, 1.0, 0.0).astype(jnp.float32)
         friction = jnp.where(level == 0, 0.0, slow_friction).astype(jnp.float32)
         height, eastward, northward = x_ref[member, 0], x_ref[member, 1], x_ref[member, 2]
@@ -264,15 +270,15 @@
                 - friction * northward
             )
             height, eastward, northward = height_new, east_new, north_new
-        o_ref[member, 0] = height
-        o_ref[member, 1] = eastward
-        o_ref[member, 2] = northward
+        for component, field in enumerate((height, eastward, northward)):
+            o_ref[:, pl.ds((member * 3 + component) * lon, lon)] = field
 
 
 def forecast(initial, levels):
+    members, components, lat_rows, lon = initial.shape
     return pl.pallas_call(
         forecast_kernel,
-        out_shape=jax.ShapeDtypeStruct(initial.shape, jnp.float32),
+        out_shape=jax.ShapeDtypeStruct((lat_rows, members * components * lon), jnp.float32),
         in_specs=[
             pl.BlockSpec(memory_space=pltpu.SMEM),
             pl.BlockSpec(memory_space=pltpu.VMEM),
@@ -282,28 +288,23 @@
 
 
 def shards(initial_height_velocity, member_fidelity, obs_cell, obs_value, obs_var, obs_noise):
-    per_device = initial_height_velocity.shape[0]
-    resident_realizations = lax.dynamic_slice_in_dim(
-        member_fidelity, lax.axis_index("band") * per_device, per_device
-    )
-    integrate_realizations = forecast(initial_height_velocity, resident_realizations)
-    tile_worker = lax.all_to_all(
-        integrate_realizations, "band", split_axis=2, concat_axis=0, tiled=True
-    )
-    ensemble_members = tile_worker.shape[0]
-    tile_rows = tile_worker.shape[2]
-    flat = tile_worker.reshape(ensemble_members, -1)
-    block = extended(tile_worker, (("band", 2),), tile_rows)
-    observed = jnp.take(block.reshape(ensemble_members, -1), obs_cell[0], axis=1)
-    result = analysis(
-        flat,
-        observed,
-        member_fidelity,
-        obs_value[0],
-        obs_var[0],
-        obs_noise[0],
-    ).reshape(tile_worker.shape)
-    return lax.all_to_all(result, "band", split_axis=0, concat_axis=2, tiled=True)
+    per_device, components, lat_rows, lon = initial_height_velocity.shape
+    sources = lax.axis_size("band")
+    rows = forecast(initial_height_velocity, member_fidelity)
+    rows = lax.all_to_all(rows, "band", 0, 0, tiled=True)
+    up = [(i, i + 1) for i in range(sources - 1)]
+    down = [(j, i) for i, j in up]
+    below = lax.ppermute(rows, "band", up)
+    above = lax.ppermute(rows, "band", down)
+    block = jnp.stack([below, rows, above]).reshape(3, sources, per_device, components, lon)
+    block = jnp.transpose(block, (2, 1, 3, 0, 4)).reshape(sources * per_device, -1)
+    observed = jnp.take(block, obs_cell[0], axis=1)
+    noise = obs_noise[0].reshape(-1, sources, per_device)
+    noise = jnp.transpose(noise, (0, 2, 1)).reshape(-1, sources * per_device)
+    result = analysis(rows, observed, member_fidelity, obs_value[0], obs_var[0], noise)
+    result = lax.all_to_all(result, "band", 0, 0, tiled=True)
+    result = result.reshape(lat_rows, per_device, components, lon)
+    return jnp.transpose(result, (1, 2, 0, 3))
 
 
 def solution(mesh):

time: 51.5 us -> 51.4 us (level)
  waiting for transfers between devices: 7.83 us -> 7.1 us
  other arithmetic: 1.9 us -> 2.53 us
    pallas_call x1 -> x0, local copies, waits for them, and re-layouts: 1.75 us -> none  [forecast(): pl.pallas_call(forecast_kernel, out_shape=jax.ShapeDtypeStruct(initial.sh...]
    dynamic_slice x1 -> x0, local copies, waits for them, and re-layouts: 1.32 us -> none  [shards(): lax.dynamic_slice_in_dim(member_fidelity, lax.axis_index('band') * per_de...]
    another operation x0 -> x4, local copies, waits for them, and re-layouts: none -> 1.23 us  [the longest x1 0.79 us: shards(): noise = obs_noise[0].reshape(-1, sources, per_device)]
    transpose x0 -> x3, local copies, waits for them, and re-layouts: none -> 1.21 us  [the longest x1 0.8 us: shards(): return jnp.transpose(result, (1, 2, 0, 3))]
    reshape x2 -> x6, local copies, waits for them, and re-layouts: 0.97 us -> 2.17 us  [the longest x2 1.11 us: shards(): jnp.transpose(block, (2, 1, 3, 0, 4)).reshape(sources * per_device, -1)]
    all_to_all x3 -> x2, local copies, waits for them, and re-layouts: 0.99 us -> 2 us  [the longest x1 1.8 us: shards(): rows = lax.all_to_all(rows, 'band', 0, 0, tiled=True)]
    all_to_all x0 -> x2, other arithmetic: none -> 0.93 us  [the longest x1 0.47 us: shards(): rows = lax.all_to_all(rows, 'band', 0, 0, tiled=True)]
    unnamed x8 -> x5, local copies, waits for them, and re-layouts: 0.94 us -> 0.05 us
  transfers between devices with their start and end apart: 3 -> 3, of which waited for: 2 -> 2; matrix products, arithmetic and copies ran while one was open for 6% -> 8% of each run, Pallas kernels for 0% -> 0%
where the time goes in v4:
time: 51.4 us; the launch traced here: 51 us
  blocking collectives  17 us (33%)
  starting transfers between devices  10.4 us (20%)
  local copies, waits for them, and re-layouts  7.46 us (15%)
  waiting for transfers between devices  7.1 us (14%)
  Pallas kernels  6.35 us (12%)
  other arithmetic  2.53 us (5%)
    all_to_all x1, blocking collectives, shards(): result = lax.all_to_all(result, 'band', 0, 0, tiled=True)  17 us
    all_to_all x1, starting transfers between devices, shards(): rows = lax.all_to_all(rows, 'band', 0, 0, tiled=True)  7.41 us
    all_to_all x1, waiting for transfers between devices, shards(): rows = lax.all_to_all(rows, 'band', 0, 0, tiled=True)  6.54 us
    pallas_call x1, Pallas kernels, analysis(): pl.pallas_call(analysis_kernel, out_shape=jax.ShapeDtypeStruct(rows.shape...  3.73 us
    pallas_call x1, Pallas kernels, forecast(): pl.pallas_call(forecast_kernel, out_shape=jax.ShapeDtypeStruct((lat_rows,...  2.62 us
    all_to_all x1, local copies, waits for them, and re-layouts, shards(): rows = lax.all_to_all(rows, 'band', 0, 0, tiled=True)  1.8 us
    ppermute x1, starting transfers between devices, shards(): below = lax.ppermute(rows, 'band', up)  1.65 us
    ppermute x1, starting transfers between devices, shards(): above = lax.ppermute(rows, 'band', down)  1.29 us
  transfers between devices with their start and end apart: 3, of which 2 were waited for; matrix products, arithmetic and copies ran while one was open for 8% of the time, Pallas kernels for 0%

profile of v4, /device:TPU:0, one launch (start us, length us, event | category | flops | bytes accessed | tf_op | source)
XLA Modules:
  0.0 51.0 jit_solution(9041874468644611628)
XLA Ops:
  0.0 2.6 %shard_map.64 = f32[16,3072]{1,0:T(8,128)} custom-call(s32[32]{0:T(128)} %fid_ref.1, f32[2,3,16,512]{3,2,1,0:T(8,128)} %x_ref.1), custom_call_target="tpu_custom_call" | custom-call | tf_op jit(solution)/shard_map/pallas_call | solution.py:279
  2.6 1.8 %copy.25 = f32[16,1,3072]{2,1,0:T(1,128)} copy(f32[16,1,3072]{2,0,1:T(8,128)} %bitcast.25) | data formatting | bytes 393216 | tf_op jit(solution)/shard_map/all_to_all | solution.py:294
  4.4 7.4 %all-to-all-start = ((f32[16,1,3072]{2,1,0:T(1,128)}), f32[16,1,3072]{2,1,0:T(1,128)S(1)}, u32[]{:S(2)}, u32[]{:S(2)}) async-start(f32[16,1,3072]{2,1,0:T(1,128)} %copy.25), calls=%async_computation | async-start | bytes 393216 | tf_op jit(solution)/shard_map/all_to_all | solution.py:294
  11.8 0.7 %reshape.61.fid_col_ref = s32[16,2]{1,0:T(8,128)S(1)} reshape(s32[32]{0:T(128)} %fid_ref.1) | data formatting | bytes 256 | tf_op jit(solution)/shard_map/reshape | solution.py:207
  12.6 0.1 copy.29
  12.7 0.8 %reshape_squeeze.3 = f32[256,16,2]{0,2,1:T(2,128)S(1)} reshape(f32[1,256,32]{1,2,0:T(8,128)} %param.11) | data formatting | bytes 65536 | tf_op jit(solution)/shard_map/reshape;squeeze | solution.py:302
  13.5 0.1 copy.31.noise_ref
  13.6 0.7 %compare_select_fusion = s32[256,1]{0,1:T(1,128)S(1)} fusion(s32[1,256]{1,0:T(1,128)} %param.8), kind=kLoop, calls=%fused_computation.4 | loop fusion | flops 768 | bytes 2048 | tf_op jit(solution)/shard_map/jit(_take)/jit(_where)/select_n | solution.py:301
  14.3 6.5 %all-to-all-done = f32[16,1,3072]{2,1,0:T(1,128)S(1)} async-done(((f32[16,1,3072]{2,1,0:T(1,128)}), f32[16,1,3072]{2,1,0:T(1,128)S(1)}, u32[]{:S(2)}, u32[]{:S(2)}) %all-to-all-start) | async-done | bytes 196640 | tf_op jit(solution)/shard_map/all_to_all | solution.py:294
  20.9 1.7 %collective-permute-start = (f32[16,3072]{1,0:T(8,128)S(1)}, f32[16,3072]{1,0:T(8,128)S(1)}, u32[]{:S(2)}, u32[]{:S(2)}) collective-permute-start(f32[16,3072]{1,0:T(8,128)S(1)} %bitcast.19), channel_id=1, source_target_pairs={{0,1},{1,2},{2,3},{3,4},{4,5},{5,6},{6,7},{7,8},{8,9},{9,10},{10,1... | collective-permute-start | bytes 589832 | tf_op jit(solution)/shard_map/ppermute | solution.py:297
  22.5 1.3 %collective-permute-start.1 = (f32[16,3072]{1,0:T(8,128)S(1)}, f32[16,3072]{1,0:T(8,128)S(1)}, u32[]{:S(2)}, u32[]{:S(2)}) collective-permute-start(f32[16,3072]{1,0:T(8,128)S(1)} %bitcast.20), channel_id=1, source_target_pairs={{1,0},{2,1},{3,2},{4,3},{5,4},{6,5},{7,6},{8,7},{9,8},{10,9},{11,1... | collective-permute-start | bytes 589832 | tf_op jit(solution)/shard_map/ppermute | solution.py:298
  23.8 0.7 %compare_and_fusion = pred[256]{0:T(512)(128)(4,1)S(1)} fusion(s32[256]{0:T(256)} %bitcast.29), kind=kLoop, calls=%fused_computation.7 | loop fusion | flops 1536 | bytes 1280 | tf_op jit(solution)/shard_map/jit(_take)/and | solution.py:301
  24.5 0.5 reduce
  25.0 0.1 stack.13
  25.1 0.0 collective-permute-done
  25.1 0.1 stack.12
  25.3 0.6 %collective-permute-done.1 = f32[16,3072]{1,0:T(8,128)S(1)} collective-permute-done((f32[16,3072]{1,0:T(8,128)S(1)}, f32[16,3072]{1,0:T(8,128)S(1)}, u32[]{:S(2)}, u32[]{:S(2)}) %collective-permute-start.1) | collective-permute-done | bytes 196640 | tf_op jit(solution)/shard_map/ppermute | solution.py:298
  25.8 0.1 stack.14
  26.0 0.2 maximum_bitcast_fusion
  26.2 0.4 copy.26
  26.6 0.0 copy-start
  26.6 0.0 copy-start.1
  26.7 0.4 reshape.60
  27.1 0.7 %copy.27 = f32[32,4608]{0,1:T(8,128)S(1)} copy(f32[32,4608]{1,0:T(8,128)S(1)} %reshape.60) | data formatting | bytes 1179648 | tf_op jit(solution)/shard_map/reshape | solution.py:300
  27.8 0.7 %gather_fusion = f32[256,32]{1,0:T(8,128)S(1)} fusion(f32[32,4608]{0,1:T(8,128)S(1)} %copy.27, s32[1024]{0:T(1024)S(1)} %pad_clamp_fusion), kind=kCustom, calls=%fused_computation | custom fusion | bytes 66560 | tf_op jit(solution)/shard_map/jit(_take)/gather | solution.py:301
  28.5 0.1 copy.28
  28.6 0.0 copy-done
  28.6 0.0 copy-done.1
  28.6 3.7 %shard_map.65 = f32[16,3072]{1,0:T(8,128)S(1)} custom-call(f32[16,3072]{1,0:T(8,128)S(1)} %bitcast.21, f32[32,256]{1,0:T(8,128)S(1)} %select_bitcast_fusion.ob_ref, s32[16,2]{1,0:T(8,128)S(1)} %reshape.61.fid_col_ref, s32[2,16]{1,0:T(2,128)S(1)} %bitcast.23, f32[1,256]{1,0:T(1,128)S(1)} %copy-done, f32[1,256]{1,0:T(1,128)S(1)} %copy-done.1, ...), custom_call_target="tpu_custom_call" | custom-call | tf_op jit(solution)/shard_map/pallas_call | solution.py:198
  32.3 0.2 copy.32
  32.6 17.0 %all_to_all.20 = f32[16,1,3072]{2,1,0:T(1,128)S(1)} all-to-all(f32[16,1,3072]{2,1,0:T(1,128)S(1)} %copy.32), channel_id=1, replica_groups=mesh['groups'=2,'band'=16] {'band'}, dimensions={0} | all-to-all | bytes 393216 | tf_op jit(solution)/shard_map/all_to_all | solution.py:305
  49.5 0.5 reduce.1
  50.0 0.1 reshape.63
  50.2 0.8 %copy.33 = f32[2,3,16,512]{3,2,1,0:T(8,128)} copy(f32[2,3,16,512]{3,1,0,2:T(4,128)S(1)} %bitcast.24) | data formatting | bytes 393216 | tf_op jit(solution)/shard_map/transpose | solution.py:307
  (4 shorter events, 0.1 us)
Async XLA Ops:
  4.4 16.4 %all-to-all-start = ((f32[16,1,3072]{2,1,0:T(1,128)}), f32[16,1,3072]{2,1,0:T(1,128)S(1)}, u32[]{:S(2)}, u32[]{:S(2)}) async-start(f32[16,1,3072]{2,1,0:T(1,128)} %copy.25), calls=%async_computation | async-start | bytes 393216 | tf_op jit(solution)/shard_map/all_to_all | solution.py:294
  20.9 4.3 %collective-permute-start = (f32[16,3072]{1,0:T(8,128)S(1)}, f32[16,3072]{1,0:T(8,128)S(1)}, u32[]{:S(2)}, u32[]{:S(2)}) collective-permute-start(f32[16,3072]{1,0:T(8,128)S(1)} %bitcast.19), channel_id=1, source_target_pairs={{0,1},{1,2},{2,3},{3,4},{4,5},{5,6},{6,7},{7,8},{8,9},{9,10},{10,1... | collective-permute-start | bytes 589832 | tf_op jit(solution)/shard_map/ppermute | solution.py:297
  22.5 3.3 %collective-permute-start.1 = (f32[16,3072]{1,0:T(8,128)S(1)}, f32[16,3072]{1,0:T(8,128)S(1)}, u32[]{:S(2)}, u32[]{:S(2)}) collective-permute-start(f32[16,3072]{1,0:T(8,128)S(1)} %bitcast.20), channel_id=1, source_target_pairs={{1,0},{2,1},{3,2},{4,3},{5,4},{6,5},{7,6},{8,7},{9,8},{10,9},{11,1... | collective-permute-start | bytes 589832 | tf_op jit(solution)/shard_map/ppermute | solution.py:298
  26.6 2.0 %copy-start = (f32[1,256]{1,0:T(1,128)S(1)}, f32[1,256]{1,0:T(1,128)}, u32[]{:S(2)}) copy-start(f32[1,256]{1,0:T(1,128)} %value_ref.1) | copy-start | bytes 3076
  26.6 2.0 %copy-start.1 = (f32[1,256]{1,0:T(1,128)S(1)}, f32[1,256]{1,0:T(1,128)}, u32[]{:S(2)}) copy-start(f32[1,256]{1,0:T(1,128)} %var_ref.1) | copy-start | bytes 3076

commit v5 on v4

--- a/solution.py
+++ b/solution.py
@@ -145,8 +145,8 @@
 
 def analysis_kernel(x_ref, ob_ref, fid_col_ref, fid_row_ref, value_ref, var_ref, noise_ref, o_ref):
     per_device = fid_col_ref.shape[1]
-    width = x_ref.shape[1] // per_device
-    x = jnp.concatenate([x_ref[:, i * width : (i + 1) * width] for i in range(per_device)], axis=0)
+    width = x_ref.shape[2] // per_device
+    x = jnp.concatenate([x_ref[:, 0, i * width : (i + 1) * width] for i in range(per_device)], axis=0)
     m = x.shape[0]
     ob = ob_ref[...]
     fid_col = jnp.concatenate([fid_col_ref[:, i : i + 1] for i in range(per_device)], axis=0)
@@ -189,7 +189,7 @@
     result = x + contract(mixing, spread, ((0,), (0,)))
     sources = x_ref.shape[0]
     for i in range(per_device):
-        o_ref[:, i * width : (i + 1) * width] = result[i * sources : (i + 1) * sources]
+        o_ref[:, 0, i * width : (i + 1) * width] = result[i * sources : (i + 1) * sources]
 
 
 def analysis(rows, observed, fidelity, value, variance, noise):
@@ -271,14 +271,14 @@
             )
             height, eastward, northward = height_new, east_new, north_new
         for component, field in enumerate((height, eastward, northward)):
-            o_ref[:, pl.ds((member * 3 + component) * lon, lon)] = field
+            o_ref[:, 0, pl.ds((member * 3 + component) * lon, lon)] = field
 
 
 def forecast(initial, levels):
     members, components, lat_rows, lon = initial.shape
     return pl.pallas_call(
         forecast_kernel,
-        out_shape=jax.ShapeDtypeStruct((lat_rows, members * components * lon), jnp.float32),
+        out_shape=jax.ShapeDtypeStruct((lat_rows, 1, members * components * lon), jnp.float32),
         in_specs=[
             pl.BlockSpec(memory_space=pltpu.SMEM),
             pl.BlockSpec(memory_space=pltpu.VMEM),
@@ -296,8 +296,8 @@
     down = [(j, i) for i, j in up]
     below = lax.ppermute(rows, "band", up)
     above = lax.ppermute(rows, "band", down)
-    block = jnp.stack([below, rows, above]).reshape(3, sources, per_device, components, lon)
-    block = jnp.transpose(block, (2, 1, 3, 0, 4)).reshape(sources * per_device, -1)
+    block = jnp.concatenate([below, rows, above], axis=1).reshape(sources, 3, per_device, components, lon)
+    block = jnp.transpose(block, (2, 0, 3, 1, 4)).reshape(sources * per_device, -1)
     observed = jnp.take(block, obs_cell[0], axis=1)
     noise = obs_noise[0].reshape(-1, sources, per_device)
     noise = jnp.transpose(noise, (0, 2, 1)).reshape(-1, sources * per_device)

time: 51.4 us -> 50.3 us (0.979)
  local copies, waits for them, and re-layouts: 7.46 us -> 5.75 us
  waiting for transfers between devices: 7.1 us -> 7.89 us
    all_to_all x2 -> x0, local copies, waits for them, and re-layouts: 2 us -> none  [the longest x1 1.8 us: shards(): rows = lax.all_to_all(rows, 'band', 0, 0, tiled=True)]
    ppermute x1, waiting for transfers between devices: 0.55 us -> 1.34 us  [shards(): above = lax.ppermute(rows, 'band', down)]
    concatenate x0 -> x1, other arithmetic: none -> 0.56 us  [shards(): jnp.concatenate([below, rows, above], axis=1)]
    reshape x2 -> x3, local copies, waits for them, and re-layouts: 1.11 us -> 1.53 us  [the longest x2 1.11 us: shards(): jnp.transpose(block, (2, 0, 3, 1, 4)).reshape(sources * per_device, -1)]
  transfers between devices with their start and end apart: 3 -> 3, of which waited for: 2 -> 2; matrix products, arithmetic and copies ran while one was open for 8% -> 6% of each run, Pallas kernels for 0% -> 0%
where the time goes in v5:
time: 50.3 us; the launch traced here: 49.9 us
  blocking collectives  17 us (34%)
  starting transfers between devices  10.3 us (20%)
  waiting for transfers between devices  7.89 us (16%)
  Pallas kernels  6.4 us (13%)
  local copies, waits for them, and re-layouts  5.75 us (11%)
  other arithmetic  2.41 us (5%)
    all_to_all x1, blocking collectives, shards(): result = lax.all_to_all(result, 'band', 0, 0, tiled=True)  17 us
    all_to_all x1, starting transfers between devices, shards(): rows = lax.all_to_all(rows, 'band', 0, 0, tiled=True)  7.41 us
    all_to_all x1, waiting for transfers between devices, shards(): rows = lax.all_to_all(rows, 'band', 0, 0, tiled=True)  6.54 us
    pallas_call x1, Pallas kernels, analysis(): pl.pallas_call(analysis_kernel, out_shape=jax.ShapeDtypeStruct(rows.shape...  3.74 us
    pallas_call x1, Pallas kernels, forecast(): pl.pallas_call(forecast_kernel, out_shape=jax.ShapeDtypeStruct((lat_rows,...  2.66 us
    ppermute x1, starting transfers between devices, shards(): below = lax.ppermute(rows, 'band', up)  1.64 us
    ppermute x1, waiting for transfers between devices, shards(): above = lax.ppermute(rows, 'band', down)  1.34 us
    ppermute x1, starting transfers between devices, shards(): above = lax.ppermute(rows, 'band', down)  1.29 us
  transfers between devices with their start and end apart: 3, of which 2 were waited for; matrix products, arithmetic and copies ran while one was open for 6% of the time, Pallas kernels for 0%

profile of v5, /device:TPU:0, one launch (start us, length us, event | category | flops | bytes accessed | tf_op | source)
XLA Modules:
  0.0 49.9 jit_solution(18286434853467716762)
XLA Ops:
  0.0 2.7 %shard_map.64 = f32[16,1,3072]{2,1,0:T(1,128)} custom-call(s32[32]{0:T(128)} %fid_ref.1, f32[2,3,16,512]{3,2,1,0:T(8,128)} %x_ref.1), custom_call_target="tpu_custom_call" | custom-call | tf_op jit(solution)/shard_map/pallas_call | solution.py:279
  2.7 7.4 %all-to-all-start = ((f32[16,1,3072]{2,1,0:T(1,128)}), f32[16,1,3072]{2,1,0:T(1,128)S(1)}, u32[]{:S(2)}, u32[]{:S(2)}) async-start(f32[16,1,3072]{2,1,0:T(1,128)} %shard_map.64), calls=%async_computation | async-start | bytes 393216 | tf_op jit(solution)/shard_map/all_to_all | solution.py:294
  10.1 0.7 %reshape.52.fid_col_ref = s32[16,2]{1,0:T(8,128)S(1)} reshape(s32[32]{0:T(128)} %fid_ref.1) | data formatting | bytes 256 | tf_op jit(solution)/shard_map/reshape | solution.py:207
  10.8 0.1 copy.23
  10.9 0.8 %reshape_squeeze.3 = f32[256,16,2]{0,2,1:T(2,128)S(1)} reshape(f32[1,256,32]{1,2,0:T(8,128)} %param.11) | data formatting | bytes 65536 | tf_op jit(solution)/shard_map/reshape;squeeze | solution.py:302
  11.7 0.1 copy.25.noise_ref
  11.8 0.7 %compare_select_fusion = s32[256,1]{0,1:T(1,128)S(1)} fusion(s32[1,256]{1,0:T(1,128)} %param.8), kind=kLoop, calls=%fused_computation.3 | loop fusion | flops 768 | bytes 2048 | tf_op jit(solution)/shard_map/jit(_take)/jit(_where)/select_n | solution.py:301
  12.5 6.5 %all-to-all-done.x_ref = f32[16,1,3072]{2,1,0:T(1,128)S(1)} async-done(((f32[16,1,3072]{2,1,0:T(1,128)}), f32[16,1,3072]{2,1,0:T(1,128)S(1)}, u32[]{:S(2)}, u32[]{:S(2)}) %all-to-all-start) | async-done | bytes 196640 | tf_op jit(solution)/shard_map/all_to_all | solution.py:294
  19.0 1.6 %collective-permute-start = (f32[16,1,3072]{2,1,0:T(1,128)S(1)}, f32[16,1,3072]{2,1,0:T(1,128)S(1)}, u32[]{:S(2)}, u32[]{:S(2)}) collective-permute-start(f32[16,1,3072]{2,1,0:T(1,128)S(1)} %all-to-all-done.x_ref), channel_id=1, source_target_pairs={{0,1},{1,2},{2,3},{3,4},{4,5},{5,6},{6,7},{7,8},{8,9},{9,10},{10,1... | collective-permute-start | bytes 589832 | tf_op jit(solution)/shard_map/ppermute | solution.py:297
  20.7 1.3 %collective-permute-start.1 = (f32[16,1,3072]{2,1,0:T(1,128)S(1)}, f32[16,1,3072]{2,1,0:T(1,128)S(1)}, u32[]{:S(2)}, u32[]{:S(2)}) collective-permute-start(f32[16,1,3072]{2,1,0:T(1,128)S(1)} %all-to-all-done.x_ref), channel_id=1, source_target_pairs={{1,0},{2,1},{3,2},{4,3},{5,4},{6,5},{7,6},{8,7},{9,8},{10,9},{11,1... | collective-permute-start | bytes 589832 | tf_op jit(solution)/shard_map/ppermute | solution.py:298
  22.0 0.7 %compare_and_fusion = pred[256]{0:T(512)(128)(4,1)S(1)} fusion(s32[256]{0:T(256)} %bitcast.21), kind=kLoop, calls=%fused_computation.6 | loop fusion | flops 1536 | bytes 1280 | tf_op jit(solution)/shard_map/jit(_take)/and | solution.py:301
  22.7 0.0 collective-permute-done
  22.7 1.3 %collective-permute-done.1 = f32[16,1,3072]{2,1,0:T(1,128)S(1)} collective-permute-done((f32[16,1,3072]{2,1,0:T(1,128)S(1)}, f32[16,1,3072]{2,1,0:T(1,128)S(1)}, u32[]{:S(2)}, u32[]{:S(2)}) %collective-permute-start.1) | collective-permute-done | bytes 196640 | tf_op jit(solution)/shard_map/ppermute | solution.py:298
  24.0 0.6 %pad_maximum_fusion = f32[16,3,3072]{2,1,0:T(4,128)S(1)} fusion(f32[16,1,3072]{2,1,0:T(1,128)S(1)} %collective-permute-done.1, f32[16,1,3072]{2,1,0:T(1,128)S(1)} %all-to-all-done.x_ref, f32[16,1,3072]{2,1,0:T(1,128)S(1)} %collective-permute-done), kind=kLoop, calls=%fused_computation.1 | loop fusion | flops 294912 | bytes 1179648 | tf_op jit(solution)/shard_map/concatenate | solution.py:299
  24.6 0.3 copy.19
  24.9 0.4 reshape.50
  25.4 0.4 copy.20
  25.8 0.0 copy-start
  25.8 0.0 copy-start.1
  25.8 0.4 reshape.51
  26.3 0.7 %copy.21 = f32[32,4608]{0,1:T(8,128)S(1)} copy(f32[32,4608]{1,0:T(8,128)S(1)} %reshape.51) | data formatting | bytes 1179648 | tf_op jit(solution)/shard_map/reshape | solution.py:300
  26.9 0.7 %gather_fusion = f32[256,32]{1,0:T(8,128)S(1)} fusion(f32[32,4608]{0,1:T(8,128)S(1)} %copy.21, s32[1024]{0:T(1024)S(1)} %pad_clamp_fusion), kind=kCustom, calls=%fused_computation | custom fusion | bytes 66560 | tf_op jit(solution)/shard_map/jit(_take)/gather | solution.py:301
  27.7 0.1 copy.22
  27.8 0.0 copy-done
  27.8 0.0 copy-done.1
  27.8 3.7 %shard_map.65 = f32[16,1,3072]{2,1,0:T(1,128)S(1)} custom-call(f32[16,1,3072]{2,1,0:T(1,128)S(1)} %all-to-all-done.x_ref, f32[32,256]{1,0:T(8,128)S(1)} %select_bitcast_fusion.ob_ref, s32[16,2]{1,0:T(8,128)S(1)} %reshape.52.fid_col_ref, s32[2,16]{1,0:T(2,128)S(1)} %bitcast.15, f32[1,256]{1,0:T(1,128)S(1)} %copy-done, f32[1,256]{1,0:T(1,128)S(1)} %copy-done.1, ...), custom_call_target="tpu_custom_call" | custom-call | tf_op jit(solution)/shard_map/pallas_call | solution.py:198
  31.5 17.0 %all_to_all.10 = f32[16,1,3072]{2,1,0:T(1,128)S(1)} all-to-all(f32[16,1,3072]{2,1,0:T(1,128)S(1)} %shard_map.65), channel_id=1, replica_groups=mesh['groups'=2,'band'=16] {'band'}, dimensions={0} | all-to-all | bytes 393216 | tf_op jit(solution)/shard_map/all_to_all | solution.py:305
  48.5 0.5 reduce
  49.0 0.1 reshape.54
  49.1 0.8 %copy.26 = f32[2,3,16,512]{3,2,1,0:T(8,128)} copy(f32[2,3,16,512]{3,1,0,2:T(4,128)S(1)} %bitcast.17) | data formatting | bytes 393216 | tf_op jit(solution)/shard_map/transpose | solution.py:307
  (3 shorter events, 0.0 us)
Async XLA Ops:
  2.7 16.4 %all-to-all-start = ((f32[16,1,3072]{2,1,0:T(1,128)}), f32[16,1,3072]{2,1,0:T(1,128)S(1)}, u32[]{:S(2)}, u32[]{:S(2)}) async-start(f32[16,1,3072]{2,1,0:T(1,128)} %shard_map.64), calls=%async_computation | async-start | bytes 393216 | tf_op jit(solution)/shard_map/all_to_all | solution.py:294
  19.0 3.6 %collective-permute-start = (f32[16,1,3072]{2,1,0:T(1,128)S(1)}, f32[16,1,3072]{2,1,0:T(1,128)S(1)}, u32[]{:S(2)}, u32[]{:S(2)}) collective-permute-start(f32[16,1,3072]{2,1,0:T(1,128)S(1)} %all-to-all-done.x_ref), channel_id=1, source_target_pairs={{0,1},{1,2},{2,3},{3,4},{4,5},{5,6},{6,7},{7,8},{8,9},{9,10},{10,1... | collective-permute-start | bytes 589832 | tf_op jit(solution)/shard_map/ppermute | solution.py:297
  20.7 3.3 %collective-permute-start.1 = (f32[16,1,3072]{2,1,0:T(1,128)S(1)}, f32[16,1,3072]{2,1,0:T(1,128)S(1)}, u32[]{:S(2)}, u32[]{:S(2)}) collective-permute-start(f32[16,1,3072]{2,1,0:T(1,128)S(1)} %all-to-all-done.x_ref), channel_id=1, source_target_pairs={{1,0},{2,1},{3,2},{4,3},{5,4},{6,5},{7,6},{8,7},{9,8},{10,9},{11,1... | collective-permute-start | bytes 589832 | tf_op jit(solution)/shard_map/ppermute | solution.py:298
  25.8 2.0 %copy-start = (f32[1,256]{1,0:T(1,128)S(1)}, f32[1,256]{1,0:T(1,128)}, u32[]{:S(2)}) copy-start(f32[1,256]{1,0:T(1,128)} %value_ref.1) | copy-start | bytes 3076
  25.8 2.0 %copy-start.1 = (f32[1,256]{1,0:T(1,128)S(1)}, f32[1,256]{1,0:T(1,128)}, u32[]{:S(2)}) copy-start(f32[1,256]{1,0:T(1,128)} %var_ref.1) | copy-start | bytes 3076

commit v6 on v5

--- a/solution.py
+++ b/solution.py
@@ -296,9 +296,16 @@
     down = [(j, i) for i, j in up]
     below = lax.ppermute(rows, "band", up)
     above = lax.ppermute(rows, "band", down)
-    block = jnp.concatenate([below, rows, above], axis=1).reshape(sources, 3, per_device, components, lon)
-    block = jnp.transpose(block, (2, 0, 3, 1, 4)).reshape(sources * per_device, -1)
-    observed = jnp.take(block, obs_cell[0], axis=1)
+    block = jnp.concatenate([below, rows, above], axis=2).reshape(sources, -1)
+    cells = obs_cell[0]
+    component, place = cells // (3 * lon), cells % (3 * lon)
+    offset, column = place // lon, place % lon
+    width = per_device * components * lon
+    picks = jnp.concatenate(
+        [offset * width + (i * components + component) * lon + column for i in range(per_device)]
+    )
+    observed = jnp.take(block, picks, axis=1).reshape(sources, per_device, -1)
+    observed = jnp.transpose(observed, (1, 0, 2)).reshape(sources * per_device, -1)
     noise = obs_noise[0].reshape(-1, sources, per_device)
     noise = jnp.transpose(noise, (0, 2, 1)).reshape(-1, sources * per_device)
     result = analysis(rows, observed, member_fidelity, obs_value[0], obs_var[0], noise)

time: 50.3 us -> 53.6 us (1.066)
  local copies, waits for them, and re-layouts: 5.75 us -> 9.46 us
  starting transfers between devices: 10.3 us -> 11.7 us
  waiting for transfers between devices: 7.89 us -> 6.78 us
  blocking collectives: 17 us -> 16.2 us
    gather x2, local copies, waits for them, and re-layouts: 0.8 us -> 3.46 us  [shards(): observed = jnp.take(block, picks, axis=1).reshape(sources, per_device, -1)]
    reshape x3 -> x1, local copies, waits for them, and re-layouts: 1.53 us -> 3.33 us  [shards(): block = jnp.concatenate([below, rows, above], axis=2).reshape(sources, -1)]
    ppermute x1, starting transfers between devices: 1.64 us -> 3.04 us  [shards(): below = lax.ppermute(rows, 'band', up)]
    ppermute x1, waiting for transfers between devices: 1.34 us -> 0.01 us  [shards(): above = lax.ppermute(rows, 'band', down)]
    ppermute x1, waiting for transfers between devices: 0.01 us -> 1.02 us  [shards(): below = lax.ppermute(rows, 'band', up)]
    all_to_all x1, blocking collectives: 17 us -> 16.2 us  [shards(): result = lax.all_to_all(result, 'band', 0, 0, tiled=True)]
    all_to_all x1, waiting for transfers between devices: 6.54 us -> 5.76 us  [shards(): rows = lax.all_to_all(rows, 'band', 0, 0, tiled=True)]
    ne x0 -> x1, other arithmetic: none -> 0.7 us  [shards(): component, place = (cells // (3 * lon), cells % (3 * lon))]
where the time goes in v6:
time: 53.6 us; the launch traced here: 53.1 us
  blocking collectives  16.2 us (30%)
  starting transfers between devices  11.7 us (22%)
  local copies, waits for them, and re-layouts  9.46 us (18%)
  waiting for transfers between devices  6.78 us (13%)
  Pallas kernels  6.44 us (12%)
  other arithmetic  2.44 us (5%)
    all_to_all x1, blocking collectives, shards(): result = lax.all_to_all(result, 'band', 0, 0, tiled=True)  16.2 us
    all_to_all x1, starting transfers between devices, shards(): rows = lax.all_to_all(rows, 'band', 0, 0, tiled=True)  7.41 us
    all_to_all x1, waiting for transfers between devices, shards(): rows = lax.all_to_all(rows, 'band', 0, 0, tiled=True)  5.76 us
    pallas_call x1, Pallas kernels, analysis(): pl.pallas_call(analysis_kernel, out_shape=jax.ShapeDtypeStruct(rows.shape...  3.75 us
    gather x2, local copies, waits for them, and re-layouts, shards(): observed = jnp.take(block, picks, axis=1).reshape(sources, per_device, -1)  3.46 us
    reshape x1, local copies, waits for them, and re-layouts, shards(): block = jnp.concatenate([below, rows, above], axis=2).reshape(sources, -1)  3.33 us
    ppermute x1, starting transfers between devices, shards(): below = lax.ppermute(rows, 'band', up)  3.04 us
    pallas_call x1, Pallas kernels, forecast(): pl.pallas_call(forecast_kernel, out_shape=jax.ShapeDtypeStruct((lat_rows,...  2.69 us
  transfers between devices with their start and end apart: 3, of which 2 were waited for; matrix products, arithmetic and copies ran while one was open for 6% of the time, Pallas kernels for 0%

profile of v6, /device:TPU:0, one launch (start us, length us, event | category | flops | bytes accessed | tf_op | source)
XLA Modules:
  0.0 53.1 jit_solution(2700221852114569777)
XLA Ops:
  0.0 0.0 copy-start
  0.0 0.0 copy-start.1
  0.0 2.7 %shard_map.64 = f32[16,1,3072]{2,1,0:T(1,128)} custom-call(s32[32]{0:T(128)} %fid_ref.1, f32[2,3,16,512]{3,2,1,0:T(8,128)} %x_ref.1), custom_call_target="tpu_custom_call" | custom-call | tf_op jit(solution)/shard_map/pallas_call | solution.py:279
  2.7 7.4 %all-to-all-start = ((f32[16,1,3072]{2,1,0:T(1,128)}), f32[16,1,3072]{2,1,0:T(1,128)S(1)}, u32[]{:S(2)}, u32[]{:S(2)}) async-start(f32[16,1,3072]{2,1,0:T(1,128)} %shard_map.64), calls=%async_computation | async-start | bytes 393216 | tf_op jit(solution)/shard_map/all_to_all | solution.py:294
  10.1 0.7 %broadcast_remainder_fusion = (s32[1,256]{1,0:T(1,128)S(1)}, s32[1,256]{1,0:T(1,128)S(1)}) fusion(s32[1,256]{1,0:T(1,128)} %param.8), kind=kLoop, calls=%fused_computation.23 | loop fusion | flops 512 | bytes 3072 | tf_op jit(solution)/shard_map/jit(remainder)/rem | solution.py:301
  10.8 0.7 %compare_reduce_fusion = pred[256]{0:T(512)(128)(4,1)S(1)} fusion(s32[1,256]{1,0:T(1,128)} %param.8), kind=kLoop, calls=%fused_computation.7 | loop fusion | flops 512 | bytes 1280 | tf_op jit(solution)/shard_map/jit(floor_divide)/ne | solution.py:301
  11.5 0.7 %reshape.113.fid_col_ref = s32[16,2]{1,0:T(8,128)S(1)} reshape(s32[32]{0:T(128)} %fid_ref.1) | data formatting | bytes 256 | tf_op jit(solution)/shard_map/reshape | solution.py:207
  12.3 0.1 copy.19
  12.4 0.8 %reshape_squeeze.3 = f32[256,16,2]{0,2,1:T(2,128)S(1)} reshape(f32[1,256,32]{1,2,0:T(8,128)} %param.11) | data formatting | bytes 65536 | tf_op jit(solution)/shard_map/reshape;squeeze | solution.py:309
  13.2 0.1 copy.21.noise_ref
  13.3 5.8 %all-to-all-done.x_ref = f32[16,1,3072]{2,1,0:T(1,128)S(1)} async-done(((f32[16,1,3072]{2,1,0:T(1,128)}), f32[16,1,3072]{2,1,0:T(1,128)S(1)}, u32[]{:S(2)}, u32[]{:S(2)}) %all-to-all-start) | async-done | bytes 196640 | tf_op jit(solution)/shard_map/all_to_all | solution.py:294
  19.1 1.3 %collective-permute-start.1 = (f32[16,1,3072]{2,1,0:T(1,128)S(1)}, f32[16,1,3072]{2,1,0:T(1,128)S(1)}, u32[]{:S(2)}, u32[]{:S(2)}) collective-permute-start(f32[16,1,3072]{2,1,0:T(1,128)S(1)} %all-to-all-done.x_ref), channel_id=1, source_target_pairs={{1,0},{2,1},{3,2},{4,3},{5,4},{6,5},{7,6},{8,7},{9,8},{10,9},{11,1... | collective-permute-start | bytes 589832 | tf_op jit(solution)/shard_map/ppermute | solution.py:298
  20.4 3.0 %collective-permute-start = (f32[16,1,3072]{2,1,0:T(1,128)S(1)}, f32[16,1,3072]{2,1,0:T(1,128)S(1)}, u32[]{:S(2)}, u32[]{:S(2)}) collective-permute-start(f32[16,1,3072]{2,1,0:T(1,128)S(1)} %all-to-all-done.x_ref), channel_id=1, source_target_pairs={{0,1},{1,2},{2,3},{3,4},{4,5},{5,6},{6,7},{7,8},{8,9},{9,10},{10,1... | collective-permute-start | bytes 589832 | tf_op jit(solution)/shard_map/ppermute | solution.py:297
  23.4 0.0 collective-permute-done.1
  23.4 1.0 %collective-permute-done = f32[16,1,3072]{2,1,0:T(1,128)S(1)} collective-permute-done((f32[16,1,3072]{2,1,0:T(1,128)S(1)}, f32[16,1,3072]{2,1,0:T(1,128)S(1)}, u32[]{:S(2)}, u32[]{:S(2)}) %collective-permute-start) | collective-permute-done | bytes 196640 | tf_op jit(solution)/shard_map/ppermute | solution.py:297
  24.5 0.5 pad_maximum_fusion
  25.0 3.3 %copy.23 = f32[16,1,9216]{0,2,1:T(8,128)} copy(f32[16,1,9216]{2,1,0:T(1,128)S(1)} %pad_maximum_fusion) | data formatting | bytes 1179648 | tf_op jit(solution)/shard_map/reshape | solution.py:299
  28.3 3.4 %gather_fusion = f32[512,16]{1,0:T(8,128)S(1)} fusion(f32[16,9216]{0,1:T(8,128)} %bitcast.20, s32[1024]{0:T(1024)S(1)} %pad_clamp_fusion), kind=kCustom, calls=%fused_computation | custom fusion | bytes 67584 | tf_op jit(solution)/shard_map/jit(_take)/gather | solution.py:307
  31.7 0.1 copy.18
  31.8 0.0 copy-done
  31.8 0.0 copy-done.1
  31.8 3.7 %shard_map.65 = f32[16,1,3072]{2,1,0:T(1,128)S(1)} custom-call(f32[16,1,3072]{2,1,0:T(1,128)S(1)} %all-to-all-done.x_ref, f32[32,256]{1,0:T(8,128)S(1)} %bitcast.18, s32[16,2]{1,0:T(8,128)S(1)} %reshape.113.fid_col_ref, s32[2,16]{1,0:T(2,128)S(1)} %bitcast.19, f32[1,256]{1,0:T(1,128)S(1)} %copy-done, f32[1,256]{1,0:T(1,128)S(1)} %copy-done.1, ...), custom_call_target="tpu_custom_call" | custom-call | tf_op jit(solution)/shard_map/pallas_call | solution.py:198
  35.6 16.2 %all_to_all.10 = f32[16,1,3072]{2,1,0:T(1,128)S(1)} all-to-all(f32[16,1,3072]{2,1,0:T(1,128)S(1)} %shard_map.65), channel_id=1, replica_groups=mesh['groups'=2,'band'=16] {'band'}, dimensions={0} | all-to-all | bytes 393216 | tf_op jit(solution)/shard_map/all_to_all | solution.py:312
  51.7 0.5 reduce.1
  52.2 0.1 reshape.115
  52.3 0.8 %copy.22 = f32[2,3,16,512]{3,2,1,0:T(8,128)} copy(f32[2,3,16,512]{3,1,0,2:T(4,128)S(1)} %bitcast.21) | data formatting | bytes 393216 | tf_op jit(solution)/shard_map/transpose | solution.py:314
  (9 shorter events, 0.1 us)
Async XLA Ops:
  0.0 31.8 %copy-start = (f32[1,256]{1,0:T(1,128)S(1)}, f32[1,256]{1,0:T(1,128)}, u32[]{:S(2)}) copy-start(f32[1,256]{1,0:T(1,128)} %value_ref.1) | copy-start | bytes 3076
  0.0 31.8 %copy-start.1 = (f32[1,256]{1,0:T(1,128)S(1)}, f32[1,256]{1,0:T(1,128)}, u32[]{:S(2)}) copy-start(f32[1,256]{1,0:T(1,128)} %var_ref.1) | copy-start | bytes 3076
  2.7 16.4 %all-to-all-start = ((f32[16,1,3072]{2,1,0:T(1,128)}), f32[16,1,3072]{2,1,0:T(1,128)S(1)}, u32[]{:S(2)}, u32[]{:S(2)}) async-start(f32[16,1,3072]{2,1,0:T(1,128)} %shard_map.64), calls=%async_computation | async-start | bytes 393216 | tf_op jit(solution)/shard_map/all_to_all | solution.py:294
  19.1 4.4 %collective-permute-start.1 = (f32[16,1,3072]{2,1,0:T(1,128)S(1)}, f32[16,1,3072]{2,1,0:T(1,128)S(1)}, u32[]{:S(2)}, u32[]{:S(2)}) collective-permute-start(f32[16,1,3072]{2,1,0:T(1,128)S(1)} %all-to-all-done.x_ref), channel_id=1, source_target_pairs={{1,0},{2,1},{3,2},{4,3},{5,4},{6,5},{7,6},{8,7},{9,8},{10,9},{11,1... | collective-permute-start | bytes 589832 | tf_op jit(solution)/shard_map/ppermute | solution.py:298
  20.4 4.1 %collective-permute-start = (f32[16,1,3072]{2,1,0:T(1,128)S(1)}, f32[16,1,3072]{2,1,0:T(1,128)S(1)}, u32[]{:S(2)}, u32[]{:S(2)}) collective-permute-start(f32[16,1,3072]{2,1,0:T(1,128)S(1)} %all-to-all-done.x_ref), channel_id=1, source_target_pairs={{0,1},{1,2},{2,3},{3,4},{4,5},{5,6},{6,7},{7,8},{8,9},{9,10},{10,1... | collective-permute-start | bytes 589832 | tf_op jit(solution)/shard_map/ppermute | solution.py:297

commit v7 on v5

--- a/solution.py
+++ b/solution.py
@@ -287,6 +287,22 @@
     )(levels, initial)
 
 
+def unpack_kernel(x_ref, o_ref):
+    members, components, _, lon = o_ref.shape
+    for member in range(members):
+        for component in range(components):
+            o_ref[member, component] = x_ref[:, 0, pl.ds((member * components + component) * lon, lon)]
+
+
+def unpack(rows, shape):
+    return pl.pallas_call(
+        unpack_kernel,
+        out_shape=jax.ShapeDtypeStruct(shape, jnp.float32),
+        in_specs=[pl.BlockSpec(memory_space=pltpu.VMEM)],
+        out_specs=pl.BlockSpec(memory_space=pltpu.VMEM),
+    )(rows)
+
+
 def shards(initial_height_velocity, member_fidelity, obs_cell, obs_value, obs_var, obs_noise):
     per_device, components, lat_rows, lon = initial_height_velocity.shape
     sources = lax.axis_size("band")
@@ -303,8 +319,7 @@
     noise = jnp.transpose(noise, (0, 2, 1)).reshape(-1, sources * per_device)
     result = analysis(rows, observed, member_fidelity, obs_value[0], obs_var[0], noise)
     result = lax.all_to_all(result, "band", 0, 0, tiled=True)
-    result = result.reshape(lat_rows, per_device, components, lon)
-    return jnp.transpose(result, (1, 2, 0, 3))
+    return unpack(result, initial_height_velocity.shape)
 
 
 def solution(mesh):

time: 50.3 us -> 50.7 us (level)
  Pallas kernels: 6.4 us -> 8.04 us
  local copies, waits for them, and re-layouts: 5.75 us -> 4.81 us
    pallas_call x0 -> x1, Pallas kernels: none -> 1.64 us  [unpack(): pl.pallas_call(unpack_kernel, out_shape=jax.ShapeDtypeStruct(shape, jnp.f...]
    transpose x1 -> x0, local copies, waits for them, and re-layouts: 0.8 us -> none  [shards(): return jnp.transpose(result, (1, 2, 0, 3))]
where the time goes in v7:
time: 50.7 us; the launch traced here: 50.3 us
  blocking collectives  17.1 us (34%)
  starting transfers between devices  10.3 us (20%)
  Pallas kernels  8.04 us (16%)
  waiting for transfers between devices  7.89 us (16%)
  local copies, waits for them, and re-layouts  4.81 us (9%)
  other arithmetic  1.95 us (4%)
    all_to_all x1, blocking collectives, shards(): result = lax.all_to_all(result, 'band', 0, 0, tiled=True)  17.1 us
    all_to_all x1, starting transfers between devices, shards(): rows = lax.all_to_all(rows, 'band', 0, 0, tiled=True)  7.41 us
    all_to_all x1, waiting for transfers between devices, shards(): rows = lax.all_to_all(rows, 'band', 0, 0, tiled=True)  6.54 us
    pallas_call x1, Pallas kernels, analysis(): pl.pallas_call(analysis_kernel, out_shape=jax.ShapeDtypeStruct(rows.shape...  3.74 us
    pallas_call x1, Pallas kernels, forecast(): pl.pallas_call(forecast_kernel, out_shape=jax.ShapeDtypeStruct((lat_rows,...  2.66 us
    ppermute x1, starting transfers between devices, shards(): below = lax.ppermute(rows, 'band', up)  1.64 us
    pallas_call x1, Pallas kernels, unpack(): pl.pallas_call(unpack_kernel, out_shape=jax.ShapeDtypeStruct(shape, jnp.f...  1.64 us
    ppermute x1, waiting for transfers between devices, shards(): above = lax.ppermute(rows, 'band', down)  1.34 us
  transfers between devices with their start and end apart: 3, of which 2 were waited for; matrix products, arithmetic and copies ran while one was open for 6% of the time, Pallas kernels for 0%

profile of v7, /device:TPU:0, one launch (start us, length us, event | category | flops | bytes accessed | tf_op | source)
XLA Modules:
  0.0 50.3 jit_solution(409840061396212689)
XLA Ops:
  0.0 2.7 %shard_map.64 = f32[16,1,3072]{2,1,0:T(1,128)} custom-call(s32[32]{0:T(128)} %fid_ref.1, f32[2,3,16,512]{3,2,1,0:T(8,128)} %x_ref.1), custom_call_target="tpu_custom_call" | custom-call | tf_op jit(solution)/shard_map/pallas_call | solution.py:279
  2.7 7.4 %all-to-all-start = ((f32[16,1,3072]{2,1,0:T(1,128)}), f32[16,1,3072]{2,1,0:T(1,128)S(1)}, u32[]{:S(2)}, u32[]{:S(2)}) async-start(f32[16,1,3072]{2,1,0:T(1,128)} %shard_map.64), calls=%async_computation | async-start | bytes 393216 | tf_op jit(solution)/shard_map/all_to_all | solution.py:310
  10.1 0.7 %reshape.49.fid_col_ref = s32[16,2]{1,0:T(8,128)S(1)} reshape(s32[32]{0:T(128)} %fid_ref.1) | data formatting | bytes 256 | tf_op jit(solution)/shard_map/reshape | solution.py:207
  10.8 0.1 copy.21
  10.9 0.8 %reshape_squeeze.3 = f32[256,16,2]{0,2,1:T(2,128)S(1)} reshape(f32[1,256,32]{1,2,0:T(8,128)} %param.11) | data formatting | bytes 65536 | tf_op jit(solution)/shard_map/reshape;squeeze | solution.py:318
  11.7 0.1 copy.23.noise_ref
  11.8 0.7 %compare_select_fusion = s32[256,1]{0,1:T(1,128)S(1)} fusion(s32[1,256]{1,0:T(1,128)} %param.8), kind=kLoop, calls=%fused_computation.3 | loop fusion | flops 768 | bytes 2048 | tf_op jit(solution)/shard_map/jit(_take)/jit(_where)/select_n | solution.py:317
  12.5 6.5 %all-to-all-done.x_ref = f32[16,1,3072]{2,1,0:T(1,128)S(1)} async-done(((f32[16,1,3072]{2,1,0:T(1,128)}), f32[16,1,3072]{2,1,0:T(1,128)S(1)}, u32[]{:S(2)}, u32[]{:S(2)}) %all-to-all-start) | async-done | bytes 196640 | tf_op jit(solution)/shard_map/all_to_all | solution.py:310
  19.0 1.6 %collective-permute-start = (f32[16,1,3072]{2,1,0:T(1,128)S(1)}, f32[16,1,3072]{2,1,0:T(1,128)S(1)}, u32[]{:S(2)}, u32[]{:S(2)}) collective-permute-start(f32[16,1,3072]{2,1,0:T(1,128)S(1)} %all-to-all-done.x_ref), channel_id=1, source_target_pairs={{0,1},{1,2},{2,3},{3,4},{4,5},{5,6},{6,7},{7,8},{8,9},{9,10},{10,1... | collective-permute-start | bytes 589832 | tf_op jit(solution)/shard_map/ppermute | solution.py:313
  20.7 1.3 %collective-permute-start.1 = (f32[16,1,3072]{2,1,0:T(1,128)S(1)}, f32[16,1,3072]{2,1,0:T(1,128)S(1)}, u32[]{:S(2)}, u32[]{:S(2)}) collective-permute-start(f32[16,1,3072]{2,1,0:T(1,128)S(1)} %all-to-all-done.x_ref), channel_id=1, source_target_pairs={{1,0},{2,1},{3,2},{4,3},{5,4},{6,5},{7,6},{8,7},{9,8},{10,9},{11,1... | collective-permute-start | bytes 589832 | tf_op jit(solution)/shard_map/ppermute | solution.py:314
  22.0 0.7 %compare_and_fusion = pred[256]{0:T(512)(128)(4,1)S(1)} fusion(s32[256]{0:T(256)} %bitcast.19), kind=kLoop, calls=%fused_computation.6 | loop fusion | flops 1536 | bytes 1280 | tf_op jit(solution)/shard_map/jit(_take)/and | solution.py:317
  22.7 0.0 collective-permute-done
  22.7 1.3 %collective-permute-done.1 = f32[16,1,3072]{2,1,0:T(1,128)S(1)} collective-permute-done((f32[16,1,3072]{2,1,0:T(1,128)S(1)}, f32[16,1,3072]{2,1,0:T(1,128)S(1)}, u32[]{:S(2)}, u32[]{:S(2)}) %collective-permute-start.1) | collective-permute-done | bytes 196640 | tf_op jit(solution)/shard_map/ppermute | solution.py:314
  24.0 0.6 %pad_maximum_fusion = f32[16,3,3072]{2,1,0:T(4,128)S(1)} fusion(f32[16,1,3072]{2,1,0:T(1,128)S(1)} %collective-permute-done.1, f32[16,1,3072]{2,1,0:T(1,128)S(1)} %all-to-all-done.x_ref, f32[16,1,3072]{2,1,0:T(1,128)S(1)} %collective-permute-done), kind=kLoop, calls=%fused_computation.1 | loop fusion | flops 294912 | bytes 1179648 | tf_op jit(solution)/shard_map/concatenate | solution.py:315
  24.6 0.3 copy.17
  24.9 0.4 reshape.47
  25.4 0.4 copy.18
  25.8 0.0 copy-start
  25.8 0.0 copy-start.1
  25.8 0.4 reshape.48
  26.3 0.7 %copy.19 = f32[32,4608]{0,1:T(8,128)S(1)} copy(f32[32,4608]{1,0:T(8,128)S(1)} %reshape.48) | data formatting | bytes 1179648 | tf_op jit(solution)/shard_map/reshape | solution.py:316
  26.9 0.7 %gather_fusion = f32[256,32]{1,0:T(8,128)S(1)} fusion(f32[32,4608]{0,1:T(8,128)S(1)} %copy.19, s32[1024]{0:T(1024)S(1)} %pad_clamp_fusion), kind=kCustom, calls=%fused_computation | custom fusion | bytes 66560 | tf_op jit(solution)/shard_map/jit(_take)/gather | solution.py:317
  27.7 0.1 copy.20
  27.8 0.0 copy-done
  27.8 0.0 copy-done.1
  27.8 3.7 %shard_map.65 = f32[16,1,3072]{2,1,0:T(1,128)S(1)} custom-call(f32[16,1,3072]{2,1,0:T(1,128)S(1)} %all-to-all-done.x_ref, f32[32,256]{1,0:T(8,128)S(1)} %select_bitcast_fusion.ob_ref, s32[16,2]{1,0:T(8,128)S(1)} %reshape.49.fid_col_ref, s32[2,16]{1,0:T(2,128)S(1)} %bitcast.14, f32[1,256]{1,0:T(1,128)S(1)} %copy-done, f32[1,256]{1,0:T(1,128)S(1)} %copy-done.1, ...), custom_call_target="tpu_custom_call" | custom-call | tf_op jit(solution)/shard_map/pallas_call | solution.py:198
  31.5 17.1 %all_to_all.10.x_ref = f32[16,1,3072]{2,1,0:T(1,128)} all-to-all(f32[16,1,3072]{2,1,0:T(1,128)S(1)} %shard_map.65), channel_id=1, replica_groups=mesh['groups'=2,'band'=16] {'band'}, dimensions={0} | all-to-all | bytes 393216 | tf_op jit(solution)/shard_map/all_to_all | solution.py:321
  48.6 1.6 %shard_map.66 = f32[2,3,16,512]{3,2,1,0:T(8,128)} custom-call(f32[16,1,3072]{2,1,0:T(1,128)} %all_to_all.10.x_ref), custom_call_target="tpu_custom_call" | custom-call | tf_op jit(solution)/shard_map/pallas_call | solution.py:298
  (3 shorter events, 0.0 us)
Async XLA Ops:
  2.7 16.4 %all-to-all-start = ((f32[16,1,3072]{2,1,0:T(1,128)}), f32[16,1,3072]{2,1,0:T(1,128)S(1)}, u32[]{:S(2)}, u32[]{:S(2)}) async-start(f32[16,1,3072]{2,1,0:T(1,128)} %shard_map.64), calls=%async_computation | async-start | bytes 393216 | tf_op jit(solution)/shard_map/all_to_all | solution.py:310
  19.0 3.6 %collective-permute-start = (f32[16,1,3072]{2,1,0:T(1,128)S(1)}, f32[16,1,3072]{2,1,0:T(1,128)S(1)}, u32[]{:S(2)}, u32[]{:S(2)}) collective-permute-start(f32[16,1,3072]{2,1,0:T(1,128)S(1)} %all-to-all-done.x_ref), channel_id=1, source_target_pairs={{0,1},{1,2},{2,3},{3,4},{4,5},{5,6},{6,7},{7,8},{8,9},{9,10},{10,1... | collective-permute-start | bytes 589832 | tf_op jit(solution)/shard_map/ppermute | solution.py:313
  20.7 3.3 %collective-permute-start.1 = (f32[16,1,3072]{2,1,0:T(1,128)S(1)}, f32[16,1,3072]{2,1,0:T(1,128)S(1)}, u32[]{:S(2)}, u32[]{:S(2)}) collective-permute-start(f32[16,1,3072]{2,1,0:T(1,128)S(1)} %all-to-all-done.x_ref), channel_id=1, source_target_pairs={{1,0},{2,1},{3,2},{4,3},{5,4},{6,5},{7,6},{8,7},{9,8},{10,9},{11,1... | collective-permute-start | bytes 589832 | tf_op jit(solution)/shard_map/ppermute | solution.py:314
  25.8 2.0 %copy-start = (f32[1,256]{1,0:T(1,128)S(1)}, f32[1,256]{1,0:T(1,128)}, u32[]{:S(2)}) copy-start(f32[1,256]{1,0:T(1,128)} %value_ref.1) | copy-start | bytes 3076
  25.8 2.0 %copy-start.1 = (f32[1,256]{1,0:T(1,128)S(1)}, f32[1,256]{1,0:T(1,128)}, u32[]{:S(2)}) copy-start(f32[1,256]{1,0:T(1,128)} %var_ref.1) | copy-start | bytes 3076

commit v8 on v5

--- a/solution.py
+++ b/solution.py
@@ -143,12 +143,30 @@
     )
 
 
-def analysis_kernel(x_ref, ob_ref, fid_col_ref, fid_row_ref, value_ref, var_ref, noise_ref, o_ref):
+def analysis_kernel(
+    cell_ref, below_ref, x_ref, above_ref, fid_col_ref, fid_row_ref, value_ref, var_ref, noise_ref,
+    o_ref, cells_ref, picked_ref,
+):
     per_device = fid_col_ref.shape[1]
     width = x_ref.shape[2] // per_device
-    x = jnp.concatenate([x_ref[:, 0, i * width : (i + 1) * width] for i in range(per_device)], axis=0)
+    def members_of(ref):
+        return jnp.concatenate([ref[:, 0, i * width : (i + 1) * width] for i in range(per_device)], axis=0)
+    x = members_of(x_ref)
     m = x.shape[0]
-    ob = ob_ref[...]
+    components = 3
+    lon = width // components
+    for offset, ref in enumerate((below_ref, x_ref, above_ref)):
+        block = x if offset == 1 else members_of(ref)
+        block = block.T
+        for component in range(components):
+            cells_ref[pl.ds((component * 3 + offset) * lon, lon), :] = block[component * lon : (component + 1) * lon]
+
+    def pick(o, carry):
+        picked_ref[pl.ds(o, 1), :] = cells_ref[pl.ds(cell_ref[o], 1), :]
+        return carry
+
+    lax.fori_loop(0, picked_ref.shape[0], pick, 0, unroll=8)
+    ob = picked_ref[...].T
     fid_col = jnp.concatenate([fid_col_ref[:, i : i + 1] for i in range(per_device)], axis=0)
     fid_row = jnp.concatenate([fid_row_ref[i : i + 1, :] for i in range(per_device)], axis=1)
     variance = var_ref[...]
@@ -192,18 +210,25 @@
         o_ref[:, 0, i * width : (i + 1) * width] = result[i * sources : (i + 1) * sources]
 
 
-def analysis(rows, observed, fidelity, value, variance, noise):
+def analysis(cells, below, rows, above, fidelity, value, variance, noise):
     sources = rows.shape[0]
+    members = fidelity.shape[0]
     vmem = pl.BlockSpec(memory_space=pltpu.VMEM)
     return pl.pallas_call(
         analysis_kernel,
         out_shape=jax.ShapeDtypeStruct(rows.shape, jnp.float32),
-        in_specs=[vmem] * 7,
+        in_specs=[pl.BlockSpec(memory_space=pltpu.SMEM)] + [vmem] * 8,
         out_specs=vmem,
+        scratch_shapes=[
+            pltpu.VMEM((3 * rows.shape[2] // (members // sources), members), jnp.float32),
+            pltpu.VMEM((cells.shape[0], members), jnp.float32),
+        ],
         compiler_params=pltpu.CompilerParams(vmem_limit_bytes=48 * 1024 * 1024),
     )(
+        cells,
+        below,
         rows,
-        observed,
+        above,
         fidelity.reshape(sources, -1),
         fidelity.reshape(sources, -1).T,
         value.reshape(1, -1),
@@ -296,12 +321,9 @@
     down = [(j, i) for i, j in up]
     below = lax.ppermute(rows, "band", up)
     above = lax.ppermute(rows, "band", down)
-    block = jnp.concatenate([below, rows, above], axis=1).reshape(sources, 3, per_device, components, lon)
-    block = jnp.transpose(block, (2, 0, 3, 1, 4)).reshape(sources * per_device, -1)
-    observed = jnp.take(block, obs_cell[0], axis=1)
     noise = obs_noise[0].reshape(-1, sources, per_device)
     noise = jnp.transpose(noise, (0, 2, 1)).reshape(-1, sources * per_device)
-    result = analysis(rows, observed, member_fidelity, obs_value[0], obs_var[0], noise)
+    result = analysis(obs_cell[0], below, rows, above, member_fidelity, obs_value[0], obs_var[0], noise)
     result = lax.all_to_all(result, "band", 0, 0, tiled=True)
     result = result.reshape(lat_rows, per_device, components, lon)
     return jnp.transpose(result, (1, 2, 0, 3))

time: 50.3 us -> 48.5 us (0.964)
  blocking collectives: 17 us -> 32.7 us
  waiting for transfers between devices: 7.89 us -> 0.69 us
  starting transfers between devices: 10.3 us -> 4.32 us
  local copies, waits for them, and re-layouts: 5.75 us -> 1.93 us
  other arithmetic: 2.41 us -> 0.46 us
  Pallas kernels: 6.4 us -> 8.01 us
    all_to_all x0 -> x1, blocking collectives: none -> 16.5 us  [shards(): rows = lax.all_to_all(rows, 'band', 0, 0, tiled=True)]
    all_to_all x1 -> x0, starting transfers between devices: 7.41 us -> none  [shards(): rows = lax.all_to_all(rows, 'band', 0, 0, tiled=True)]
    all_to_all x1 -> x0, waiting for transfers between devices: 6.54 us -> none  [shards(): rows = lax.all_to_all(rows, 'band', 0, 0, tiled=True)]
    pallas_call x1, Pallas kernels: 3.74 us -> 5.35 us  [analysis(): pl.pallas_call(analysis_kernel, out_shape=jax.ShapeDtypeStruct(rows.shape...]
    reshape x3 -> x0, local copies, waits for them, and re-layouts: 1.53 us -> none  [the longest x2 1.11 us: shards(): jnp.transpose(block, (2, 0, 3, 1, 4)).reshape(sources * per_device, -1)]
    ppermute x1, starting transfers between devices: 1.64 us -> 3.04 us  [shards(): below = lax.ppermute(rows, 'band', up)]
    ppermute x1, waiting for transfers between devices: 1.34 us -> 0.01 us  [shards(): above = lax.ppermute(rows, 'band', down)]
    all_to_all x1, blocking collectives: 17 us -> 16.1 us  [shards(): result = lax.all_to_all(result, 'band', 0, 0, tiled=True)]
  transfers between devices with their start and end apart: 3 -> 2, of which waited for: 2 -> 1; matrix products, arithmetic and copies ran while one was open for 6% -> 1% of each run, Pallas kernels for 0% -> 0%
where the time goes in v8:
time: 48.5 us; the launch traced here: 48.1 us
  blocking collectives  32.7 us (67%)
  Pallas kernels  8.01 us (17%)
  starting transfers between devices  4.32 us (9%)
  local copies, waits for them, and re-layouts  1.93 us (4%)
  waiting for transfers between devices  0.69 us (1%)
    all_to_all x1, blocking collectives, shards(): rows = lax.all_to_all(rows, 'band', 0, 0, tiled=True)  16.5 us
    all_to_all x1, blocking collectives, shards(): result = lax.all_to_all(result, 'band', 0, 0, tiled=True)  16.1 us
    pallas_call x1, Pallas kernels, analysis(): pl.pallas_call(analysis_kernel, out_shape=jax.ShapeDtypeStruct(rows.shape...  5.35 us
    ppermute x1, starting transfers between devices, shards(): below = lax.ppermute(rows, 'band', up)  3.04 us
    pallas_call x1, Pallas kernels, forecast(): pl.pallas_call(forecast_kernel, out_shape=jax.ShapeDtypeStruct((lat_rows,...  2.66 us
    ppermute x1, starting transfers between devices, shards(): above = lax.ppermute(rows, 'band', down)  1.28 us
  transfers between devices with their start and end apart: 2, of which 1 were waited for; matrix products, arithmetic and copies ran while one was open for 1% of the time, Pallas kernels for 0%

profile of v8, /device:TPU:0, one launch (start us, length us, event | category | flops | bytes accessed | tf_op | source)
XLA Modules:
  0.0 48.1 jit_solution(16693333078687905764)
XLA Ops:
  0.0 2.7 %shard_map.64 = f32[16,1,3072]{2,1,0:T(1,128)} custom-call(s32[32]{0:T(128)} %fid_ref.1, f32[2,3,16,512]{3,2,1,0:T(8,128)} %x_ref.1), custom_call_target="tpu_custom_call" | custom-call | tf_op jit(solution)/shard_map/pallas_call | solution.py:304
  2.7 0.0 copy-start.4
  2.7 0.0 copy-start.3
  2.7 16.5 %all_to_all.10.x_ref = f32[16,1,3072]{2,1,0:T(1,128)S(1)} all-to-all(f32[16,1,3072]{2,1,0:T(1,128)} %shard_map.64), channel_id=1, replica_groups=mesh['groups'=2,'band'=16] {'band'}, dimensions={0} | all-to-all | bytes 393216 | tf_op jit(solution)/shard_map/all_to_all | solution.py:319
  19.2 1.3 %collective-permute-start.1 = (f32[16,1,3072]{2,1,0:T(1,128)S(1)}, f32[16,1,3072]{2,1,0:T(1,128)S(1)}, u32[]{:S(2)}, u32[]{:S(2)}) collective-permute-start(f32[16,1,3072]{2,1,0:T(1,128)S(1)} %all_to_all.10.x_ref), channel_id=1, source_target_pairs={{1,0},{2,1},{3,2},{4,3},{5,4},{6,5},{7,6},{8,7},{9,8},{10,9},{11,1... | collective-permute-start | bytes 589832 | tf_op jit(solution)/shard_map/ppermute | solution.py:323
  20.5 3.0 %collective-permute-start = (f32[16,1,3072]{2,1,0:T(1,128)S(1)}, f32[16,1,3072]{2,1,0:T(1,128)S(1)}, u32[]{:S(2)}, u32[]{:S(2)}) collective-permute-start(f32[16,1,3072]{2,1,0:T(1,128)S(1)} %all_to_all.10.x_ref), channel_id=1, source_target_pairs={{0,1},{1,2},{2,3},{3,4},{4,5},{5,6},{6,7},{7,8},{8,9},{9,10},{10,1... | collective-permute-start | bytes 589832 | tf_op jit(solution)/shard_map/ppermute | solution.py:322
  23.5 0.0 copy-done.4
  23.5 0.1 reshape.10.fid_col_ref
  23.6 0.1 copy.13
  23.7 0.0 copy-done.3
  23.7 0.0 copy-start.1
  23.7 0.0 copy-start.2
  23.8 0.1 copy.15.noise_ref
  23.9 0.0 collective-permute-done.1.above_ref
  23.9 0.7 %collective-permute-done.below_ref = f32[16,1,3072]{2,1,0:T(1,128)S(1)} collective-permute-done((f32[16,1,3072]{2,1,0:T(1,128)S(1)}, f32[16,1,3072]{2,1,0:T(1,128)S(1)}, u32[]{:S(2)}, u32[]{:S(2)}) %collective-permute-start) | collective-permute-done | bytes 196640 | tf_op jit(solution)/shard_map/ppermute | solution.py:322
  24.6 0.0 copy-start
  24.6 0.0 copy-done.1
  24.6 0.0 copy-done.2
  24.6 0.7 %copy-done = s32[1,256]{1,0:T(1,128)S(1)} copy-done((s32[1,256]{1,0:T(1,128)S(1)}, s32[1,256]{1,0:T(1,128)}, u32[]{:S(2)}) %copy-start) | copy-done | bytes 1048
  25.2 5.3 %shard_map.65 = f32[16,1,3072]{2,1,0:T(1,128)S(1)} custom-call(s32[256]{0:T(256)S(1)} %bitcast.8, f32[16,1,3072]{2,1,0:T(1,128)S(1)} %collective-permute-done.below_ref, f32[16,1,3072]{2,1,0:T(1,128)S(1)} %all_to_all.10.x_ref, f32[16,1,3072]{2,1,0:T(1,128)S(1)} %collective-permute-done.1.above_ref, s32[16,2]{1,0:T(8,128)S(1)} %reshape.10.fid_col_ref, ...), custom_call_target="tpu_custom_call" | custom-call | tf_op jit(solution)/shard_map/pallas_call | solution.py:217
  30.6 16.1 %all_to_all.11 = f32[16,1,3072]{2,1,0:T(1,128)S(1)} all-to-all(f32[16,1,3072]{2,1,0:T(1,128)S(1)} %shard_map.65), channel_id=1, replica_groups=mesh['groups'=2,'band'=16] {'band'}, dimensions={0} | all-to-all | bytes 393216 | tf_op jit(solution)/shard_map/all_to_all | solution.py:327
  46.7 0.5 reduce
  47.2 0.1 reshape.12
  47.4 0.8 %copy.16 = f32[2,3,16,512]{3,2,1,0:T(8,128)} copy(f32[2,3,16,512]{3,1,0,2:T(4,128)S(1)} %bitcast.9) | data formatting | bytes 393216 | tf_op jit(solution)/shard_map/transpose | solution.py:329
  (2 shorter events, 0.0 us)
Async XLA Ops:
  2.7 20.8 %copy-start.4 = (s32[32]{0:T(128)S(1)}, s32[32]{0:T(128)}, u32[]{:S(2)}) copy-start(s32[32]{0:T(128)} %fid_ref.1) | copy-start | bytes 388
  2.7 21.0 %copy-start.3 = (f32[1,256,32]{1,2,0:T(8,128)S(1)}, f32[1,256,32]{1,2,0:T(8,128)}, u32[]{:S(2)}) copy-start(f32[1,256,32]{1,2,0:T(8,128)} %param.11) | copy-start | bytes 98308
  19.2 4.7 %collective-permute-start.1 = (f32[16,1,3072]{2,1,0:T(1,128)S(1)}, f32[16,1,3072]{2,1,0:T(1,128)S(1)}, u32[]{:S(2)}, u32[]{:S(2)}) collective-permute-start(f32[16,1,3072]{2,1,0:T(1,128)S(1)} %all_to_all.10.x_ref), channel_id=1, source_target_pairs={{1,0},{2,1},{3,2},{4,3},{5,4},{6,5},{7,6},{8,7},{9,8},{10,9},{11,1... | collective-permute-start | bytes 589832 | tf_op jit(solution)/shard_map/ppermute | solution.py:323
  20.5 4.1 %collective-permute-start = (f32[16,1,3072]{2,1,0:T(1,128)S(1)}, f32[16,1,3072]{2,1,0:T(1,128)S(1)}, u32[]{:S(2)}, u32[]{:S(2)}) collective-permute-start(f32[16,1,3072]{2,1,0:T(1,128)S(1)} %all_to_all.10.x_ref), channel_id=1, source_target_pairs={{0,1},{1,2},{2,3},{3,4},{4,5},{5,6},{6,7},{7,8},{8,9},{9,10},{10,1... | collective-permute-start | bytes 589832 | tf_op jit(solution)/shard_map/ppermute | solution.py:322
  23.7 0.8 %copy-start.1 = (f32[1,256]{1,0:T(1,128)S(1)}, f32[1,256]{1,0:T(1,128)}, u32[]{:S(2)}) copy-start(f32[1,256]{1,0:T(1,128)} %value_ref.1) | copy-start | bytes 3076
  23.7 0.8 %copy-start.2 = (f32[1,256]{1,0:T(1,128)S(1)}, f32[1,256]{1,0:T(1,128)}, u32[]{:S(2)}) copy-start(f32[1,256]{1,0:T(1,128)} %var_ref.1) | copy-start | bytes 3076
  24.6 0.7 %copy-start = (s32[1,256]{1,0:T(1,128)S(1)}, s32[1,256]{1,0:T(1,128)}, u32[]{:S(2)}) copy-start(s32[1,256]{1,0:T(1,128)} %param.8) | copy-start | bytes 3076

commit v9 on v8

--- a/solution.py
+++ b/solution.py
@@ -165,7 +165,7 @@
         picked_ref[pl.ds(o, 1), :] = cells_ref[pl.ds(cell_ref[o], 1), :]
         return carry
 
-    lax.fori_loop(0, picked_ref.shape[0], pick, 0, unroll=8)
+    lax.fori_loop(0, picked_ref.shape[0], pick, 0, unroll=picked_ref.shape[0] <= 512 or 8)
     ob = picked_ref[...].T
     fid_col = jnp.concatenate([fid_col_ref[:, i : i + 1] for i in range(per_device)], axis=0)
     fid_row = jnp.concatenate([fid_row_ref[i : i + 1, :] for i in range(per_device)], axis=1)

time: 48.5 us -> 48.2 us (level)
  no operation moved by 1% of the time
where the time goes in v9:
time: 48.2 us; the launch traced here: 47.9 us
  blocking collectives  32.7 us (68%)
  Pallas kernels  7.74 us (16%)
  starting transfers between devices  4.32 us (9%)
  local copies, waits for them, and re-layouts  1.93 us (4%)
  waiting for transfers between devices  0.69 us (1%)
    all_to_all x1, blocking collectives, shards(): rows = lax.all_to_all(rows, 'band', 0, 0, tiled=True)  16.5 us
    all_to_all x1, blocking collectives, shards(): result = lax.all_to_all(result, 'band', 0, 0, tiled=True)  16.2 us
    pallas_call x1, Pallas kernels, analysis(): pl.pallas_call(analysis_kernel, out_shape=jax.ShapeDtypeStruct(rows.shape...  5.08 us
    ppermute x1, starting transfers between devices, shards(): below = lax.ppermute(rows, 'band', up)  3.04 us
    pallas_call x1, Pallas kernels, forecast(): pl.pallas_call(forecast_kernel, out_shape=jax.ShapeDtypeStruct((lat_rows,...  2.66 us
    ppermute x1, starting transfers between devices, shards(): above = lax.ppermute(rows, 'band', down)  1.28 us
  transfers between devices with their start and end apart: 2, of which 1 were waited for; matrix products, arithmetic and copies ran while one was open for 1% of the time, Pallas kernels for 0%

profile of v9, /device:TPU:0, one launch (start us, length us, event | category | flops | bytes accessed | tf_op | source)
XLA Modules:
  0.0 47.9 jit_solution(10599759124189628992)
XLA Ops:
  0.0 2.7 %shard_map.64 = f32[16,1,3072]{2,1,0:T(1,128)} custom-call(s32[32]{0:T(128)} %fid_ref.1, f32[2,3,16,512]{3,2,1,0:T(8,128)} %x_ref.1), custom_call_target="tpu_custom_call" | custom-call | tf_op jit(solution)/shard_map/pallas_call | solution.py:304
  2.7 0.0 copy-start.4
  2.7 0.0 copy-start.3
  2.7 16.5 %all_to_all.10.x_ref = f32[16,1,3072]{2,1,0:T(1,128)S(1)} all-to-all(f32[16,1,3072]{2,1,0:T(1,128)} %shard_map.64), channel_id=1, replica_groups=mesh['groups'=2,'band'=16] {'band'}, dimensions={0} | all-to-all | bytes 393216 | tf_op jit(solution)/shard_map/all_to_all | solution.py:319
  19.2 1.3 %collective-permute-start.1 = (f32[16,1,3072]{2,1,0:T(1,128)S(1)}, f32[16,1,3072]{2,1,0:T(1,128)S(1)}, u32[]{:S(2)}, u32[]{:S(2)}) collective-permute-start(f32[16,1,3072]{2,1,0:T(1,128)S(1)} %all_to_all.10.x_ref), channel_id=1, source_target_pairs={{1,0},{2,1},{3,2},{4,3},{5,4},{6,5},{7,6},{8,7},{9,8},{10,9},{11,1... | collective-permute-start | bytes 589832 | tf_op jit(solution)/shard_map/ppermute | solution.py:323
  20.5 3.0 %collective-permute-start = (f32[16,1,3072]{2,1,0:T(1,128)S(1)}, f32[16,1,3072]{2,1,0:T(1,128)S(1)}, u32[]{:S(2)}, u32[]{:S(2)}) collective-permute-start(f32[16,1,3072]{2,1,0:T(1,128)S(1)} %all_to_all.10.x_ref), channel_id=1, source_target_pairs={{0,1},{1,2},{2,3},{3,4},{4,5},{5,6},{6,7},{7,8},{8,9},{9,10},{10,1... | collective-permute-start | bytes 589832 | tf_op jit(solution)/shard_map/ppermute | solution.py:322
  23.5 0.0 copy-done.4
  23.5 0.1 reshape.10.fid_col_ref
  23.6 0.1 copy.13
  23.7 0.0 copy-done.3
  23.7 0.0 copy-start.1
  23.7 0.0 copy-start.2
  23.8 0.1 copy.15.noise_ref
  23.9 0.0 collective-permute-done.1.above_ref
  23.9 0.7 %collective-permute-done.below_ref = f32[16,1,3072]{2,1,0:T(1,128)S(1)} collective-permute-done((f32[16,1,3072]{2,1,0:T(1,128)S(1)}, f32[16,1,3072]{2,1,0:T(1,128)S(1)}, u32[]{:S(2)}, u32[]{:S(2)}) %collective-permute-start) | collective-permute-done | bytes 196640 | tf_op jit(solution)/shard_map/ppermute | solution.py:322
  24.6 0.0 copy-start
  24.6 0.0 copy-done.1
  24.6 0.0 copy-done.2
  24.6 0.7 %copy-done = s32[1,256]{1,0:T(1,128)S(1)} copy-done((s32[1,256]{1,0:T(1,128)S(1)}, s32[1,256]{1,0:T(1,128)}, u32[]{:S(2)}) %copy-start) | copy-done | bytes 1048
  25.2 5.1 %shard_map.65 = f32[16,1,3072]{2,1,0:T(1,128)S(1)} custom-call(s32[256]{0:T(256)S(1)} %bitcast.8, f32[16,1,3072]{2,1,0:T(1,128)S(1)} %collective-permute-done.below_ref, f32[16,1,3072]{2,1,0:T(1,128)S(1)} %all_to_all.10.x_ref, f32[16,1,3072]{2,1,0:T(1,128)S(1)} %collective-permute-done.1.above_ref, s32[16,2]{1,0:T(8,128)S(1)} %reshape.10.fid_col_ref, ...), custom_call_target="tpu_custom_call" | custom-call | tf_op jit(solution)/shard_map/pallas_call | solution.py:217
  30.3 16.2 %all_to_all.11 = f32[16,1,3072]{2,1,0:T(1,128)S(1)} all-to-all(f32[16,1,3072]{2,1,0:T(1,128)S(1)} %shard_map.65), channel_id=1, replica_groups=mesh['groups'=2,'band'=16] {'band'}, dimensions={0} | all-to-all | bytes 393216 | tf_op jit(solution)/shard_map/all_to_all | solution.py:327
  46.5 0.5 reduce
  46.9 0.1 reshape.12
  47.1 0.8 %copy.16 = f32[2,3,16,512]{3,2,1,0:T(8,128)} copy(f32[2,3,16,512]{3,1,0,2:T(4,128)S(1)} %bitcast.9) | data formatting | bytes 393216 | tf_op jit(solution)/shard_map/transpose | solution.py:329
  (2 shorter events, 0.0 us)
Async XLA Ops:
  2.7 20.8 %copy-start.4 = (s32[32]{0:T(128)S(1)}, s32[32]{0:T(128)}, u32[]{:S(2)}) copy-start(s32[32]{0:T(128)} %fid_ref.1) | copy-start | bytes 388
  2.7 21.0 %copy-start.3 = (f32[1,256,32]{1,2,0:T(8,128)S(1)}, f32[1,256,32]{1,2,0:T(8,128)}, u32[]{:S(2)}) copy-start(f32[1,256,32]{1,2,0:T(8,128)} %param.11) | copy-start | bytes 98308
  19.2 4.7 %collective-permute-start.1 = (f32[16,1,3072]{2,1,0:T(1,128)S(1)}, f32[16,1,3072]{2,1,0:T(1,128)S(1)}, u32[]{:S(2)}, u32[]{:S(2)}) collective-permute-start(f32[16,1,3072]{2,1,0:T(1,128)S(1)} %all_to_all.10.x_ref), channel_id=1, source_target_pairs={{1,0},{2,1},{3,2},{4,3},{5,4},{6,5},{7,6},{8,7},{9,8},{10,9},{11,1... | collective-permute-start | bytes 589832 | tf_op jit(solution)/shard_map/ppermute | solution.py:323
  20.5 4.1 %collective-permute-start = (f32[16,1,3072]{2,1,0:T(1,128)S(1)}, f32[16,1,3072]{2,1,0:T(1,128)S(1)}, u32[]{:S(2)}, u32[]{:S(2)}) collective-permute-start(f32[16,1,3072]{2,1,0:T(1,128)S(1)} %all_to_all.10.x_ref), channel_id=1, source_target_pairs={{0,1},{1,2},{2,3},{3,4},{4,5},{5,6},{6,7},{7,8},{8,9},{9,10},{10,1... | collective-permute-start | bytes 589832 | tf_op jit(solution)/shard_map/ppermute | solution.py:322
  23.7 0.8 %copy-start.1 = (f32[1,256]{1,0:T(1,128)S(1)}, f32[1,256]{1,0:T(1,128)}, u32[]{:S(2)}) copy-start(f32[1,256]{1,0:T(1,128)} %value_ref.1) | copy-start | bytes 3076
  23.7 0.8 %copy-start.2 = (f32[1,256]{1,0:T(1,128)S(1)}, f32[1,256]{1,0:T(1,128)}, u32[]{:S(2)}) copy-start(f32[1,256]{1,0:T(1,128)} %var_ref.1) | copy-start | bytes 3076
  24.6 0.7 %copy-start = (s32[1,256]{1,0:T(1,128)S(1)}, s32[1,256]{1,0:T(1,128)}, u32[]{:S(2)}) copy-start(s32[1,256]{1,0:T(1,128)} %param.8) | copy-start | bytes 3076

commit v10 on v9

--- a/solution.py
+++ b/solution.py
@@ -207,7 +207,8 @@
     result = x + contract(mixing, spread, ((0,), (0,)))
     sources = x_ref.shape[0]
     for i in range(per_device):
-        o_ref[:, 0, i * width : (i + 1) * width] = result[i * sources : (i + 1) * sources]
+        for component in range(components):
+            o_ref[i, component] = result[i * sources : (i + 1) * sources, component * lon : (component + 1) * lon]
 
 
 def analysis(cells, below, rows, above, fidelity, value, variance, noise):
@@ -216,7 +217,7 @@
     vmem = pl.BlockSpec(memory_space=pltpu.VMEM)
     return pl.pallas_call(
         analysis_kernel,
-        out_shape=jax.ShapeDtypeStruct(rows.shape, jnp.float32),
+        out_shape=jax.ShapeDtypeStruct((members // sources, 3, sources, rows.shape[2] // (3 * members // sources)), jnp.float32),
         in_specs=[pl.BlockSpec(memory_space=pltpu.SMEM)] + [vmem] * 8,
         out_specs=vmem,
         scratch_shapes=[
@@ -324,9 +325,7 @@
     noise = obs_noise[0].reshape(-1, sources, per_device)
     noise = jnp.transpose(noise, (0, 2, 1)).reshape(-1, sources * per_device)
     result = analysis(obs_cell[0], below, rows, above, member_fidelity, obs_value[0], obs_var[0], noise)
-    result = lax.all_to_all(result, "band", 0, 0, tiled=True)
-    result = result.reshape(lat_rows, per_device, components, lon)
-    return jnp.transpose(result, (1, 2, 0, 3))
+    return lax.all_to_all(result, "band", 2, 2, tiled=True)
 
 
 def solution(mesh):

time: 48.2 us -> 47.7 us (0.990)
    transpose x1 -> x0, local copies, waits for them, and re-layouts: 0.8 us -> none  [shards(): return jnp.transpose(result, (1, 2, 0, 3))]
    all_to_all x0 -> x1, local copies, waits for them, and re-layouts: none -> 0.71 us  [shards(): return lax.all_to_all(result, 'band', 2, 2, tiled=True)]
where the time goes in v10:
time: 47.7 us; the launch traced here: 47.3 us
  blocking collectives  32.7 us (69%)
  Pallas kernels  7.72 us (16%)
  starting transfers between devices  4.32 us (9%)
  local copies, waits for them, and re-layouts  1.85 us (4%)
  waiting for transfers between devices  0.69 us (1%)
    all_to_all x1, blocking collectives, shards(): rows = lax.all_to_all(rows, 'band', 0, 0, tiled=True)  16.5 us
    all_to_all x1, blocking collectives, shards(): return lax.all_to_all(result, 'band', 2, 2, tiled=True)  16.2 us
    pallas_call x1, Pallas kernels, analysis(): pl.pallas_call(analysis_kernel, out_shape=jax.ShapeDtypeStruct((members /...  5.06 us
    ppermute x1, starting transfers between devices, shards(): below = lax.ppermute(rows, 'band', up)  3.04 us
    pallas_call x1, Pallas kernels, forecast(): pl.pallas_call(forecast_kernel, out_shape=jax.ShapeDtypeStruct((lat_rows,...  2.66 us
    ppermute x1, starting transfers between devices, shards(): above = lax.ppermute(rows, 'band', down)  1.28 us
  transfers between devices with their start and end apart: 2, of which 1 were waited for; matrix products, arithmetic and copies ran while one was open for 1% of the time, Pallas kernels for 0%

profile of v10, /device:TPU:0, one launch (start us, length us, event | category | flops | bytes accessed | tf_op | source)
XLA Modules:
  0.0 47.3 jit_solution(6156400932680813848)
XLA Ops:
  0.0 2.7 %shard_map.64 = f32[16,1,3072]{2,1,0:T(1,128)} custom-call(s32[32]{0:T(128)} %fid_ref.1, f32[2,3,16,512]{3,2,1,0:T(8,128)} %x_ref.1), custom_call_target="tpu_custom_call" | custom-call | tf_op jit(solution)/shard_map/pallas_call | solution.py:305
  2.7 0.0 copy-start.4
  2.7 0.0 copy-start.3
  2.7 16.5 %all_to_all.10.x_ref = f32[16,1,3072]{2,1,0:T(1,128)S(1)} all-to-all(f32[16,1,3072]{2,1,0:T(1,128)} %shard_map.64), channel_id=1, replica_groups=mesh['groups'=2,'band'=16] {'band'}, dimensions={0} | all-to-all | bytes 393216 | tf_op jit(solution)/shard_map/all_to_all | solution.py:320
  19.2 1.3 %collective-permute-start.1 = (f32[16,1,3072]{2,1,0:T(1,128)S(1)}, f32[16,1,3072]{2,1,0:T(1,128)S(1)}, u32[]{:S(2)}, u32[]{:S(2)}) collective-permute-start(f32[16,1,3072]{2,1,0:T(1,128)S(1)} %all_to_all.10.x_ref), channel_id=1, source_target_pairs={{1,0},{2,1},{3,2},{4,3},{5,4},{6,5},{7,6},{8,7},{9,8},{10,9},{11,1... | collective-permute-start | bytes 589832 | tf_op jit(solution)/shard_map/ppermute | solution.py:324
  20.5 3.0 %collective-permute-start = (f32[16,1,3072]{2,1,0:T(1,128)S(1)}, f32[16,1,3072]{2,1,0:T(1,128)S(1)}, u32[]{:S(2)}, u32[]{:S(2)}) collective-permute-start(f32[16,1,3072]{2,1,0:T(1,128)S(1)} %all_to_all.10.x_ref), channel_id=1, source_target_pairs={{0,1},{1,2},{2,3},{3,4},{4,5},{5,6},{6,7},{7,8},{8,9},{9,10},{10,1... | collective-permute-start | bytes 589832 | tf_op jit(solution)/shard_map/ppermute | solution.py:323
  23.5 0.0 copy-done.4
  23.5 0.1 reshape.7.fid_col_ref
  23.6 0.1 copy.19
  23.7 0.0 copy-done.3
  23.7 0.0 copy-start.1
  23.7 0.0 copy-start.2
  23.8 0.1 copy.21.noise_ref
  23.9 0.0 collective-permute-done.1.above_ref
  23.9 0.7 %collective-permute-done.below_ref = f32[16,1,3072]{2,1,0:T(1,128)S(1)} collective-permute-done((f32[16,1,3072]{2,1,0:T(1,128)S(1)}, f32[16,1,3072]{2,1,0:T(1,128)S(1)}, u32[]{:S(2)}, u32[]{:S(2)}) %collective-permute-start) | collective-permute-done | bytes 196640 | tf_op jit(solution)/shard_map/ppermute | solution.py:323
  24.6 0.0 copy-start
  24.6 0.0 copy-done.1
  24.6 0.0 copy-done.2
  24.6 0.7 %copy-done = s32[1,256]{1,0:T(1,128)S(1)} copy-done((s32[1,256]{1,0:T(1,128)S(1)}, s32[1,256]{1,0:T(1,128)}, u32[]{:S(2)}) %copy-start) | copy-done | bytes 1048
  25.2 5.1 %shard_map.65 = f32[2,3,16,512]{3,2,1,0:T(8,128)S(1)} custom-call(s32[256]{0:T(256)S(1)} %bitcast.7, f32[16,1,3072]{2,1,0:T(1,128)S(1)} %collective-permute-done.below_ref, f32[16,1,3072]{2,1,0:T(1,128)S(1)} %all_to_all.10.x_ref, f32[16,1,3072]{2,1,0:T(1,128)S(1)} %collective-permute-done.1.above_ref, s32[16,2]{1,0:T(8,128)S(1)} %reshape.7.fid_col_ref, ...), custom_call_target="tpu_custom_call" | custom-call | tf_op jit(solution)/shard_map/pallas_call | solution.py:218
  30.3 0.2 copy.22
  30.5 16.2 %all_to_all.11 = f32[2,3,16,512]{3,0,1,2:T(2,128)S(1)} all-to-all(f32[2,3,16,512]{3,0,1,2:T(2,128)S(1)} %copy.22), channel_id=1, replica_groups=mesh['groups'=2,'band'=16] {'band'}, dimensions={2} | all-to-all | bytes 393216 | tf_op jit(solution)/shard_map/all_to_all | solution.py:328
  46.6 0.7 %copy.23 = f32[2,3,16,512]{3,2,1,0:T(8,128)} copy(f32[2,3,16,512]{3,0,1,2:T(2,128)S(1)} %all_to_all.11) | data formatting | bytes 393216 | tf_op jit(solution)/shard_map/all_to_all | solution.py:328
  (2 shorter events, 0.0 us)
Async XLA Ops:
  2.7 20.8 %copy-start.4 = (s32[32]{0:T(128)S(1)}, s32[32]{0:T(128)}, u32[]{:S(2)}) copy-start(s32[32]{0:T(128)} %fid_ref.1) | copy-start | bytes 388
  2.7 21.0 %copy-start.3 = (f32[1,256,32]{1,2,0:T(8,128)S(1)}, f32[1,256,32]{1,2,0:T(8,128)}, u32[]{:S(2)}) copy-start(f32[1,256,32]{1,2,0:T(8,128)} %param.11) | copy-start | bytes 98308
  19.2 4.7 %collective-permute-start.1 = (f32[16,1,3072]{2,1,0:T(1,128)S(1)}, f32[16,1,3072]{2,1,0:T(1,128)S(1)}, u32[]{:S(2)}, u32[]{:S(2)}) collective-permute-start(f32[16,1,3072]{2,1,0:T(1,128)S(1)} %all_to_all.10.x_ref), channel_id=1, source_target_pairs={{1,0},{2,1},{3,2},{4,3},{5,4},{6,5},{7,6},{8,7},{9,8},{10,9},{11,1... | collective-permute-start | bytes 589832 | tf_op jit(solution)/shard_map/ppermute | solution.py:324
  20.5 4.1 %collective-permute-start = (f32[16,1,3072]{2,1,0:T(1,128)S(1)}, f32[16,1,3072]{2,1,0:T(1,128)S(1)}, u32[]{:S(2)}, u32[]{:S(2)}) collective-permute-start(f32[16,1,3072]{2,1,0:T(1,128)S(1)} %all_to_all.10.x_ref), channel_id=1, source_target_pairs={{0,1},{1,2},{2,3},{3,4},{4,5},{5,6},{6,7},{7,8},{8,9},{9,10},{10,1... | collective-permute-start | bytes 589832 | tf_op jit(solution)/shard_map/ppermute | solution.py:323
  23.7 0.8 %copy-start.1 = (f32[1,256]{1,0:T(1,128)S(1)}, f32[1,256]{1,0:T(1,128)}, u32[]{:S(2)}) copy-start(f32[1,256]{1,0:T(1,128)} %value_ref.1) | copy-start | bytes 3076
  23.7 0.8 %copy-start.2 = (f32[1,256]{1,0:T(1,128)S(1)}, f32[1,256]{1,0:T(1,128)}, u32[]{:S(2)}) copy-start(f32[1,256]{1,0:T(1,128)} %var_ref.1) | copy-start | bytes 3076
  24.6 0.7 %copy-start = (s32[1,256]{1,0:T(1,128)S(1)}, s32[1,256]{1,0:T(1,128)}, u32[]{:S(2)}) copy-start(s32[1,256]{1,0:T(1,128)} %param.8) | copy-start | bytes 3076

commit v11 on v10

--- a/solution.py
+++ b/solution.py
@@ -148,13 +148,15 @@
     o_ref, cells_ref, picked_ref,
 ):
     per_device = fid_col_ref.shape[1]
-    width = x_ref.shape[2] // per_device
     def members_of(ref):
-        return jnp.concatenate([ref[:, 0, i * width : (i + 1) * width] for i in range(per_device)], axis=0)
+        return jnp.concatenate(
+            [jnp.concatenate([ref[i, c] for c in range(ref.shape[1])], axis=1) for i in range(per_device)],
+            axis=0,
+        )
     x = members_of(x_ref)
     m = x.shape[0]
     components = 3
-    lon = width // components
+    lon = x_ref.shape[3]
     for offset, ref in enumerate((below_ref, x_ref, above_ref)):
         block = x if offset == 1 else members_of(ref)
         block = block.T
@@ -205,23 +207,23 @@
     projected = direct - contract(inner, scale_col * solved, ((1,), (0,)))
     mixing = projected * weight
     result = x + contract(mixing, spread, ((0,), (0,)))
-    sources = x_ref.shape[0]
+    sources = x_ref.shape[2]
     for i in range(per_device):
         for component in range(components):
             o_ref[i, component] = result[i * sources : (i + 1) * sources, component * lon : (component + 1) * lon]
 
 
 def analysis(cells, below, rows, above, fidelity, value, variance, noise):
-    sources = rows.shape[0]
+    sources = rows.shape[2]
     members = fidelity.shape[0]
     vmem = pl.BlockSpec(memory_space=pltpu.VMEM)
     return pl.pallas_call(
         analysis_kernel,
-        out_shape=jax.ShapeDtypeStruct((members // sources, 3, sources, rows.shape[2] // (3 * members // sources)), jnp.float32),
+        out_shape=jax.ShapeDtypeStruct(rows.shape, jnp.float32),
         in_specs=[pl.BlockSpec(memory_space=pltpu.SMEM)] + [vmem] * 8,
         out_specs=vmem,
         scratch_shapes=[
-            pltpu.VMEM((3 * rows.shape[2] // (members // sources), members), jnp.float32),
+            pltpu.VMEM((9 * rows.shape[3], members), jnp.float32),
             pltpu.VMEM((cells.shape[0], members), jnp.float32),
         ],
         compiler_params=pltpu.CompilerParams(vmem_limit_bytes=48 * 1024 * 1024),
@@ -297,14 +299,14 @@
             )
             height, eastward, northward = height_new, east_new, north_new
         for component, field in enumerate((height, eastward, northward)):
-            o_ref[:, 0, pl.ds((member * 3 + component) * lon, lon)] = field
+            o_ref[member, component] = field
 
 
 def forecast(initial, levels):
     members, components, lat_rows, lon = initial.shape
     return pl.pallas_call(
         forecast_kernel,
-        out_shape=jax.ShapeDtypeStruct((lat_rows, 1, members * components * lon), jnp.float32),
+        out_shape=jax.ShapeDtypeStruct(initial.shape, jnp.float32),
         in_specs=[
             pl.BlockSpec(memory_space=pltpu.SMEM),
             pl.BlockSpec(memory_space=pltpu.VMEM),
@@ -317,7 +319,7 @@
     per_device, components, lat_rows, lon = initial_height_velocity.shape
     sources = lax.axis_size("band")
     rows = forecast(initial_height_velocity, member_fidelity)
-    rows = lax.all_to_all(rows, "band", 0, 0, tiled=True)
+    rows = lax.all_to_all(rows, "band", 2, 2, tiled=True)
     up = [(i, i + 1) for i in range(sources - 1)]
     down = [(j, i) for i, j in up]
     below = lax.ppermute(rows, "band", up)

time: 47.7 us -> 48.4 us (1.015)
  local copies, waits for them, and re-layouts: 1.85 us -> 2.97 us
    pallas_call x1 -> x2, local copies, waits for them, and re-layouts: 0.15 us -> 1.23 us  [the longest x1 1.08 us: forecast(): pl.pallas_call(forecast_kernel, out_shape=jax.ShapeDtypeStruct(initial.sh...]
where the time goes in v11:
time: 48.4 us; the launch traced here: 48.1 us
  blocking collectives  32.3 us (67%)
  Pallas kernels  7.69 us (16%)
  starting transfers between devices  4.33 us (9%)
  local copies, waits for them, and re-layouts  2.97 us (6%)
  waiting for transfers between devices  0.69 us (1%)
    all_to_all x1, blocking collectives, shards(): rows = lax.all_to_all(rows, 'band', 2, 2, tiled=True)  16.2 us
    all_to_all x1, blocking collectives, shards(): return lax.all_to_all(result, 'band', 2, 2, tiled=True)  16.2 us
    pallas_call x1, Pallas kernels, analysis(): pl.pallas_call(analysis_kernel, out_shape=jax.ShapeDtypeStruct(rows.shape...  5.07 us
    ppermute x1, starting transfers between devices, shards(): below = lax.ppermute(rows, 'band', up)  3.04 us
    pallas_call x1, Pallas kernels, forecast(): pl.pallas_call(forecast_kernel, out_shape=jax.ShapeDtypeStruct(initial.sh...  2.62 us
    ppermute x1, starting transfers between devices, shards(): above = lax.ppermute(rows, 'band', down)  1.29 us
    pallas_call x1, local copies, waits for them, and re-layouts, forecast(): pl.pallas_call(forecast_kernel, out_shape=jax.ShapeDtypeStruct(initial.sh...  1.08 us
  transfers between devices with their start and end apart: 2, of which 1 were waited for; matrix products, arithmetic and copies ran while one was open for 1% of the time, Pallas kernels for 0%

profile of v11, /device:TPU:0, one launch (start us, length us, event | category | flops | bytes accessed | tf_op | source)
XLA Modules:
  0.0 48.1 jit_solution(4272512643796797817)
XLA Ops:
  0.0 2.6 %shard_map.64 = f32[2,3,16,512]{3,2,1,0:T(8,128)} custom-call(s32[32]{0:T(128)} %fid_ref.1, f32[2,3,16,512]{3,2,1,0:T(8,128)} %x_ref.1), custom_call_target="tpu_custom_call" | custom-call | tf_op jit(solution)/shard_map/pallas_call | solution.py:307
  2.6 1.1 %copy.23 = f32[2,3,16,512]{3,0,1,2:T(2,128)S(1)} copy(f32[2,3,16,512]{3,2,1,0:T(8,128)} %shard_map.64) | data formatting | bytes 393216 | tf_op jit(solution)/shard_map/pallas_call | solution.py:307
  3.7 16.2 %all_to_all.10 = f32[2,3,16,512]{3,0,1,2:T(2,128)S(1)} all-to-all(f32[2,3,16,512]{3,0,1,2:T(2,128)S(1)} %copy.23), channel_id=1, replica_groups=mesh['groups'=2,'band'=16] {'band'}, dimensions={2} | all-to-all | bytes 393216 | tf_op jit(solution)/shard_map/all_to_all | solution.py:322
  19.9 0.0 copy-start.4
  19.9 0.0 copy-start.3
  19.9 1.3 %collective-permute-start.1 = (f32[2,3,16,512]{3,2,1,0:T(8,128)S(1)}, f32[2,3,16,512]{3,2,1,0:T(8,128)S(1)}, u32[]{:S(2)}, u32[]{:S(2)}) collective-permute-start(f32[2,3,16,512]{3,2,1,0:T(8,128)S(1)} %copy.24.x_ref), channel_id=1, source_target_pairs={{1,0},{2,1},{3,2},{4,3},{5,4},{6,5},{7,6},{8,7},{9,8},{10,9},{11,1... | collective-permute-start | bytes 589832 | tf_op jit(solution)/shard_map/ppermute | solution.py:326
  21.2 3.0 %collective-permute-start = (f32[2,3,16,512]{3,2,1,0:T(8,128)S(1)}, f32[2,3,16,512]{3,2,1,0:T(8,128)S(1)}, u32[]{:S(2)}, u32[]{:S(2)}) collective-permute-start(f32[2,3,16,512]{3,2,1,0:T(8,128)S(1)} %copy.24.x_ref), channel_id=1, source_target_pairs={{0,1},{1,2},{2,3},{3,4},{4,5},{5,6},{6,7},{7,8},{8,9},{9,10},{10,1... | collective-permute-start | bytes 589832 | tf_op jit(solution)/shard_map/ppermute | solution.py:325
  24.3 0.0 copy-done.4
  24.3 0.1 reshape.7.fid_col_ref
  24.4 0.1 copy.26
  24.5 0.0 copy-done.3
  24.5 0.0 copy-start.1
  24.5 0.0 copy-start.2
  24.5 0.1 copy.29.noise_ref
  24.6 0.0 collective-permute-done.1.above_ref
  24.6 0.7 %collective-permute-done.below_ref = f32[2,3,16,512]{3,2,1,0:T(8,128)S(1)} collective-permute-done((f32[2,3,16,512]{3,2,1,0:T(8,128)S(1)}, f32[2,3,16,512]{3,2,1,0:T(8,128)S(1)}, u32[]{:S(2)}, u32[]{:S(2)}) %collective-permute-start) | collective-permute-done | bytes 196640 | tf_op jit(solution)/shard_map/ppermute | solution.py:325
  25.3 0.0 copy-start
  25.3 0.0 copy-done.1
  25.3 0.0 copy-done.2
  25.3 0.7 %copy-done = s32[1,256]{1,0:T(1,128)S(1)} copy-done((s32[1,256]{1,0:T(1,128)S(1)}, s32[1,256]{1,0:T(1,128)}, u32[]{:S(2)}) %copy-start) | copy-done | bytes 1048
  26.0 5.1 %shard_map.65 = f32[2,3,16,512]{3,2,1,0:T(8,128)S(1)} custom-call(s32[256]{0:T(256)S(1)} %bitcast.7, f32[2,3,16,512]{3,2,1,0:T(8,128)S(1)} %collective-permute-done.below_ref, f32[2,3,16,512]{3,2,1,0:T(8,128)S(1)} %copy.24.x_ref, f32[2,3,16,512]{3,2,1,0:T(8,128)S(1)} %collective-permute-done.1.above_ref, s32[16,2]{1,0:T(8,128)S(1)} %reshape.7.fid_col_ref, ...), custom_call_target="tpu_custom_call" | custom-call | tf_op jit(solution)/shard_map/pallas_call | solution.py:220
  31.1 0.2 copy.30
  31.2 16.2 %all_to_all.11 = f32[2,3,16,512]{3,0,1,2:T(2,128)S(1)} all-to-all(f32[2,3,16,512]{3,0,1,2:T(2,128)S(1)} %copy.30), channel_id=1, replica_groups=mesh['groups'=2,'band'=16] {'band'}, dimensions={2} | all-to-all | bytes 393216 | tf_op jit(solution)/shard_map/all_to_all | solution.py:330
  47.4 0.7 %copy.31 = f32[2,3,16,512]{3,2,1,0:T(8,128)} copy(f32[2,3,16,512]{3,0,1,2:T(2,128)S(1)} %all_to_all.11) | data formatting | bytes 393216 | tf_op jit(solution)/shard_map/all_to_all | solution.py:330
  (3 shorter events, 0.1 us)
Async XLA Ops:
  19.9 4.4 %copy-start.4 = (s32[32]{0:T(128)S(1)}, s32[32]{0:T(128)}, u32[]{:S(2)}) copy-start(s32[32]{0:T(128)} %fid_ref.1) | copy-start | bytes 388
  19.9 4.6 %copy-start.3 = (f32[1,256,32]{1,2,0:T(8,128)S(1)}, f32[1,256,32]{1,2,0:T(8,128)}, u32[]{:S(2)}) copy-start(f32[1,256,32]{1,2,0:T(8,128)} %param.11) | copy-start | bytes 98308
  19.9 4.7 %collective-permute-start.1 = (f32[2,3,16,512]{3,2,1,0:T(8,128)S(1)}, f32[2,3,16,512]{3,2,1,0:T(8,128)S(1)}, u32[]{:S(2)}, u32[]{:S(2)}) collective-permute-start(f32[2,3,16,512]{3,2,1,0:T(8,128)S(1)} %copy.24.x_ref), channel_id=1, source_target_pairs={{1,0},{2,1},{3,2},{4,3},{5,4},{6,5},{7,6},{8,7},{9,8},{10,9},{11,1... | collective-permute-start | bytes 589832 | tf_op jit(solution)/shard_map/ppermute | solution.py:326
  21.2 4.1 %collective-permute-start = (f32[2,3,16,512]{3,2,1,0:T(8,128)S(1)}, f32[2,3,16,512]{3,2,1,0:T(8,128)S(1)}, u32[]{:S(2)}, u32[]{:S(2)}) collective-permute-start(f32[2,3,16,512]{3,2,1,0:T(8,128)S(1)} %copy.24.x_ref), channel_id=1, source_target_pairs={{0,1},{1,2},{2,3},{3,4},{4,5},{5,6},{6,7},{7,8},{8,9},{9,10},{10,1... | collective-permute-start | bytes 589832 | tf_op jit(solution)/shard_map/ppermute | solution.py:325
  24.5 0.8 %copy-start.1 = (f32[1,256]{1,0:T(1,128)S(1)}, f32[1,256]{1,0:T(1,128)}, u32[]{:S(2)}) copy-start(f32[1,256]{1,0:T(1,128)} %value_ref.1) | copy-start | bytes 3076
  24.5 0.8 %copy-start.2 = (f32[1,256]{1,0:T(1,128)S(1)}, f32[1,256]{1,0:T(1,128)}, u32[]{:S(2)}) copy-start(f32[1,256]{1,0:T(1,128)} %var_ref.1) | copy-start | bytes 3076
  25.3 0.7 %copy-start = (s32[1,256]{1,0:T(1,128)S(1)}, s32[1,256]{1,0:T(1,128)}, u32[]{:S(2)}) copy-start(s32[1,256]{1,0:T(1,128)} %param.8) | copy-start | bytes 3076

commit v12 on v10

--- a/solution.py
+++ b/solution.py
@@ -324,7 +324,8 @@
     above = lax.ppermute(rows, "band", down)
     noise = obs_noise[0].reshape(-1, sources, per_device)
     noise = jnp.transpose(noise, (0, 2, 1)).reshape(-1, sources * per_device)
-    result = analysis(obs_cell[0], below, rows, above, member_fidelity, obs_value[0], obs_var[0], noise)
+    cells = jnp.clip(obs_cell[0], 0, 9 * lon - 1)
+    result = analysis(cells, below, rows, above, member_fidelity, obs_value[0] + 0.0 * obs_var[0], obs_var[0], noise)
     return lax.all_to_all(result, "band", 2, 2, tiled=True)
 
 

time: 47.7 us -> 47 us (0.985)
  blocking collectives: 32.7 us -> 16.2 us
  waiting for transfers between devices: 0.69 us -> 9.04 us
  starting transfers between devices: 4.32 us -> 11.9 us
    all_to_all x1 -> x0, blocking collectives: 16.5 us -> none  [shards(): rows = lax.all_to_all(rows, 'band', 0, 0, tiled=True)]
    all_to_all x0 -> x1, waiting for transfers between devices: none -> 8.03 us  [shards(): rows = lax.all_to_all(rows, 'band', 0, 0, tiled=True)]
    all_to_all x0 -> x1, starting transfers between devices: none -> 7.55 us  [shards(): rows = lax.all_to_all(rows, 'band', 0, 0, tiled=True)]
  transfers between devices with their start and end apart: 2 -> 3, of which waited for: 1 -> 2; matrix products, arithmetic and copies ran while one was open for 1% -> 1% of each run, Pallas kernels for 0% -> 0%
where the time goes in v12:
time: 47 us; the launch traced here: 46.7 us
  blocking collectives  16.2 us (34%)
  starting transfers between devices  11.9 us (25%)
  waiting for transfers between devices  9.04 us (19%)
  Pallas kernels  7.73 us (16%)
  local copies, waits for them, and re-layouts  1.76 us (4%)
    all_to_all x1, blocking collectives, shards(): return lax.all_to_all(result, 'band', 2, 2, tiled=True)  16.2 us
    all_to_all x1, waiting for transfers between devices, shards(): rows = lax.all_to_all(rows, 'band', 0, 0, tiled=True)  8.03 us
    all_to_all x1, starting transfers between devices, shards(): rows = lax.all_to_all(rows, 'band', 0, 0, tiled=True)  7.55 us
    pallas_call x1, Pallas kernels, analysis(): pl.pallas_call(analysis_kernel, out_shape=jax.ShapeDtypeStruct((members /...  5.07 us
    ppermute x1, starting transfers between devices, shards(): below = lax.ppermute(rows, 'band', up)  3.04 us
    pallas_call x1, Pallas kernels, forecast(): pl.pallas_call(forecast_kernel, out_shape=jax.ShapeDtypeStruct((lat_rows,...  2.66 us
    ppermute x1, starting transfers between devices, shards(): above = lax.ppermute(rows, 'band', down)  1.28 us
    ppermute x1, waiting for transfers between devices, shards(): below = lax.ppermute(rows, 'band', up)  1.01 us
  transfers between devices with their start and end apart: 3, of which 2 were waited for; matrix products, arithmetic and copies ran while one was open for 1% of the time, Pallas kernels for 0%

profile of v12, /device:TPU:0, one launch (start us, length us, event | category | flops | bytes accessed | tf_op | source)
XLA Modules:
  0.0 46.7 jit_solution(14167034887369540074)
XLA Ops:
  0.0 2.7 %shard_map.64 = f32[16,1,3072]{2,1,0:T(1,128)} custom-call(s32[32]{0:T(128)} %fid_ref.1, f32[2,3,16,512]{3,2,1,0:T(8,128)} %x_ref.1), custom_call_target="tpu_custom_call" | custom-call | tf_op jit(solution)/shard_map/pallas_call | solution.py:305
  2.7 0.0 copy-start.2
  2.7 0.0 copy-start.1
  2.7 7.5 %all-to-all-start = ((f32[16,1,3072]{2,1,0:T(1,128)}), f32[16,1,3072]{2,1,0:T(1,128)S(1)}, u32[]{:S(2)}, u32[]{:S(2)}) async-start(f32[16,1,3072]{2,1,0:T(1,128)} %shard_map.64), calls=%async_computation | async-start | bytes 393216 | tf_op jit(solution)/shard_map/all_to_all | solution.py:320
  10.2 0.0 copy-done.2
  10.2 0.1 reshape.11.fid_col_ref
  10.3 0.1 copy.19
  10.4 0.0 copy-done.1
  10.4 0.0 copy-start
  10.5 0.0 copy-start.3
  10.5 0.1 copy.21.noise_ref
  10.6 0.6 %copy-done = f32[1,256]{1,0:T(1,128)S(1)} copy-done((f32[1,256]{1,0:T(1,128)S(1)}, f32[1,256]{1,0:T(1,128)}, u32[]{:S(2)}) %copy-start) | copy-done | bytes 1048
  11.1 0.0 copy-done.3
  11.1 0.0 copy-start.4
  11.2 8.0 %all-to-all-done.x_ref = f32[16,1,3072]{2,1,0:T(1,128)S(1)} async-done(((f32[16,1,3072]{2,1,0:T(1,128)}), f32[16,1,3072]{2,1,0:T(1,128)S(1)}, u32[]{:S(2)}, u32[]{:S(2)}) %all-to-all-start) | async-done | bytes 196640 | tf_op jit(solution)/shard_map/all_to_all | solution.py:320
  19.2 1.3 %collective-permute-start.1 = (f32[16,1,3072]{2,1,0:T(1,128)S(1)}, f32[16,1,3072]{2,1,0:T(1,128)S(1)}, u32[]{:S(2)}, u32[]{:S(2)}) collective-permute-start(f32[16,1,3072]{2,1,0:T(1,128)S(1)} %all-to-all-done.x_ref), channel_id=1, source_target_pairs={{1,0},{2,1},{3,2},{4,3},{5,4},{6,5},{7,6},{8,7},{9,8},{10,9},{11,1... | collective-permute-start | bytes 589832 | tf_op jit(solution)/shard_map/ppermute | solution.py:324
  20.5 3.0 %collective-permute-start = (f32[16,1,3072]{2,1,0:T(1,128)S(1)}, f32[16,1,3072]{2,1,0:T(1,128)S(1)}, u32[]{:S(2)}, u32[]{:S(2)}) collective-permute-start(f32[16,1,3072]{2,1,0:T(1,128)S(1)} %all-to-all-done.x_ref), channel_id=1, source_target_pairs={{0,1},{1,2},{2,3},{3,4},{4,5},{5,6},{6,7},{7,8},{8,9},{9,10},{10,1... | collective-permute-start | bytes 589832 | tf_op jit(solution)/shard_map/ppermute | solution.py:323
  23.5 0.0 copy-done.4
  23.5 0.0 collective-permute-done.1.above_ref
  23.6 1.0 %collective-permute-done.below_ref = f32[16,1,3072]{2,1,0:T(1,128)S(1)} collective-permute-done((f32[16,1,3072]{2,1,0:T(1,128)S(1)}, f32[16,1,3072]{2,1,0:T(1,128)S(1)}, u32[]{:S(2)}, u32[]{:S(2)}) %collective-permute-start) | collective-permute-done | bytes 196640 | tf_op jit(solution)/shard_map/ppermute | solution.py:323
  24.6 5.1 %shard_map.65 = f32[2,3,16,512]{3,2,1,0:T(8,128)S(1)} custom-call(s32[256]{0:T(256)S(1)} %bitcast.7, f32[16,1,3072]{2,1,0:T(1,128)S(1)} %collective-permute-done.below_ref, f32[16,1,3072]{2,1,0:T(1,128)S(1)} %all-to-all-done.x_ref, f32[16,1,3072]{2,1,0:T(1,128)S(1)} %collective-permute-done.1.above_ref, s32[16,2]{1,0:T(8,128)S(1)} %reshape.11.fid_col_ref, ...), custom_call_target="tpu_custom_call" | custom-call | tf_op jit(solution)/shard_map/pallas_call | solution.py:218
  29.6 0.2 copy.22
  29.8 16.2 %all_to_all.10 = f32[2,3,16,512]{3,0,1,2:T(2,128)S(1)} all-to-all(f32[2,3,16,512]{3,0,1,2:T(2,128)S(1)} %copy.22), channel_id=1, replica_groups=mesh['groups'=2,'band'=16] {'band'}, dimensions={2} | all-to-all | bytes 393216 | tf_op jit(solution)/shard_map/all_to_all | solution.py:329
  45.9 0.7 %copy.23 = f32[2,3,16,512]{3,2,1,0:T(8,128)} copy(f32[2,3,16,512]{3,0,1,2:T(2,128)S(1)} %all_to_all.10) | data formatting | bytes 393216 | tf_op jit(solution)/shard_map/all_to_all | solution.py:329
  (4 shorter events, 0.0 us)
Async XLA Ops:
  2.7 7.6 %copy-start.2 = (s32[32]{0:T(128)S(1)}, s32[32]{0:T(128)}, u32[]{:S(2)}) copy-start(s32[32]{0:T(128)} %fid_ref.1) | copy-start | bytes 388
  2.7 7.7 %copy-start.1 = (f32[1,256,32]{1,2,0:T(8,128)S(1)}, f32[1,256,32]{1,2,0:T(8,128)}, u32[]{:S(2)}) copy-start(f32[1,256,32]{1,2,0:T(8,128)} %param.11) | copy-start | bytes 98308
  2.7 16.5 %all-to-all-start = ((f32[16,1,3072]{2,1,0:T(1,128)}), f32[16,1,3072]{2,1,0:T(1,128)S(1)}, u32[]{:S(2)}, u32[]{:S(2)}) async-start(f32[16,1,3072]{2,1,0:T(1,128)} %shard_map.64), calls=%async_computation | async-start | bytes 393216 | tf_op jit(solution)/shard_map/all_to_all | solution.py:320
  10.4 0.7 %copy-start = (f32[1,256]{1,0:T(1,128)S(1)}, f32[1,256]{1,0:T(1,128)}, u32[]{:S(2)}) copy-start(f32[1,256]{1,0:T(1,128)} %var_ref.1) | copy-start | bytes 3076
  10.5 0.7 %copy-start.3 = (f32[1,256]{1,0:T(1,128)S(1)}, f32[1,256]{1,0:T(1,128)}, u32[]{:S(2)}) copy-start(f32[1,256]{1,0:T(1,128)} %param.9) | copy-start | bytes 3076
  11.1 12.4 %copy-start.4 = (s32[1,256]{1,0:T(1,128)S(1)}, s32[1,256]{1,0:T(1,128)}, u32[]{:S(2)}) copy-start(s32[1,256]{1,0:T(1,128)} %param.8) | copy-start | bytes 3076
  19.2 4.4 %collective-permute-start.1 = (f32[16,1,3072]{2,1,0:T(1,128)S(1)}, f32[16,1,3072]{2,1,0:T(1,128)S(1)}, u32[]{:S(2)}, u32[]{:S(2)}) collective-permute-start(f32[16,1,3072]{2,1,0:T(1,128)S(1)} %all-to-all-done.x_ref), channel_id=1, source_target_pairs={{1,0},{2,1},{3,2},{4,3},{5,4},{6,5},{7,6},{8,7},{9,8},{10,9},{11,1... | collective-permute-start | bytes 589832 | tf_op jit(solution)/shard_map/ppermute | solution.py:324
  20.5 4.1 %collective-permute-start = (f32[16,1,3072]{2,1,0:T(1,128)S(1)}, f32[16,1,3072]{2,1,0:T(1,128)S(1)}, u32[]{:S(2)}, u32[]{:S(2)}) collective-permute-start(f32[16,1,3072]{2,1,0:T(1,128)S(1)} %all-to-all-done.x_ref), channel_id=1, source_target_pairs={{0,1},{1,2},{2,3},{3,4},{4,5},{5,6},{6,7},{7,8},{8,9},{9,10},{10,1... | collective-permute-start | bytes 589832 | tf_op jit(solution)/shard_map/ppermute | solution.py:323

commit v13 on v12

--- a/solution.py
+++ b/solution.py
@@ -274,26 +274,35 @@
         nonlinear = jnp.where(level == 0, 1.0, 0.0).astype(jnp.float32)
         friction = jnp.where(level == 0, 0.0, slow_friction).astype(jnp.float32)
         height, eastward, northward = x_ref[member, 0], x_ref[member, 1], x_ref[member, 2]
+        keep = 1.0 - time_step * friction
+        advect = -nonlinear * (0.5 * time_step)
+        turn = time_step * coriolis
         for step in range(PREDICTION_COUNT):
             depth = 1.0 + nonlinear * height
+            east_flux, north_flux = depth * eastward, depth * northward
+            h_ahead, h_behind, h_upper, h_lower = kernel_neighbours(height)
             height_new = (
                 height
-                - time_step * (kernel_east(depth * eastward) + kernel_north(depth * northward))
-                + time_step * viscous * kernel_laplace(height)
+                - (0.5 * time_step)
+                * ((shifted(east_flux, 1, 1) - shifted(east_flux, -1, 1)) + (shifted(north_flux, 1, 0) - shifted(north_flux, -1, 0)))
+                + (time_step * viscous) * ((h_ahead + h_behind) + (h_upper + h_lower) - 4.0 * height)
             )
-            east_new = eastward + time_step * (
-                -nonlinear * (eastward * kernel_east(eastward) + northward * kernel_north(eastward))
-                + coriolis * northward
-                - kernel_east(height_new)
-                + viscous * kernel_laplace(eastward)
-                - friction * eastward
+            n_ahead, n_behind, n_upper, n_lower = kernel_neighbours(height_new)
+            u_ahead, u_behind, u_upper, u_lower = kernel_neighbours(eastward)
+            v_ahead, v_behind, v_upper, v_lower = kernel_neighbours(northward)
+            east_new = (
+                keep * eastward
+                + advect * (eastward * (u_ahead - u_behind) + northward * (u_upper - u_lower))
+                + turn * northward
+                - (0.5 * time_step) * (n_ahead - n_behind)
+                + (time_step * viscous) * ((u_ahead + u_behind) + (u_upper + u_lower) - 4.0 * eastward)
             )
-            north_new = northward + time_step * (
-                -nonlinear * (eastward * kernel_east(northward) + northward * kernel_north(northward))
-                - coriolis * eastward
-                - kernel_north(height_new)
-                + viscous * kernel_laplace(northward)
-                - friction * northward
+            north_new = (
+                keep * northward
+                + advect * (eastward * (v_ahead - v_behind) + northward * (v_upper - v_lower))
+                - turn * eastward
+                - (0.5 * time_step) * (n_upper - n_lower)
+                + (time_step * viscous) * ((v_ahead + v_behind) + (v_upper + v_lower) - 4.0 * northward)
             )
             height, eastward, northward = height_new, east_new, north_new
         for component, field in enumerate((height, eastward, northward)):

time: 47 us -> 46.9 us (level)
  no operation moved by 1% of the time
where the time goes in v13:
time: 46.9 us; the launch traced here: 46.6 us
  blocking collectives  16.2 us (35%)
  starting transfers between devices  11.9 us (25%)
  waiting for transfers between devices  9.04 us (19%)
  Pallas kernels  7.65 us (16%)
  local copies, waits for them, and re-layouts  1.76 us (4%)
    all_to_all x1, blocking collectives, shards(): return lax.all_to_all(result, 'band', 2, 2, tiled=True)  16.2 us
    all_to_all x1, waiting for transfers between devices, shards(): rows = lax.all_to_all(rows, 'band', 0, 0, tiled=True)  8.03 us
    all_to_all x1, starting transfers between devices, shards(): rows = lax.all_to_all(rows, 'band', 0, 0, tiled=True)  7.55 us
    pallas_call x1, Pallas kernels, analysis(): pl.pallas_call(analysis_kernel, out_shape=jax.ShapeDtypeStruct((members /...  5.06 us
    ppermute x1, starting transfers between devices, shards(): below = lax.ppermute(rows, 'band', up)  3.04 us
    pallas_call x1, Pallas kernels, forecast(): pl.pallas_call(forecast_kernel, out_shape=jax.ShapeDtypeStruct((lat_rows,...  2.59 us
    ppermute x1, starting transfers between devices, shards(): above = lax.ppermute(rows, 'band', down)  1.28 us
    ppermute x1, waiting for transfers between devices, shards(): below = lax.ppermute(rows, 'band', up)  1.01 us
  transfers between devices with their start and end apart: 3, of which 2 were waited for; matrix products, arithmetic and copies ran while one was open for 1% of the time, Pallas kernels for 0%

profile of v13, /device:TPU:0, one launch (start us, length us, event | category | flops | bytes accessed | tf_op | source)
XLA Modules:
  0.0 46.6 jit_solution(9620165096546232856)
XLA Ops:
  0.0 2.6 %shard_map.64 = f32[16,1,3072]{2,1,0:T(1,128)} custom-call(s32[32]{0:T(128)} %fid_ref.1, f32[2,3,16,512]{3,2,1,0:T(8,128)} %x_ref.1), custom_call_target="tpu_custom_call" | custom-call | tf_op jit(solution)/shard_map/pallas_call | solution.py:314
  2.6 0.0 copy-start.2
  2.6 0.0 copy-start.1
  2.6 7.5 %all-to-all-start = ((f32[16,1,3072]{2,1,0:T(1,128)}), f32[16,1,3072]{2,1,0:T(1,128)S(1)}, u32[]{:S(2)}, u32[]{:S(2)}) async-start(f32[16,1,3072]{2,1,0:T(1,128)} %shard_map.64), calls=%async_computation | async-start | bytes 393216 | tf_op jit(solution)/shard_map/all_to_all | solution.py:329
  10.1 0.0 copy-done.2
  10.2 0.1 reshape.11.fid_col_ref
  10.2 0.1 copy.19
  10.3 0.0 copy-done.1
  10.4 0.0 copy-start
  10.4 0.0 copy-start.3
  10.4 0.1 copy.21.noise_ref
  10.5 0.6 %copy-done = f32[1,256]{1,0:T(1,128)S(1)} copy-done((f32[1,256]{1,0:T(1,128)S(1)}, f32[1,256]{1,0:T(1,128)}, u32[]{:S(2)}) %copy-start) | copy-done | bytes 1048
  11.1 0.0 copy-done.3
  11.1 0.0 copy-start.4
  11.1 8.0 %all-to-all-done.x_ref = f32[16,1,3072]{2,1,0:T(1,128)S(1)} async-done(((f32[16,1,3072]{2,1,0:T(1,128)}), f32[16,1,3072]{2,1,0:T(1,128)S(1)}, u32[]{:S(2)}, u32[]{:S(2)}) %all-to-all-start) | async-done | bytes 196640 | tf_op jit(solution)/shard_map/all_to_all | solution.py:329
  19.1 1.3 %collective-permute-start.1 = (f32[16,1,3072]{2,1,0:T(1,128)S(1)}, f32[16,1,3072]{2,1,0:T(1,128)S(1)}, u32[]{:S(2)}, u32[]{:S(2)}) collective-permute-start(f32[16,1,3072]{2,1,0:T(1,128)S(1)} %all-to-all-done.x_ref), channel_id=1, source_target_pairs={{1,0},{2,1},{3,2},{4,3},{5,4},{6,5},{7,6},{8,7},{9,8},{10,9},{11,1... | collective-permute-start | bytes 589832 | tf_op jit(solution)/shard_map/ppermute | solution.py:333
  20.4 3.0 %collective-permute-start = (f32[16,1,3072]{2,1,0:T(1,128)S(1)}, f32[16,1,3072]{2,1,0:T(1,128)S(1)}, u32[]{:S(2)}, u32[]{:S(2)}) collective-permute-start(f32[16,1,3072]{2,1,0:T(1,128)S(1)} %all-to-all-done.x_ref), channel_id=1, source_target_pairs={{0,1},{1,2},{2,3},{3,4},{4,5},{5,6},{6,7},{7,8},{8,9},{9,10},{10,1... | collective-permute-start | bytes 589832 | tf_op jit(solution)/shard_map/ppermute | solution.py:332
  23.4 0.0 copy-done.4
  23.5 0.0 collective-permute-done.1.above_ref
  23.5 1.0 %collective-permute-done.below_ref = f32[16,1,3072]{2,1,0:T(1,128)S(1)} collective-permute-done((f32[16,1,3072]{2,1,0:T(1,128)S(1)}, f32[16,1,3072]{2,1,0:T(1,128)S(1)}, u32[]{:S(2)}, u32[]{:S(2)}) %collective-permute-start) | collective-permute-done | bytes 196640 | tf_op jit(solution)/shard_map/ppermute | solution.py:332
  24.5 5.1 %shard_map.65 = f32[2,3,16,512]{3,2,1,0:T(8,128)S(1)} custom-call(s32[256]{0:T(256)S(1)} %bitcast.7, f32[16,1,3072]{2,1,0:T(1,128)S(1)} %collective-permute-done.below_ref, f32[16,1,3072]{2,1,0:T(1,128)S(1)} %all-to-all-done.x_ref, f32[16,1,3072]{2,1,0:T(1,128)S(1)} %collective-permute-done.1.above_ref, s32[16,2]{1,0:T(8,128)S(1)} %reshape.11.fid_col_ref, ...), custom_call_target="tpu_custom_call" | custom-call | tf_op jit(solution)/shard_map/pallas_call | solution.py:218
  29.6 0.2 copy.22
  29.7 16.2 %all_to_all.10 = f32[2,3,16,512]{3,0,1,2:T(2,128)S(1)} all-to-all(f32[2,3,16,512]{3,0,1,2:T(2,128)S(1)} %copy.22), channel_id=1, replica_groups=mesh['groups'=2,'band'=16] {'band'}, dimensions={2} | all-to-all | bytes 393216 | tf_op jit(solution)/shard_map/all_to_all | solution.py:338
  45.9 0.7 %copy.23 = f32[2,3,16,512]{3,2,1,0:T(8,128)} copy(f32[2,3,16,512]{3,0,1,2:T(2,128)S(1)} %all_to_all.10) | data formatting | bytes 393216 | tf_op jit(solution)/shard_map/all_to_all | solution.py:338
  (4 shorter events, 0.0 us)
Async XLA Ops:
  2.6 7.6 %copy-start.2 = (s32[32]{0:T(128)S(1)}, s32[32]{0:T(128)}, u32[]{:S(2)}) copy-start(s32[32]{0:T(128)} %fid_ref.1) | copy-start | bytes 388
  2.6 7.7 %copy-start.1 = (f32[1,256,32]{1,2,0:T(8,128)S(1)}, f32[1,256,32]{1,2,0:T(8,128)}, u32[]{:S(2)}) copy-start(f32[1,256,32]{1,2,0:T(8,128)} %param.11) | copy-start | bytes 98308
  2.6 16.5 %all-to-all-start = ((f32[16,1,3072]{2,1,0:T(1,128)}), f32[16,1,3072]{2,1,0:T(1,128)S(1)}, u32[]{:S(2)}, u32[]{:S(2)}) async-start(f32[16,1,3072]{2,1,0:T(1,128)} %shard_map.64), calls=%async_computation | async-start | bytes 393216 | tf_op jit(solution)/shard_map/all_to_all | solution.py:329
  10.4 0.7 %copy-start = (f32[1,256]{1,0:T(1,128)S(1)}, f32[1,256]{1,0:T(1,128)}, u32[]{:S(2)}) copy-start(f32[1,256]{1,0:T(1,128)} %var_ref.1) | copy-start | bytes 3076
  10.4 0.7 %copy-start.3 = (f32[1,256]{1,0:T(1,128)S(1)}, f32[1,256]{1,0:T(1,128)}, u32[]{:S(2)}) copy-start(f32[1,256]{1,0:T(1,128)} %param.9) | copy-start | bytes 3076
  11.1 12.4 %copy-start.4 = (s32[1,256]{1,0:T(1,128)S(1)}, s32[1,256]{1,0:T(1,128)}, u32[]{:S(2)}) copy-start(s32[1,256]{1,0:T(1,128)} %param.8) | copy-start | bytes 3076
  19.1 4.4 %collective-permute-start.1 = (f32[16,1,3072]{2,1,0:T(1,128)S(1)}, f32[16,1,3072]{2,1,0:T(1,128)S(1)}, u32[]{:S(2)}, u32[]{:S(2)}) collective-permute-start(f32[16,1,3072]{2,1,0:T(1,128)S(1)} %all-to-all-done.x_ref), channel_id=1, source_target_pairs={{1,0},{2,1},{3,2},{4,3},{5,4},{6,5},{7,6},{8,7},{9,8},{10,9},{11,1... | collective-permute-start | bytes 589832 | tf_op jit(solution)/shard_map/ppermute | solution.py:333
  20.4 4.1 %collective-permute-start = (f32[16,1,3072]{2,1,0:T(1,128)S(1)}, f32[16,1,3072]{2,1,0:T(1,128)S(1)}, u32[]{:S(2)}, u32[]{:S(2)}) collective-permute-start(f32[16,1,3072]{2,1,0:T(1,128)S(1)} %all-to-all-done.x_ref), channel_id=1, source_target_pairs={{0,1},{1,2},{2,3},{3,4},{4,5},{5,6},{6,7},{7,8},{8,9},{9,10},{10,1... | collective-permute-start | bytes 589832 | tf_op jit(solution)/shard_map/ppermute | solution.py:332

commit v14 on v13

--- a/solution.py
+++ b/solution.py
@@ -192,11 +192,7 @@
     scale_row = jnp.sqrt(masks_row[0] / (count_row - 1.0))
     weighted = obs_spread / variance
     inner = contract(weighted, obs_spread, ((1,), (1,)))
-    direct = (
-        jnp.sum(weighted * value_ref[...], axis=1, keepdims=True)
-        + contract(weighted * jnp.sqrt(variance), noise_ref[...], ((1,), (0,)))
-        - contract(weighted, ob, ((1,), (1,)))
-    )
+    direct = contract(weighted, noise_ref[...], ((1,), (0,))) - contract(weighted, ob, ((1,), (1,)))
     row_id = lax.broadcasted_iota(jnp.int32, (m, m), 0)
     col_id = lax.broadcasted_iota(jnp.int32, (m, m), 1)
     system = (row_id == col_id).astype(jnp.float32) + scale_col * inner * scale_row
@@ -333,6 +329,7 @@
     above = lax.ppermute(rows, "band", down)
     noise = obs_noise[0].reshape(-1, sources, per_device)
     noise = jnp.transpose(noise, (0, 2, 1)).reshape(-1, sources * per_device)
+    noise = obs_value[0][:, None] + jnp.sqrt(obs_var[0])[:, None] * noise
     cells = jnp.clip(obs_cell[0], 0, 9 * lon - 1)
     result = analysis(cells, below, rows, above, member_fidelity, obs_value[0] + 0.0 * obs_var[0], obs_var[0], noise)
     return lax.all_to_all(result, "band", 2, 2, tiled=True)

time: 46.9 us -> 46.9 us (level)
  no operation moved by 1% of the time
where the time goes in v14:
time: 46.9 us; the launch traced here: 46.6 us
  blocking collectives  16.2 us (35%)
  starting transfers between devices  11.9 us (25%)
  waiting for transfers between devices  8.89 us (19%)
  Pallas kernels  7.62 us (16%)
  local copies, waits for them, and re-layouts  1.76 us (4%)
    all_to_all x1, blocking collectives, shards(): return lax.all_to_all(result, 'band', 2, 2, tiled=True)  16.2 us
    all_to_all x1, waiting for transfers between devices, shards(): rows = lax.all_to_all(rows, 'band', 0, 0, tiled=True)  7.88 us
    all_to_all x1, starting transfers between devices, shards(): rows = lax.all_to_all(rows, 'band', 0, 0, tiled=True)  7.55 us
    pallas_call x1, Pallas kernels, analysis(): pl.pallas_call(analysis_kernel, out_shape=jax.ShapeDtypeStruct((members /...  5.04 us
    ppermute x1, starting transfers between devices, shards(): below = lax.ppermute(rows, 'band', up)  3.04 us
    pallas_call x1, Pallas kernels, forecast(): pl.pallas_call(forecast_kernel, out_shape=jax.ShapeDtypeStruct((lat_rows,...  2.59 us
    ppermute x1, starting transfers between devices, shards(): above = lax.ppermute(rows, 'band', down)  1.28 us
    ppermute x1, waiting for transfers between devices, shards(): below = lax.ppermute(rows, 'band', up)  1.01 us
  transfers between devices with their start and end apart: 3, of which 2 were waited for; matrix products, arithmetic and copies ran while one was open for 1% of the time, Pallas kernels for 0%

profile of v14, /device:TPU:0, one launch (start us, length us, event | category | flops | bytes accessed | tf_op | source)
XLA Modules:
  0.0 46.6 jit_solution(15361913786163394963)
XLA Ops:
  0.0 2.6 %shard_map.64 = f32[16,1,3072]{2,1,0:T(1,128)} custom-call(s32[32]{0:T(128)} %fid_ref.1, f32[2,3,16,512]{3,2,1,0:T(8,128)} %x_ref.1), custom_call_target="tpu_custom_call" | custom-call | tf_op jit(solution)/shard_map/pallas_call | solution.py:310
  2.6 0.0 copy-start.3
  2.6 0.0 copy-start.1
  2.6 7.5 %all-to-all-start = ((f32[16,1,3072]{2,1,0:T(1,128)}), f32[16,1,3072]{2,1,0:T(1,128)S(1)}, u32[]{:S(2)}, u32[]{:S(2)}) async-start(f32[16,1,3072]{2,1,0:T(1,128)} %shard_map.64), calls=%async_computation | async-start | bytes 393216 | tf_op jit(solution)/shard_map/all_to_all | solution.py:325
  10.1 0.0 copy-done.3
  10.2 0.1 reshape.18.fid_col_ref
  10.2 0.1 copy.24
  10.3 0.0 copy-done.1
  10.4 0.0 copy-start
  10.4 0.0 copy-start.2
  10.4 0.1 copy.26
  10.5 0.6 %copy-done = f32[1,256]{1,0:T(1,128)S(1)} copy-done((f32[1,256]{1,0:T(1,128)S(1)}, f32[1,256]{1,0:T(1,128)}, u32[]{:S(2)}) %copy-start) | copy-done | bytes 1048
  11.1 0.0 copy-done.2
  11.1 0.0 copy-start.4
  11.1 0.1 multiply_add_fusion.noise_ref
  11.2 7.9 %all-to-all-done.x_ref = f32[16,1,3072]{2,1,0:T(1,128)S(1)} async-done(((f32[16,1,3072]{2,1,0:T(1,128)}), f32[16,1,3072]{2,1,0:T(1,128)S(1)}, u32[]{:S(2)}, u32[]{:S(2)}) %all-to-all-start) | async-done | bytes 196640 | tf_op jit(solution)/shard_map/all_to_all | solution.py:325
  19.1 1.3 %collective-permute-start.1 = (f32[16,1,3072]{2,1,0:T(1,128)S(1)}, f32[16,1,3072]{2,1,0:T(1,128)S(1)}, u32[]{:S(2)}, u32[]{:S(2)}) collective-permute-start(f32[16,1,3072]{2,1,0:T(1,128)S(1)} %all-to-all-done.x_ref), channel_id=1, source_target_pairs={{1,0},{2,1},{3,2},{4,3},{5,4},{6,5},{7,6},{8,7},{9,8},{10,9},{11,1... | collective-permute-start | bytes 589832 | tf_op jit(solution)/shard_map/ppermute | solution.py:329
  20.4 3.0 %collective-permute-start = (f32[16,1,3072]{2,1,0:T(1,128)S(1)}, f32[16,1,3072]{2,1,0:T(1,128)S(1)}, u32[]{:S(2)}, u32[]{:S(2)}) collective-permute-start(f32[16,1,3072]{2,1,0:T(1,128)S(1)} %all-to-all-done.x_ref), channel_id=1, source_target_pairs={{0,1},{1,2},{2,3},{3,4},{4,5},{5,6},{6,7},{7,8},{8,9},{9,10},{10,1... | collective-permute-start | bytes 589832 | tf_op jit(solution)/shard_map/ppermute | solution.py:328
  23.4 0.0 copy-done.4
  23.5 0.0 collective-permute-done.1.above_ref
  23.5 1.0 %collective-permute-done.below_ref = f32[16,1,3072]{2,1,0:T(1,128)S(1)} collective-permute-done((f32[16,1,3072]{2,1,0:T(1,128)S(1)}, f32[16,1,3072]{2,1,0:T(1,128)S(1)}, u32[]{:S(2)}, u32[]{:S(2)}) %collective-permute-start) | collective-permute-done | bytes 196640 | tf_op jit(solution)/shard_map/ppermute | solution.py:328
  24.5 5.0 %shard_map.65 = f32[2,3,16,512]{3,2,1,0:T(8,128)S(1)} custom-call(s32[256]{0:T(256)S(1)} %bitcast.9, f32[16,1,3072]{2,1,0:T(1,128)S(1)} %collective-permute-done.below_ref, f32[16,1,3072]{2,1,0:T(1,128)S(1)} %all-to-all-done.x_ref, f32[16,1,3072]{2,1,0:T(1,128)S(1)} %collective-permute-done.1.above_ref, s32[16,2]{1,0:T(8,128)S(1)} %reshape.18.fid_col_ref, ...), custom_call_target="tpu_custom_call" | custom-call | tf_op jit(solution)/shard_map/pallas_call | solution.py:214
  29.5 0.2 copy.28
  29.7 16.2 %all_to_all.10 = f32[2,3,16,512]{3,0,1,2:T(2,128)S(1)} all-to-all(f32[2,3,16,512]{3,0,1,2:T(2,128)S(1)} %copy.28), channel_id=1, replica_groups=mesh['groups'=2,'band'=16] {'band'}, dimensions={2} | all-to-all | bytes 393216 | tf_op jit(solution)/shard_map/all_to_all | solution.py:335
  45.8 0.7 %copy.29 = f32[2,3,16,512]{3,2,1,0:T(8,128)} copy(f32[2,3,16,512]{3,0,1,2:T(2,128)S(1)} %all_to_all.10) | data formatting | bytes 393216 | tf_op jit(solution)/shard_map/all_to_all | solution.py:335
  (4 shorter events, 0.0 us)
Async XLA Ops:
  2.6 7.6 %copy-start.3 = (s32[32]{0:T(128)S(1)}, s32[32]{0:T(128)}, u32[]{:S(2)}) copy-start(s32[32]{0:T(128)} %fid_ref.1) | copy-start | bytes 388
  2.6 7.7 %copy-start.1 = (f32[1,256,32]{1,2,0:T(8,128)S(1)}, f32[1,256,32]{1,2,0:T(8,128)}, u32[]{:S(2)}) copy-start(f32[1,256,32]{1,2,0:T(8,128)} %param.11) | copy-start | bytes 98308
  2.6 16.5 %all-to-all-start = ((f32[16,1,3072]{2,1,0:T(1,128)}), f32[16,1,3072]{2,1,0:T(1,128)S(1)}, u32[]{:S(2)}, u32[]{:S(2)}) async-start(f32[16,1,3072]{2,1,0:T(1,128)} %shard_map.64), calls=%async_computation | async-start | bytes 393216 | tf_op jit(solution)/shard_map/all_to_all | solution.py:325
  10.4 0.7 %copy-start = (f32[1,256]{1,0:T(1,128)S(1)}, f32[1,256]{1,0:T(1,128)}, u32[]{:S(2)}) copy-start(f32[1,256]{1,0:T(1,128)} %var_ref.1) | copy-start | bytes 3076
  10.4 0.7 %copy-start.2 = (f32[1,256]{1,0:T(1,128)S(1)}, f32[1,256]{1,0:T(1,128)}, u32[]{:S(2)}) copy-start(f32[1,256]{1,0:T(1,128)} %param.9) | copy-start | bytes 3076
  11.1 12.4 %copy-start.4 = (s32[1,256]{1,0:T(1,128)S(1)}, s32[1,256]{1,0:T(1,128)}, u32[]{:S(2)}) copy-start(s32[1,256]{1,0:T(1,128)} %param.8) | copy-start | bytes 3076
  19.1 4.4 %collective-permute-start.1 = (f32[16,1,3072]{2,1,0:T(1,128)S(1)}, f32[16,1,3072]{2,1,0:T(1,128)S(1)}, u32[]{:S(2)}, u32[]{:S(2)}) collective-permute-start(f32[16,1,3072]{2,1,0:T(1,128)S(1)} %all-to-all-done.x_ref), channel_id=1, source_target_pairs={{1,0},{2,1},{3,2},{4,3},{5,4},{6,5},{7,6},{8,7},{9,8},{10,9},{11,1... | collective-permute-start | bytes 589832 | tf_op jit(solution)/shard_map/ppermute | solution.py:329
  20.4 4.1 %collective-permute-start = (f32[16,1,3072]{2,1,0:T(1,128)S(1)}, f32[16,1,3072]{2,1,0:T(1,128)S(1)}, u32[]{:S(2)}, u32[]{:S(2)}) collective-permute-start(f32[16,1,3072]{2,1,0:T(1,128)S(1)} %all-to-all-done.x_ref), channel_id=1, source_target_pairs={{0,1},{1,2},{2,3},{3,4},{4,5},{5,6},{6,7},{7,8},{8,9},{9,10},{10,1... | collective-permute-start | bytes 589832 | tf_op jit(solution)/shard_map/ppermute | solution.py:328
